TPU v7x, 256 devices: a whole 4x4x8 slice. The times are simulated.
256 devices in a mesh: req: 64 (over z, y_lo, x), tp: 4 (over y_hi, core).
Axes of the slice: x: 4, y: 4 (y_hi: 2, y_lo: 2; y = y_hi * 2 + y_lo), z: 8, core: 2. Of those that a mesh axis runs over, the one named last changes fastest.
Arguments:
- hidden: bfloat16 [32768, 4096], P(('req', 'tp')), may hold values from -6 to 6
- norm_gain: bfloat16 [4096], replicated, may hold values from 0.099609375 to 1.8984375
- w_qkv: bfloat16 [4096, 3072], P('req', 'tp'), may hold values from -0.09375 to 0.09375
- w_out: bfloat16 [2048, 4096], P('tp', 'req'), may hold values from -0.125 to 0.125
- lengths: int32 [256], replicated, may hold values from 1 to 3072, as said below
- deal: int32 [256], replicated, may hold values from 0 to 255, as said below
- pages: int32 [256, 24], P('req'), may hold values from 0 to 95, as said below
- pool: bfloat16 [6144, 128, 1024], P('req', None, 'tp'), may hold values from -360 to 360
Outputs:
- attn_out: bfloat16 [32768, 4096], P(('req', 'tp'))
- new_kv: bfloat16 [32768, 1024], P('req', 'tp')
Inputs may be any that keep to these rules, and one draw needn't show every extreme that they name: `lengths`: at least one request has exactly 3072 cached tokens. `deal`: a permutation of the requests. `pages`: the 4 rows of one req index together hold each page number of its pool block once.
All inputs are finite; a program needn't handle non-finite values.
Results may differ from a plain program's by a relative error of at most 0.01.
The roundings to bfloat16 on the way count: a program that leaves them out, or rounds other values in their place, can miss the bound.
Values may be sent and summed in bfloat16 or wider, within the bound.
No kernel may reach another device: no remote copies, remote signals or barrier semaphores. Data moves between devices by JAX's collectives and lax.ppermute only.
A program may use at most 128 MiB of HBM per device.

v0:
```python
import math

import jax
import jax.numpy as jnp
from jax import lax
from jax.sharding import PartitionSpec as P

HEAD = 128
QH = 16
KVH = 4
PAGE = 128
NEW = 128


def rotate(values, position):
    half = values.shape[-1] // 2
    freqs = 500000.0 ** (-(jnp.arange(half, dtype=jnp.float32) * 2.0 / values.shape[-1]))
    angles = position.astype(jnp.float32)[:, None] * freqs[None, :]
    target = (angles.shape[0],) + (1,) * (values.ndim - 2) + (half,)
    cosine = jnp.cos(angles).reshape(target)
    sine = jnp.sin(angles).reshape(target)
    former = values[..., :half]
    latter = values[..., half:]
    return jnp.concatenate([former * cosine - latter * sine, latter * cosine + former * sine], -1)


def fresh_scores_of(query_matrix, recent_key_rows, score_scale):
    scores = (
        jnp.einsum(
            "eksv,qkv->kseq", query_matrix, recent_key_rows, preferred_element_type=jnp.float32
        )
        * score_scale
    )
    count_new = query_matrix.shape[0]
    causal = jnp.arange(count_new)[:, None] >= jnp.arange(count_new)[None, :]
    return jnp.where(causal, scores, -jnp.inf)


def value_weighted_rows(weights, values, form):
    return jnp.einsum(
        form, weights.astype(jnp.bfloat16), values, preferred_element_type=jnp.float32
    )


def padded_attention(
    query_matrix, recent_key_rows, recent_value_rows, pool_view, page_row, length, score_scale
):
    heads_here = pool_view.shape[2]
    cache = pool_view[page_row].reshape(-1, heads_here, 2, HEAD)
    span = cache.shape[0]
    cached_scores = (
        jnp.einsum(
            "nhgd,khd->hgnk", query_matrix, cache[:, :, 0], preferred_element_type=jnp.float32
        )
        * score_scale
    )
    cached_scores = jnp.where(jnp.arange(span, dtype=jnp.int32) < length, cached_scores, -jnp.inf)
    recent_score_rows = fresh_scores_of(query_matrix, recent_key_rows, score_scale)
    row_max = jnp.maximum(cached_scores.max(-1), recent_score_rows.max(-1))[..., None]
    cached_exp = jnp.exp(cached_scores - row_max)
    recent_exponent = jnp.exp(recent_score_rows - row_max)
    total = cached_exp.sum(-1) + recent_exponent.sum(-1)
    summed_total = value_weighted_rows(cached_exp, cache[:, :, 1], "hgnk,khd->hgnd")
    summed_total = summed_total + value_weighted_rows(
        recent_exponent, recent_value_rows, "tvqa,ats->tvqs"
    )
    return summed_total / total[..., None]


def per_device(hidden, norm_gain, w_qkv, w_out, lengths, deal, pages, pool):
    states = hidden.astype(jnp.float32)
    mean_square = jnp.mean(states * states, axis=1, keepdims=True)
    normed = (states * lax.rsqrt(mean_square + 1e-05) * norm_gain.astype(jnp.float32)).astype(
        jnp.bfloat16
    )
    gathered = lax.all_gather(normed, "tp", axis=0, tiled=True)
    tok_rows = gathered.shape[0]
    projected = jnp.dot(
        gathered,
        lax.all_gather(w_qkv, "req", axis=0, tiled=True),
        preferred_element_type=jnp.float32,
    ).astype(jnp.bfloat16)
    full_out = lax.all_gather(w_out, "req", axis=1, tiled=True)
    group = QH // KVH
    heads_here = w_qkv.shape[1] // ((group + 2) * HEAD)
    slot_count = tok_rows // NEW
    slot_ids = lax.axis_index("req") * slot_count + jnp.arange(slot_count, dtype=jnp.int32)
    slot_length = lengths[deal[slot_ids]]
    position = jnp.repeat(slot_length, NEW) + jnp.tile(jnp.arange(NEW, dtype=jnp.int32), slot_count)
    projected = projected.reshape(tok_rows, heads_here, group + 2, HEAD)
    queries = rotate(projected[:, :, :group].astype(jnp.float32), position).astype(jnp.bfloat16)
    keys_new = rotate(projected[:, :, group].astype(jnp.float32), position).astype(jnp.bfloat16)
    values_new = projected[:, :, group + 1]
    new_kv = jnp.stack([keys_new, values_new], 2).reshape(tok_rows, heads_here * 2 * HEAD)
    pool_view = pool.reshape(pool.shape[0], PAGE, heads_here, 2, HEAD)
    score_scale = 1.0 / math.sqrt(HEAD)

    def attend(local_slot):
        begin = local_slot * NEW
        query_matrix = lax.dynamic_slice_in_dim(queries, begin, NEW, 0)
        recent_key_rows = lax.dynamic_slice_in_dim(keys_new, begin, NEW, 0)
        recent_value_rows = lax.dynamic_slice_in_dim(values_new, begin, NEW, 0)
        page_row = pages[local_slot]
        length = slot_length[local_slot]
        result = padded_attention(
            query_matrix,
            recent_key_rows,
            recent_value_rows,
            pool_view,
            page_row,
            length,
            score_scale,
        )
        result = result.astype(jnp.bfloat16)
        return result.transpose(2, 0, 1, 3).reshape(NEW, heads_here * group * HEAD)

    contexts = lax.map(attend, jnp.arange(slot_count, dtype=jnp.int32))
    context = contexts.reshape(tok_rows, heads_here * group * HEAD)
    attn_out = lax.psum_scatter(
        jnp.dot(context, full_out, preferred_element_type=jnp.float32).astype(jnp.bfloat16),
        "tp",
        scatter_dimension=0,
        tiled=True,
    )
    return (attn_out, new_kv)


def solution(mesh):
    in_specs = (
        P(("req", "tp"), None),
        P(),
        P("req", "tp"),
        P("tp", "req"),
        P(),
        P(),
        P("req", None),
        P("req", None, "tp"),
    )
    out_specs = (P(("req", "tp"), None), P("req", "tp"))
    return jax.shard_map(
        per_device, mesh=mesh, in_specs=in_specs, out_specs=out_specs, check_vma=False
    )
```

profile of v0, /device:TPU:1, one launch (start us, length us, event | category | flops | bytes accessed | tf_op | source)
XLA Modules:
  0.0 734.8 jit_solution(14359055821439632575)
XLA Ops:
  7.2 0.7 convert_element_type.81
  7.9 1.5 fusion.32
  9.5 2.5 fusion.34
  12.1 0.7 all-gather.6.cloned.1.call-update
  12.8 0.7 all-gather.8.cloned.1.call-update
  13.6 0.6 gather_fusion.1
  14.3 0.6 gather_fusion.2
  15.0 9.7 %reshape.408 = bf16[96,128,1,2,128]{4,3,2,1,0:T(2,128)(2,1)} reshape(bf16[96,128,256]{2,1,0:T(8,128)(2,1)} %param.17) | data formatting | bytes 12582912 | tf_op jit(solution)/shard_map/reshape | solution.py:95
  25.3 32.2 %all-gather.4.cloned.1.call-done = bf16[512,4096]{1,0:T(8,128)(2,1)} async-done(((bf16[128,4096]{1,0:T(8,128)(2,1)}), bf16[512,4096]{1,0:T(8,128)(2,1)}) %all-gather.4.cloned.1.call-update) | async-done | bytes 4194320 | tf_op jit(solution)/shard_map/all_gather | solution.py:76
  57.4 262.9 %all-gather.6.cloned.1.call-done = bf16[4096,768]{1,0:T(8,128)(2,1)} async-done(((bf16[64,768]{1,0:T(8,128)(2,1)}), bf16[4096,768]{1,0:T(8,128)(2,1)}) %all-gather.6.cloned.1.call-update) | async-done | bytes 6291472 | tf_op jit(solution)/shard_map/all_gather | solution.py:80
  320.4 7.5 %convolution_convert_fusion.1 = bf16[512,768]{1,0:T(8,128)(2,1)S(1)} fusion(bf16[512,4096]{1,0:T(8,128)(2,1)} %all-gather.4.cloned.1.call-done, bf16[4096,768]{1,0:T(8,128)(2,1)} %all-gather.6.cloned.1.call-done), kind=kOutput, calls=%fused_computation.53 | convolution fusion | flops 3221618688 | bytes 11272192 | tf_op jit(solution)/shard_map/dot_general | solution.py:78
  329.1 76.6 %while.10 = (s32[]{:T(128)}, bf16[4,128,512]{2,1,0:T(8,128)(2,1)S(1)}, s32[4]{0:T(128)S(1)}, s32[4]{0:T(128)S(1)}, s32[4,24]{1,0:T(4,128)}, /*index=5*/bf16[96,1...) while((s32[]{:T(128)}, ...), condition=%wide.region_6.7_spmd, body=%wide.region_1.6_spmd.sunk | while | flops 856837184 | bytes 29113984 | solution.py:117
  329.1 0.6 dynamic_slice.60
  332.3 0.7 fusion.64
  333.0 8.2 %gather_fusion = bf16[24,128,2,128]{3,2,1,0:T(2,128)(2,1)S(1)} fusion(bf16[96,128,2,128]{3,2,1,0:T(2,128)(2,1)} %bitcast.156, s32[1024]{0:T(1024)S(1)} %pad_clamp_fusion.4), kind=kCustom, calls=%fused_computation.clone.1 | custom fusion | bytes 3145824 | tf_op jit(solution)/shard_map/while/body/eval_jaxpr/gather | solution.py:49
  341.6 0.6 dynamic_slice.61
  342.2 0.7 iota_compare_fusion.4
  342.8 1.0 bitcast_reduce_fusion.2
  344.2 2.0 fusion.67
  346.2 1.7 fusion.66
  348.3 0.6 dynamic_slice.60
  351.4 0.7 fusion.64
  352.1 8.2 %gather_fusion = bf16[24,128,2,128]{3,2,1,0:T(2,128)(2,1)S(1)} fusion(bf16[96,128,2,128]{3,2,1,0:T(2,128)(2,1)} %bitcast.156, s32[1024]{0:T(1024)S(1)} %pad_clamp_fusion.4), kind=kCustom, calls=%fused_computation.clone.1 | custom fusion | bytes 3145824 | tf_op jit(solution)/shard_map/while/body/eval_jaxpr/gather | solution.py:49
  360.7 0.6 dynamic_slice.61
  361.3 0.7 iota_compare_fusion.4
  362.0 1.0 bitcast_reduce_fusion.2
  363.3 2.0 fusion.67
  365.3 1.7 fusion.66
  367.4 0.6 dynamic_slice.60
  370.6 0.7 fusion.64
  371.3 8.2 %gather_fusion = bf16[24,128,2,128]{3,2,1,0:T(2,128)(2,1)S(1)} fusion(bf16[96,128,2,128]{3,2,1,0:T(2,128)(2,1)} %bitcast.156, s32[1024]{0:T(1024)S(1)} %pad_clamp_fusion.4), kind=kCustom, calls=%fused_computation.clone.1 | custom fusion | bytes 3145824 | tf_op jit(solution)/shard_map/while/body/eval_jaxpr/gather | solution.py:49
  379.9 0.6 dynamic_slice.61
  380.5 0.7 iota_compare_fusion.4
  381.1 1.0 bitcast_reduce_fusion.2
  382.4 2.0 fusion.67
  384.4 1.7 fusion.66
  386.5 0.6 dynamic_slice.60
  389.7 0.7 fusion.64
  390.4 8.2 %gather_fusion = bf16[24,128,2,128]{3,2,1,0:T(2,128)(2,1)S(1)} fusion(bf16[96,128,2,128]{3,2,1,0:T(2,128)(2,1)} %bitcast.156, s32[1024]{0:T(1024)S(1)} %pad_clamp_fusion.4), kind=kCustom, calls=%fused_computation.clone.1 | custom fusion | bytes 3145824 | tf_op jit(solution)/shard_map/while/body/eval_jaxpr/gather | solution.py:49
  399.0 0.6 dynamic_slice.61
  399.6 0.7 iota_compare_fusion.4
  400.3 1.0 bitcast_reduce_fusion.2
  401.6 2.0 fusion.67
  403.6 1.7 fusion.66
  405.7 216.2 %all-gather.8.cloned.1.call-done = bf16[512,4096]{0,1:T(8,128)(2,1)} async-done(((bf16[512,64]{0,1:T(8,128)(2,1)}), bf16[512,4096]{0,1:T(8,128)(2,1)}) %all-gather.8.cloned.1.call-update) | async-done | bytes 4194320 | tf_op jit(solution)/shard_map/all_gather | solution.py:83
  621.9 6.5 convolution_convert_fusion
  628.5 0.8 copy.27
  629.3 98.9 %reduce-scatter.2.cloned.1.call-done = bf16[128,4096]{1,0:T(8,128)(2,1)} async-done(((bf16[512,4096]{1,0:T(8,128)(2,1)}), bf16[128,4096]{1,0:T(8,128)(2,1)}) %reduce-scatter.2.cloned.1.call-update) | async-done | bytes 1048592 | tf_op jit(solution)/shard_map/reduce_scatter | solution.py:119
  (68 shorter events, 6.3 us)
Async XLA Ops:
  7.2 6.4 copy-start
  7.2 7.1 copy-start.1
  7.2 50.2 %all-gather.4.cloned.1.call-start = ((), (), s32[]{:S(2)}) async-start(), calls=%async_computation.1 | async-start | bytes 5242880 | tf_op jit(solution)/shard_map/all_gather | solution.py:76
  12.0 308.3 %all-gather.6.cloned.1.call-start = ((), (), s32[]{:S(2)}) async-start(), calls=%async_computation.2 | async-start | bytes 6389760 | tf_op jit(solution)/shard_map/all_gather | solution.py:80
  12.8 609.2 %all-gather.8.cloned.1.call-start = ((), (), s32[]{:S(2)}) async-start(), calls=%async_computation.3 | async-start | bytes 4259840 | tf_op jit(solution)/shard_map/all_gather | solution.py:83
  13.5 714.7 %reduce-scatter.2.cloned.1.call-start = ((), (), s32[]{:S(2)}) async-start(), calls=%async_computation.4 | async-start | bytes 5242880 | tf_op jit(solution)/shard_map/reduce_scatter | solution.py:119
Sparse Core Ops, SparseCore 0:
  12.1 45.2 all-gather.3
  59.2 261.0 all-gather.5
  322.1 299.7 all-gather.7
  628.6 99.5 reduce-scatter.1
where the time goes:
time: 736 us; the launch traced here: 735 us
  waiting for transfers between devices  612 us (83%)
  local copies, waits for them, and re-layouts  51.7 us (7%)
  matrix products  26.6 us (4%)
  other arithmetic  20 us (3%)
  between operations  13.9 us (2%)
  loops' own time  10.8 us (1%)
    all_gather x1, waiting for transfers between devices, per_device(): lax.all_gather(w_qkv, 'req', axis=0, tiled=True)  263 us
    all_gather x1, waiting for transfers between devices, per_device(): full_out = lax.all_gather(w_out, 'req', axis=1, tiled=True)  216 us
    reduce_scatter x1, waiting for transfers between devices, per_device(): lax.psum_scatter(jnp.dot(context, full_out, preferred_element_type=jnp.fl...  98.9 us
    gather x8, local copies, waits for them, and re-layouts, padded_attention(): cache = pool_view[page_row].reshape(-1, heads_here, 2, HEAD)  34.3 us
    all_gather x1, waiting for transfers between devices, per_device(): gathered = lax.all_gather(normed, 'tp', axis=0, tiled=True)  32.2 us
  transfers between devices with their start and end apart: 4, of which 4 were waited for; matrix products, arithmetic and copies ran while one was open for 12% of the time, Pallas kernels for 0%

commit v1 on v0

--- a/solution.py
+++ b/solution.py
@@ -67,24 +67,34 @@
     return summed_total / total[..., None]
 
 
+REQ_AXES = ("z", "ylo", "x")
+TP_AXES = ("yhi", "core")
+
+
+def staged_gather(values, axes, axis):
+    for name in reversed(axes):
+        values = lax.all_gather(values, name, axis=axis, tiled=True)
+    return values
+
+
 def per_device(hidden, norm_gain, w_qkv, w_out, lengths, deal, pages, pool):
     states = hidden.astype(jnp.float32)
     mean_square = jnp.mean(states * states, axis=1, keepdims=True)
     normed = (states * lax.rsqrt(mean_square + 1e-05) * norm_gain.astype(jnp.float32)).astype(
         jnp.bfloat16
     )
-    gathered = lax.all_gather(normed, "tp", axis=0, tiled=True)
+    gathered = lax.all_gather(normed, TP_AXES, axis=0, tiled=True)
     tok_rows = gathered.shape[0]
     projected = jnp.dot(
         gathered,
-        lax.all_gather(w_qkv, "req", axis=0, tiled=True),
+        staged_gather(w_qkv, REQ_AXES, 0),
         preferred_element_type=jnp.float32,
     ).astype(jnp.bfloat16)
-    full_out = lax.all_gather(w_out, "req", axis=1, tiled=True)
+    full_out = staged_gather(w_out, REQ_AXES, 1)
     group = QH // KVH
     heads_here = w_qkv.shape[1] // ((group + 2) * HEAD)
     slot_count = tok_rows // NEW
-    slot_ids = lax.axis_index("req") * slot_count + jnp.arange(slot_count, dtype=jnp.int32)
+    slot_ids = lax.axis_index(REQ_AXES) * slot_count + jnp.arange(slot_count, dtype=jnp.int32)
     slot_length = lengths[deal[slot_ids]]
     position = jnp.repeat(slot_length, NEW) + jnp.tile(jnp.arange(NEW, dtype=jnp.int32), slot_count)
     projected = projected.reshape(tok_rows, heads_here, group + 2, HEAD)
@@ -118,7 +128,7 @@
     context = contexts.reshape(tok_rows, heads_here * group * HEAD)
     attn_out = lax.psum_scatter(
         jnp.dot(context, full_out, preferred_element_type=jnp.float32).astype(jnp.bfloat16),
-        "tp",
+        TP_AXES,
         scatter_dimension=0,
         tiled=True,
     )
@@ -126,17 +136,18 @@
 
 
 def solution(mesh):
+    fine = jax.sharding.Mesh(mesh.devices.reshape(8, 2, 4, 2, 2), REQ_AXES + TP_AXES)
     in_specs = (
-        P(("req", "tp"), None),
+        P(REQ_AXES + TP_AXES, None),
         P(),
-        P("req", "tp"),
-        P("tp", "req"),
+        P(REQ_AXES, TP_AXES),
+        P(TP_AXES, REQ_AXES),
         P(),
         P(),
-        P("req", None),
-        P("req", None, "tp"),
+        P(REQ_AXES, None),
+        P(REQ_AXES, None, TP_AXES),
     )
-    out_specs = (P(("req", "tp"), None), P("req", "tp"))
+    out_specs = (P(REQ_AXES + TP_AXES, None), P(REQ_AXES, TP_AXES))
     return jax.shard_map(
-        per_device, mesh=mesh, in_specs=in_specs, out_specs=out_specs, check_vma=False
+        per_device, mesh=fine, in_specs=in_specs, out_specs=out_specs, check_vma=False
     )

time: 736 us -> 295 us (0.40)
  waiting for transfers between devices: 612 us -> 126 us
  blocking collectives: 0 us -> 44.1 us
    all_gather x3, waiting for transfers between devices: 511 us -> 71.6 us  [the longest x2 71.5 us: staged_gather(): values = lax.all_gather(values, name, axis=axis, tiled=True)]
    reduce_scatter x1, waiting for transfers between devices: 98.9 us -> 54.7 us  [per_device(): lax.psum_scatter(jnp.dot(context, full_out, preferred_element_type=jnp.fl...]
    all_gather x0 -> x4, blocking collectives: none -> 44.1 us  [staged_gather(): values = lax.all_gather(values, name, axis=axis, tiled=True)]
  transfers between devices with their start and end apart: 4 -> 4, of which waited for: 4 -> 2; matrix products, arithmetic and copies ran while one was open for 12% -> 30% of each run, Pallas kernels for 0% -> 0%
where the time goes in v1:
time: 295 us; the launch traced here: 294 us
  waiting for transfers between devices  126 us (43%)
  local copies, waits for them, and re-layouts  51.8 us (18%)
  blocking collectives  44.1 us (15%)
  matrix products  26.5 us (9%)
  other arithmetic  20.1 us (7%)
  between operations  14 us (5%)
  loops' own time  10.8 us (4%)
    all_gather x2, waiting for transfers between devices, staged_gather(): values = lax.all_gather(values, name, axis=axis, tiled=True)  71.5 us
    reduce_scatter x1, waiting for transfers between devices, per_device(): lax.psum_scatter(jnp.dot(context, full_out, preferred_element_type=jnp.fl...  54.7 us
    all_gather x4, blocking collectives, staged_gather(): values = lax.all_gather(values, name, axis=axis, tiled=True)  44.1 us
    gather x8, local copies, waits for them, and re-layouts, padded_attention(): cache = pool_view[page_row].reshape(-1, heads_here, 2, HEAD)  34.3 us
    another operation x1, loops' own time, per_device(): contexts = lax.map(attend, jnp.arange(slot_count, dtype=jnp.int32))  10.8 us
    reshape x1, local copies, waits for them, and re-layouts, per_device(): pool_view = pool.reshape(pool.shape[0], PAGE, heads_here, 2, HEAD)  9.76 us
    reduce_sum x8, other arithmetic, padded_attention(): total = cached_exp.sum(-1) + recent_exponent.sum(-1)  8.17 us
    dot_general x8, matrix products, value_weighted_rows(): jnp.einsum(form, weights.astype(jnp.bfloat16), values, preferred_element_...  7.69 us
  transfers between devices with their start and end apart: 4, of which 2 were waited for; matrix products, arithmetic and copies ran while one was open for 30% of the time, Pallas kernels for 0%

profile of v1, /device:TPU:1, one launch (start us, length us, event | category | flops | bytes accessed | tf_op | source)
XLA Modules:
  0.0 293.8 jit_solution(14749580712273259475)
XLA Ops:
  7.2 0.7 convert_element_type.81
  8.0 1.5 fusion.32
  9.5 2.5 fusion.34
  12.1 11.7 %all_gather.22 = bf16[256,768]{1,0:T(8,128)(2,1)S(1)} all-gather(bf16[64,768]{1,0:T(8,128)(2,1)S(1)} %copy-done.2), channel_id=1, replica_groups=mesh['z'=8,'ylo'=2,'x'=4,'yhi'=2,'core'=2] {'x'}, dimensions={0}, use_global_device_ids=true | all-gather | bytes 491520 | tf_op jit(solution)/shard_map/all_gather | solution.py:76
  23.8 9.2 %all_gather.23 = bf16[512,768]{1,0:T(8,128)(2,1)} all-gather(bf16[256,768]{1,0:T(8,128)(2,1)S(1)} %all_gather.22), channel_id=1, replica_groups=mesh['z'=8,'ylo'=2,'x'=4,'yhi'=2,'core'=2] {'ylo'}, dimensions={0}, use_global_device_ids=true | all-gather | bytes 1179648 | tf_op jit(solution)/shard_map/all_gather | solution.py:76
  33.1 10.6 %all_gather.25 = bf16[512,256]{0,1:T(8,128)(2,1)S(1)} all-gather(bf16[512,64]{0,1:T(8,128)(2,1)S(1)} %copy-done.3), channel_id=1, replica_groups=mesh['z'=8,'ylo'=2,'x'=4,'yhi'=2,'core'=2] {'x'}, dimensions={1}, use_global_device_ids=true | all-gather | bytes 327680 | tf_op jit(solution)/shard_map/all_gather | solution.py:76
  43.7 12.7 %all_gather.26 = bf16[512,512]{0,1:T(8,128)(2,1)} all-gather(bf16[512,256]{0,1:T(8,128)(2,1)S(1)} %all_gather.25), channel_id=1, replica_groups=mesh['z'=8,'ylo'=2,'x'=4,'yhi'=2,'core'=2] {'ylo'}, dimensions={1}, use_global_device_ids=true | all-gather | bytes 786432 | tf_op jit(solution)/shard_map/all_gather | solution.py:76
  56.5 0.6 gather_fusion.1
  57.2 0.6 gather_fusion.2
  57.9 9.8 %reshape.408 = bf16[96,128,1,2,128]{4,3,2,1,0:T(2,128)(2,1)} reshape(bf16[96,128,256]{2,1,0:T(8,128)(2,1)} %param.17) | data formatting | bytes 12582912 | tf_op jit(solution)/shard_map/reshape | solution.py:105
  68.2 71.5 %all-gather.6.cloned.1.call-done = bf16[4096,768]{1,0:T(8,128)(2,1)} async-done(((bf16[512,768]{1,0:T(8,128)(2,1)}), bf16[4096,768]{1,0:T(8,128)(2,1)}) %all-gather.6.cloned.1.call-update) | async-done | bytes 6291472 | tf_op jit(solution)/shard_map/all_gather | solution.py:76
  139.7 7.5 %convolution_convert_fusion.1 = bf16[512,768]{1,0:T(8,128)(2,1)S(1)} fusion(bf16[512,4096]{1,0:T(8,128)(2,1)} %all-gather.4.cloned.1.call-done, bf16[4096,768]{1,0:T(8,128)(2,1)} %all-gather.6.cloned.1.call-done), kind=kOutput, calls=%fused_computation.53 | convolution fusion | flops 3221618688 | bytes 11272192 | tf_op jit(solution)/shard_map/dot_general | solution.py:88
  148.5 76.6 %while.10 = (s32[]{:T(128)}, bf16[4,128,512]{2,1,0:T(8,128)(2,1)S(1)}, s32[4]{0:T(128)S(1)}, s32[4]{0:T(128)S(1)}, s32[4,24]{1,0:T(4,128)}, /*index=5*/bf16[96,1...) while((s32[]{:T(128)}, ...), condition=%wide.region_6.7_spmd, body=%wide.region_1.6_spmd.sunk | while | flops 856837184 | bytes 29113984 | solution.py:127
  148.5 0.6 dynamic_slice.60
  151.7 0.7 fusion.64
  152.4 8.2 %gather_fusion = bf16[24,128,2,128]{3,2,1,0:T(2,128)(2,1)S(1)} fusion(bf16[96,128,2,128]{3,2,1,0:T(2,128)(2,1)} %bitcast.156, s32[1024]{0:T(1024)S(1)} %pad_clamp_fusion.4), kind=kCustom, calls=%fused_computation.clone.1 | custom fusion | bytes 3145824 | tf_op jit(solution)/shard_map/while/body/eval_jaxpr/gather | solution.py:49
  161.0 0.6 dynamic_slice.61
  161.6 0.7 iota_compare_fusion.4
  162.2 1.0 bitcast_reduce_fusion.2
  163.6 2.0 fusion.67
  165.6 1.7 fusion.66
  167.7 0.6 dynamic_slice.60
  170.8 0.7 fusion.64
  171.5 8.2 %gather_fusion = bf16[24,128,2,128]{3,2,1,0:T(2,128)(2,1)S(1)} fusion(bf16[96,128,2,128]{3,2,1,0:T(2,128)(2,1)} %bitcast.156, s32[1024]{0:T(1024)S(1)} %pad_clamp_fusion.4), kind=kCustom, calls=%fused_computation.clone.1 | custom fusion | bytes 3145824 | tf_op jit(solution)/shard_map/while/body/eval_jaxpr/gather | solution.py:49
  180.2 0.6 dynamic_slice.61
  180.8 0.7 iota_compare_fusion.4
  181.4 1.0 bitcast_reduce_fusion.2
  182.8 2.0 fusion.67
  184.8 1.7 fusion.66
  186.8 0.6 dynamic_slice.60
  190.0 0.7 fusion.64
  190.7 8.2 %gather_fusion = bf16[24,128,2,128]{3,2,1,0:T(2,128)(2,1)S(1)} fusion(bf16[96,128,2,128]{3,2,1,0:T(2,128)(2,1)} %bitcast.156, s32[1024]{0:T(1024)S(1)} %pad_clamp_fusion.4), kind=kCustom, calls=%fused_computation.clone.1 | custom fusion | bytes 3145824 | tf_op jit(solution)/shard_map/while/body/eval_jaxpr/gather | solution.py:49
  199.3 0.6 dynamic_slice.61
  199.9 0.7 iota_compare_fusion.4
  200.6 1.0 bitcast_reduce_fusion.2
  201.9 2.0 fusion.67
  203.9 1.7 fusion.66
  206.0 0.6 dynamic_slice.60
  209.2 0.7 fusion.64
  209.9 8.2 %gather_fusion = bf16[24,128,2,128]{3,2,1,0:T(2,128)(2,1)S(1)} fusion(bf16[96,128,2,128]{3,2,1,0:T(2,128)(2,1)} %bitcast.156, s32[1024]{0:T(1024)S(1)} %pad_clamp_fusion.4), kind=kCustom, calls=%fused_computation.clone.1 | custom fusion | bytes 3145824 | tf_op jit(solution)/shard_map/while/body/eval_jaxpr/gather | solution.py:49
  218.5 0.6 dynamic_slice.61
  219.1 0.7 iota_compare_fusion.4
  219.7 1.0 bitcast_reduce_fusion.2
  221.0 2.0 fusion.67
  223.0 1.7 fusion.66
  225.2 6.5 %convolution_convert_fusion = bf16[512,4096]{1,0:T(8,128)(2,1)} fusion(bf16[512,512]{1,0:T(8,128)(2,1)S(1)} %bitcast.163, bf16[512,4096]{0,1:T(8,128)(2,1)} %all-gather.8.cloned.1.call-done), kind=kOutput, calls=%fused_computation.47 | convolution fusion | flops 2149580800 | bytes 8912896 | tf_op jit(solution)/shard_map/dot_general | solution.py:130
  231.7 0.8 copy.27
  232.6 54.7 %reduce-scatter.2.cloned.1.call-done = bf16[128,4096]{1,0:T(8,128)(2,1)} async-done(((bf16[512,4096]{1,0:T(8,128)(2,1)}), bf16[128,4096]{1,0:T(8,128)(2,1)}) %reduce-scatter.2.cloned.1.call-update) | async-done | bytes 1048592 | tf_op jit(solution)/shard_map/reduce_scatter | solution.py:129
  (76 shorter events, 6.4 us)
Async XLA Ops:
  7.2 49.3 %copy-start = (s32[256]{0:T(256)S(1)}, s32[256]{0:T(256)}, u32[]{:S(2)}) copy-start(s32[256]{0:T(256)} %param.15) | copy-start | bytes 3076
  7.2 4.9 %copy-start.2 = (bf16[64,768]{1,0:T(8,128)(2,1)S(1)}, bf16[64,768]{1,0:T(8,128)(2,1)}, u32[]{:S(2)}) copy-start(bf16[64,768]{1,0:T(8,128)(2,1)} %param.12) | copy-start | bytes 294916
  7.2 25.9 %copy-start.3 = (bf16[512,64]{0,1:T(8,128)(2,1)S(1)}, bf16[512,64]{0,1:T(8,128)(2,1)}, u32[]{:S(2)}) copy-start(bf16[512,64]{0,1:T(8,128)(2,1)} %param.13) | copy-start | bytes 196612
  7.2 61.0 %all-gather.4.cloned.1.call-start = ((), (), s32[]{:S(2)}) async-start(), calls=%async_computation.1 | async-start | bytes 5242880 | tf_op jit(solution)/shard_map/all_gather | solution.py:86
  8.0 49.2 %copy-start.1 = (s32[256]{0:T(256)S(1)}, s32[256]{0:T(256)}, u32[]{:S(2)}) copy-start(s32[256]{0:T(256)} %param.14) | copy-start | bytes 3076
  12.1 127.7 %all-gather.6.cloned.1.call-start = ((), (), s32[]{:S(2)}) async-start(), calls=%async_computation.2 | async-start | bytes 7077888 | tf_op jit(solution)/shard_map/all_gather | solution.py:76
  33.0 192.1 %all-gather.8.cloned.1.call-start = ((), (), s32[]{:S(2)}) async-start(), calls=%async_computation.3 | async-start | bytes 4718592 | tf_op jit(solution)/shard_map/all_gather | solution.py:76
  56.4 230.9 %reduce-scatter.2.cloned.1.call-start = ((), (), s32[]{:S(2)}) async-start(), calls=%async_computation.4 | async-start | bytes 5242880 | tf_op jit(solution)/shard_map/reduce_scatter | solution.py:129
Sparse Core Ops, SparseCore 0:
  12.2 53.1 all-gather.3
  67.2 72.4 all-gather.5
  141.5 53.3 all-gather.7
  231.8 55.3 reduce-scatter.1

commit v2 on v1

--- a/solution.py
+++ b/solution.py
@@ -26,9 +26,7 @@
 
 def fresh_scores_of(query_matrix, recent_key_rows, score_scale):
     scores = (
-        jnp.einsum(
-            "eksv,qkv->kseq", query_matrix, recent_key_rows, preferred_element_type=jnp.float32
-        )
+        jnp.einsum("esv,qv->seq", query_matrix, recent_key_rows, preferred_element_type=jnp.float32)
         * score_scale
     )
     count_new = query_matrix.shape[0]
@@ -43,15 +41,12 @@
 
 
 def padded_attention(
-    query_matrix, recent_key_rows, recent_value_rows, pool_view, page_row, length, score_scale
+    query_matrix, recent_key_rows, recent_value_rows, pool, page_row, length, score_scale
 ):
-    heads_here = pool_view.shape[2]
-    cache = pool_view[page_row].reshape(-1, heads_here, 2, HEAD)
+    cache = pool[page_row].reshape(-1, 2 * HEAD)
     span = cache.shape[0]
     cached_scores = (
-        jnp.einsum(
-            "nhgd,khd->hgnk", query_matrix, cache[:, :, 0], preferred_element_type=jnp.float32
-        )
+        jnp.einsum("ngd,kd->gnk", query_matrix, cache[:, :HEAD], preferred_element_type=jnp.float32)
         * score_scale
     )
     cached_scores = jnp.where(jnp.arange(span, dtype=jnp.int32) < length, cached_scores, -jnp.inf)
@@ -60,9 +55,9 @@
     cached_exp = jnp.exp(cached_scores - row_max)
     recent_exponent = jnp.exp(recent_score_rows - row_max)
     total = cached_exp.sum(-1) + recent_exponent.sum(-1)
-    summed_total = value_weighted_rows(cached_exp, cache[:, :, 1], "hgnk,khd->hgnd")
+    summed_total = value_weighted_rows(cached_exp, cache[:, HEAD:], "gnk,kd->gnd")
     summed_total = summed_total + value_weighted_rows(
-        recent_exponent, recent_value_rows, "tvqa,ats->tvqs"
+        recent_exponent, recent_value_rows, "vqa,as->vqs"
     )
     return summed_total / total[..., None]
 
@@ -83,7 +78,7 @@
     normed = (states * lax.rsqrt(mean_square + 1e-05) * norm_gain.astype(jnp.float32)).astype(
         jnp.bfloat16
     )
-    gathered = lax.all_gather(normed, TP_AXES, axis=0, tiled=True)
+    gathered = lax.all_gather(lax.all_gather(normed, "core", axis=0, tiled=True), "yhi", axis=0, tiled=True)
     tok_rows = gathered.shape[0]
     projected = jnp.dot(
         gathered,
@@ -93,16 +88,16 @@
     full_out = staged_gather(w_out, REQ_AXES, 1)
     group = QH // KVH
     heads_here = w_qkv.shape[1] // ((group + 2) * HEAD)
+    assert heads_here == 1 and pool.shape[2] == 2 * HEAD
     slot_count = tok_rows // NEW
     slot_ids = lax.axis_index(REQ_AXES) * slot_count + jnp.arange(slot_count, dtype=jnp.int32)
     slot_length = lengths[deal[slot_ids]]
     position = jnp.repeat(slot_length, NEW) + jnp.tile(jnp.arange(NEW, dtype=jnp.int32), slot_count)
-    projected = projected.reshape(tok_rows, heads_here, group + 2, HEAD)
-    queries = rotate(projected[:, :, :group].astype(jnp.float32), position).astype(jnp.bfloat16)
-    keys_new = rotate(projected[:, :, group].astype(jnp.float32), position).astype(jnp.bfloat16)
-    values_new = projected[:, :, group + 1]
-    new_kv = jnp.stack([keys_new, values_new], 2).reshape(tok_rows, heads_here * 2 * HEAD)
-    pool_view = pool.reshape(pool.shape[0], PAGE, heads_here, 2, HEAD)
+    projected = projected.reshape(tok_rows, group + 2, HEAD)
+    queries = rotate(projected[:, :group].astype(jnp.float32), position).astype(jnp.bfloat16)
+    keys_new = rotate(projected[:, group].astype(jnp.float32), position).astype(jnp.bfloat16)
+    values_new = projected[:, group + 1]
+    new_kv = jnp.concatenate([keys_new, values_new], 1)
     score_scale = 1.0 / math.sqrt(HEAD)
 
     def attend(local_slot):
@@ -116,22 +111,23 @@
             query_matrix,
             recent_key_rows,
             recent_value_rows,
-            pool_view,
+            pool,
             page_row,
             length,
             score_scale,
         )
         result = result.astype(jnp.bfloat16)
-        return result.transpose(2, 0, 1, 3).reshape(NEW, heads_here * group * HEAD)
+        return result.transpose(1, 0, 2).reshape(NEW, group * HEAD)
 
-    contexts = lax.map(attend, jnp.arange(slot_count, dtype=jnp.int32))
-    context = contexts.reshape(tok_rows, heads_here * group * HEAD)
-    attn_out = lax.psum_scatter(
-        jnp.dot(context, full_out, preferred_element_type=jnp.float32).astype(jnp.bfloat16),
-        TP_AXES,
-        scatter_dimension=0,
-        tiled=True,
-    )
+    n_hi = lax.axis_size("yhi")
+    n_core = lax.axis_size("core")
+    order = jnp.arange(slot_count, dtype=jnp.int32)
+    order = (order % n_hi) * n_core + order // n_hi
+    contexts = lax.map(attend, order)
+    context = contexts.reshape(tok_rows, group * HEAD)
+    partial = jnp.dot(context, full_out, preferred_element_type=jnp.float32).astype(jnp.bfloat16)
+    partial = lax.psum_scatter(partial, "core", scatter_dimension=0, tiled=True)
+    attn_out = lax.psum_scatter(partial, "yhi", scatter_dimension=0, tiled=True)
     return (attn_out, new_kv)
 
 

time: 295 us -> 319 us (1.081)
  waiting for transfers between devices: 126 us -> 184 us
  local copies, waits for them, and re-layouts: 51.8 us -> 21.4 us
    all_gather x1 -> x2, waiting for transfers between devices: 0.02 us -> 51.6 us  [the longest x1 31.1 us: per_device(): lax.all_gather(lax.all_gather(normed, 'core', axis=0, tiled=True), 'yhi',...]
    gather x8 -> x4, local copies, waits for them, and re-layouts: 34.3 us -> 13.8 us  [padded_attention(): cache = pool[page_row].reshape(-1, 2 * HEAD)]
    reshape x1 -> x0, local copies, waits for them, and re-layouts: 9.76 us -> none  [per_device(): pool_view = pool.reshape(pool.shape[0], PAGE, heads_here, 2, HEAD)]
    reduce_scatter x1 -> x2, waiting for transfers between devices: 54.7 us -> 58.2 us  [the longest x1 41.1 us: per_device(): attn_out = lax.psum_scatter(partial, 'yhi', scatter_dimension=0, tiled=True)]
  transfers between devices with their start and end apart: 4 -> 6, of which waited for: 2 -> 5; matrix products, arithmetic and copies ran while one was open for 30% -> 18% of each run, Pallas kernels for 0% -> 0%
where the time goes in v2:
time: 319 us; the launch traced here: 318 us
  waiting for transfers between devices  184 us (58%)
  blocking collectives  42.2 us (13%)
  matrix products  26.6 us (8%)
  local copies, waits for them, and re-layouts  21.4 us (7%)
  other arithmetic  19.2 us (6%)
  between operations  14.3 us (4%)
  loops' own time  10.8 us (3%)
    all_gather x2, waiting for transfers between devices, staged_gather(): values = lax.all_gather(values, name, axis=axis, tiled=True)  73.9 us
    all_gather x4, blocking collectives, staged_gather(): values = lax.all_gather(values, name, axis=axis, tiled=True)  42.2 us
    reduce_scatter x1, waiting for transfers between devices, per_device(): attn_out = lax.psum_scatter(partial, 'yhi', scatter_dimension=0, tiled=True)  41.1 us
    all_gather x1, waiting for transfers between devices, per_device(): lax.all_gather(lax.all_gather(normed, 'core', axis=0, tiled=True), 'yhi',...  31.1 us
    all_gather x1, waiting for transfers between devices, per_device(): lax.all_gather(normed, 'core', axis=0, tiled=True)  20.5 us
    reduce_scatter x1, waiting for transfers between devices, per_device(): partial = lax.psum_scatter(partial, 'core', scatter_dimension=0, tiled=True)  17.1 us
    gather x4, local copies, waits for them, and re-layouts, padded_attention(): cache = pool[page_row].reshape(-1, 2 * HEAD)  13.8 us
    another operation x1, loops' own time, per_device(): contexts = lax.map(attend, order)  10.8 us
  transfers between devices with their start and end apart: 6, of which 5 were waited for; matrix products, arithmetic and copies ran while one was open for 18% of the time, Pallas kernels for 0%

profile of v2, /device:TPU:1, one launch (start us, length us, event | category | flops | bytes accessed | tf_op | source)
XLA Modules:
  0.0 318.4 jit_solution(1034043087824753205)
XLA Ops:
  7.2 0.7 convert_element_type.48
  7.9 1.5 fusion.29
  9.5 2.5 fusion.31
  12.1 20.5 %all-gather.5.cloned.1.call-done = bf16[256,4096]{1,0:T(8,128)(2,1)} async-done(((bf16[128,4096]{1,0:T(8,128)(2,1)}), bf16[256,4096]{1,0:T(8,128)(2,1)}) %all-gather.5.cloned.1.call-update) | async-done | bytes 2097168 | tf_op jit(solution)/shard_map/all_gather | solution.py:81
  32.7 10.3 %all_gather.26 = bf16[256,768]{1,0:T(8,128)(2,1)S(1)} all-gather(bf16[64,768]{1,0:T(8,128)(2,1)S(1)} %copy-done.2), channel_id=1, replica_groups=mesh['z'=8,'ylo'=2,'x'=4,'yhi'=2,'core'=2] {'x'}, dimensions={0}, use_global_device_ids=true | all-gather | bytes 491520 | tf_op jit(solution)/shard_map/all_gather | solution.py:71
  43.0 8.9 %all_gather.27 = bf16[512,768]{1,0:T(8,128)(2,1)} all-gather(bf16[256,768]{1,0:T(8,128)(2,1)S(1)} %all_gather.26), channel_id=1, replica_groups=mesh['z'=8,'ylo'=2,'x'=4,'yhi'=2,'core'=2] {'ylo'}, dimensions={0}, use_global_device_ids=true | all-gather | bytes 1179648 | tf_op jit(solution)/shard_map/all_gather | solution.py:71
  52.0 10.6 %all_gather.29 = bf16[512,256]{0,1:T(8,128)(2,1)S(1)} all-gather(bf16[512,64]{0,1:T(8,128)(2,1)S(1)} %copy-done.3), channel_id=1, replica_groups=mesh['z'=8,'ylo'=2,'x'=4,'yhi'=2,'core'=2] {'x'}, dimensions={1}, use_global_device_ids=true | all-gather | bytes 327680 | tf_op jit(solution)/shard_map/all_gather | solution.py:71
  62.6 12.4 %all_gather.30 = bf16[512,512]{0,1:T(8,128)(2,1)} all-gather(bf16[512,256]{0,1:T(8,128)(2,1)S(1)} %all_gather.29), channel_id=1, replica_groups=mesh['z'=8,'ylo'=2,'x'=4,'yhi'=2,'core'=2] {'ylo'}, dimensions={1}, use_global_device_ids=true | all-gather | bytes 786432 | tf_op jit(solution)/shard_map/all_gather | solution.py:71
  75.1 0.6 gather_fusion.1
  75.8 0.6 gather_fusion.2
  76.5 31.1 %all-gather.7.cloned.1.call-done = bf16[512,4096]{1,0:T(8,128)(2,1)} async-done(((bf16[256,4096]{1,0:T(8,128)(2,1)}), bf16[512,4096]{1,0:T(8,128)(2,1)}) %all-gather.7.cloned.1.call-update) | async-done | bytes 4194320 | tf_op jit(solution)/shard_map/all_gather | solution.py:81
  107.6 73.8 %all-gather.9.cloned.1.call-done = bf16[4096,768]{1,0:T(8,128)(2,1)} async-done(((bf16[512,768]{1,0:T(8,128)(2,1)}), bf16[4096,768]{1,0:T(8,128)(2,1)}) %all-gather.9.cloned.1.call-update) | async-done | bytes 6291472 | tf_op jit(solution)/shard_map/all_gather | solution.py:71
  181.4 7.5 %convolution_convert_fusion.1 = bf16[512,768]{1,0:T(8,128)(2,1)S(1)} fusion(bf16[512,4096]{1,0:T(8,128)(2,1)} %all-gather.7.cloned.1.call-done, bf16[4096,768]{1,0:T(8,128)(2,1)} %all-gather.9.cloned.1.call-done), kind=kOutput, calls=%fused_computation.51 | convolution fusion | flops 3221618688 | bytes 11272192 | tf_op jit(solution)/shard_map/dot_general | solution.py:83
  189.4 0.6 subtract_convert_fusion.1
  190.2 55.7 %while.10 = (s32[]{:T(128)}, bf16[4,128,512]{2,1,0:T(8,128)(2,1)S(1)}, s32[4]{0:T(128)S(1)}, s32[4]{0:T(128)S(1)}, s32[4,24]{1,0:T(4,128)}, /*index=5*/bf16[96,1...) while((s32[]{:T(128)}, ...), condition=%wide.region_6.7_spmd, body=%wide.region_1.6_spmd.sunk | while | flops 856837184 | bytes 25968264 | solution.py:126
  190.2 0.6 dynamic_slice.56
  192.7 0.6 dynamic_slice.57
  193.3 0.6 iota_compare_fusion.4
  194.5 0.7 fusion.54
  195.2 3.4 %gather_fusion = bf16[24,128,256]{2,1,0:T(8,128)(2,1)S(1)} fusion(bf16[96,128,256]{2,1,0:T(8,128)(2,1)} %get-tuple-element.196, s32[1024]{0:T(1024)S(1)} %pad_clamp_fusion.4), kind=kCustom, calls=%fused_computation.clone.1 | custom fusion | bytes 3145824 | tf_op jit(solution)/shard_map/while/body/eval_jaxpr/gather | solution.py:46
  198.7 1.0 bitcast_reduce_fusion.2
  199.9 1.7 fusion.56
  201.7 2.0 fusion.57
  204.1 0.6 dynamic_slice.56
  206.6 0.6 dynamic_slice.57
  208.4 0.7 fusion.54
  209.1 3.5 %gather_fusion = bf16[24,128,256]{2,1,0:T(8,128)(2,1)S(1)} fusion(bf16[96,128,256]{2,1,0:T(8,128)(2,1)} %get-tuple-element.196, s32[1024]{0:T(1024)S(1)} %pad_clamp_fusion.4), kind=kCustom, calls=%fused_computation.clone.1 | custom fusion | bytes 3145824 | tf_op jit(solution)/shard_map/while/body/eval_jaxpr/gather | solution.py:46
  212.6 1.0 bitcast_reduce_fusion.2
  213.9 1.7 fusion.56
  215.6 2.0 fusion.57
  218.0 0.6 dynamic_slice.56
  220.6 0.6 dynamic_slice.57
  222.4 0.7 fusion.54
  223.1 3.5 %gather_fusion = bf16[24,128,256]{2,1,0:T(8,128)(2,1)S(1)} fusion(bf16[96,128,256]{2,1,0:T(8,128)(2,1)} %get-tuple-element.196, s32[1024]{0:T(1024)S(1)} %pad_clamp_fusion.4), kind=kCustom, calls=%fused_computation.clone.1 | custom fusion | bytes 3145824 | tf_op jit(solution)/shard_map/while/body/eval_jaxpr/gather | solution.py:46
  226.6 1.0 bitcast_reduce_fusion.2
  227.8 1.7 fusion.56
  229.6 2.0 fusion.57
  232.0 0.6 dynamic_slice.56
  234.5 0.6 dynamic_slice.57
  236.3 0.7 fusion.54
  237.0 3.4 %gather_fusion = bf16[24,128,256]{2,1,0:T(8,128)(2,1)S(1)} fusion(bf16[96,128,256]{2,1,0:T(8,128)(2,1)} %get-tuple-element.196, s32[1024]{0:T(1024)S(1)} %pad_clamp_fusion.4), kind=kCustom, calls=%fused_computation.clone.1 | custom fusion | bytes 3145824 | tf_op jit(solution)/shard_map/while/body/eval_jaxpr/gather | solution.py:46
  240.5 1.0 bitcast_reduce_fusion.2
  241.7 1.7 fusion.56
  243.5 2.0 fusion.57
  245.9 6.5 %convolution_convert_fusion = bf16[512,4096]{1,0:T(8,128)(2,1)} fusion(bf16[512,512]{1,0:T(8,128)(2,1)S(1)} %bitcast.107, bf16[512,4096]{0,1:T(8,128)(2,1)} %all-gather.11.cloned.1.call-done), kind=kOutput, calls=%fused_computation.45 | convolution fusion | flops 2149580800 | bytes 8912896 | tf_op jit(solution)/shard_map/dot_general | solution.py:128
  252.5 17.1 %reduce-scatter.3.cloned.1.call-done = bf16[256,4096]{1,0:T(8,128)(2,1)} async-done(((bf16[512,4096]{1,0:T(8,128)(2,1)}), bf16[256,4096]{1,0:T(8,128)(2,1)}) %reduce-scatter.3.cloned.1.call-update) | async-done | bytes 2097168 | tf_op jit(solution)/shard_map/reduce_scatter | solution.py:129
  269.6 0.8 copy.24
  270.5 41.1 %reduce-scatter.5.cloned.1.call-done = bf16[128,4096]{1,0:T(8,128)(2,1)} async-done(((bf16[256,4096]{1,0:T(8,128)(2,1)}), bf16[128,4096]{1,0:T(8,128)(2,1)}) %reduce-scatter.5.cloned.1.call-update) | async-done | bytes 1048592 | tf_op jit(solution)/shard_map/reduce_scatter | solution.py:130
  (76 shorter events, 5.5 us)
Async XLA Ops:
  7.2 67.9 %copy-start = (s32[256]{0:T(256)S(1)}, s32[256]{0:T(256)}, u32[]{:S(2)}) copy-start(s32[256]{0:T(256)} %param.15) | copy-start | bytes 3076
  7.2 25.5 %copy-start.2 = (bf16[64,768]{1,0:T(8,128)(2,1)S(1)}, bf16[64,768]{1,0:T(8,128)(2,1)}, u32[]{:S(2)}) copy-start(bf16[64,768]{1,0:T(8,128)(2,1)} %param.12) | copy-start | bytes 294916
  7.2 25.4 %all-gather.5.cloned.1.call-start = ((), (), s32[]{:S(2)}) async-start(), calls=%async_computation.2 | async-start | bytes 3145728 | tf_op jit(solution)/shard_map/all_gather | solution.py:81
  7.9 44.1 %copy-start.3 = (bf16[512,64]{0,1:T(8,128)(2,1)S(1)}, bf16[512,64]{0,1:T(8,128)(2,1)}, u32[]{:S(2)}) copy-start(bf16[512,64]{0,1:T(8,128)(2,1)} %param.13) | copy-start | bytes 196612
  12.0 63.7 %copy-start.1 = (s32[256]{0:T(256)S(1)}, s32[256]{0:T(256)}, u32[]{:S(2)}) copy-start(s32[256]{0:T(256)} %param.14) | copy-start | bytes 3076
  12.1 95.6 %all-gather.7.cloned.1.call-start = ((), (), s32[]{:S(2)}) async-start(), calls=%async_computation.3 | async-start | bytes 6291456 | tf_op jit(solution)/shard_map/all_gather | solution.py:81
  32.7 148.8 %all-gather.9.cloned.1.call-start = ((), (), s32[]{:S(2)}) async-start(), calls=%async_computation.4 | async-start | bytes 7077888 | tf_op jit(solution)/shard_map/all_gather | solution.py:71
  52.0 193.9 %all-gather.11.cloned.1.call-start = ((), (), s32[]{:S(2)}) async-start(), calls=%async_computation.5 | async-start | bytes 4718592 | tf_op jit(solution)/shard_map/all_gather | solution.py:71
  75.0 194.6 %reduce-scatter.3.cloned.1.call-start = ((), (), s32[]{:S(2)}) async-start(), calls=%async_computation.6 | async-start | bytes 6291456 | tf_op jit(solution)/shard_map/reduce_scatter | solution.py:129
  252.4 59.1 %reduce-scatter.5.cloned.1.call-start = ((), (), s32[]{:S(2)}) async-start(), calls=%async_computation.7 | async-start | bytes 3145728 | tf_op jit(solution)/shard_map/reduce_scatter | solution.py:130
Sparse Core Ops, SparseCore 0:
  12.2 20.4 all-gather.4
  34.4 73.1 all-gather.6
  109.4 71.9 all-gather.8
  183.1 53.3 all-gather.10
  252.6 16.9 reduce-scatter.2
  272.5 38.9 reduce-scatter.4

commit v3 on v2

--- a/solution.py
+++ b/solution.py
@@ -78,7 +78,13 @@
     normed = (states * lax.rsqrt(mean_square + 1e-05) * norm_gain.astype(jnp.float32)).astype(
         jnp.bfloat16
     )
-    gathered = lax.all_gather(lax.all_gather(normed, "core", axis=0, tiled=True), "yhi", axis=0, tiled=True)
+    n_tp = lax.axis_size(TP_AXES)
+    me = lax.axis_index(TP_AXES)
+    arrived = [normed] + [
+        lax.ppermute(normed, TP_AXES, perm=[(s, (s - k) % n_tp) for s in range(n_tp)])
+        for k in range(1, n_tp)
+    ]
+    gathered = jnp.concatenate(arrived, 0)
     tok_rows = gathered.shape[0]
     projected = jnp.dot(
         gathered,
@@ -90,45 +96,39 @@
     heads_here = w_qkv.shape[1] // ((group + 2) * HEAD)
     assert heads_here == 1 and pool.shape[2] == 2 * HEAD
     slot_count = tok_rows // NEW
-    slot_ids = lax.axis_index(REQ_AXES) * slot_count + jnp.arange(slot_count, dtype=jnp.int32)
+    step_slot = (me + jnp.arange(slot_count, dtype=jnp.int32)) % slot_count
+    slot_ids = lax.axis_index(REQ_AXES) * slot_count + step_slot
     slot_length = lengths[deal[slot_ids]]
     position = jnp.repeat(slot_length, NEW) + jnp.tile(jnp.arange(NEW, dtype=jnp.int32), slot_count)
     projected = projected.reshape(tok_rows, group + 2, HEAD)
     queries = rotate(projected[:, :group].astype(jnp.float32), position).astype(jnp.bfloat16)
     keys_new = rotate(projected[:, group].astype(jnp.float32), position).astype(jnp.bfloat16)
     values_new = projected[:, group + 1]
-    new_kv = jnp.concatenate([keys_new, values_new], 1)
+    stepped_kv = jnp.concatenate([keys_new, values_new], 1)
+    doubled = jnp.concatenate([stepped_kv, stepped_kv], 0)
+    new_kv = lax.dynamic_slice_in_dim(doubled, ((slot_count - me) % slot_count) * NEW, tok_rows, 0)
     score_scale = 1.0 / math.sqrt(HEAD)
 
-    def attend(local_slot):
-        begin = local_slot * NEW
-        query_matrix = lax.dynamic_slice_in_dim(queries, begin, NEW, 0)
-        recent_key_rows = lax.dynamic_slice_in_dim(keys_new, begin, NEW, 0)
-        recent_value_rows = lax.dynamic_slice_in_dim(values_new, begin, NEW, 0)
-        page_row = pages[local_slot]
-        length = slot_length[local_slot]
+    total = None
+    for k in range(slot_count):
+        rows = slice(k * NEW, (k + 1) * NEW)
         result = padded_attention(
-            query_matrix,
-            recent_key_rows,
-            recent_value_rows,
+            queries[rows],
+            keys_new[rows],
+            values_new[rows],
             pool,
-            page_row,
-            length,
+            pages[step_slot[k]],
+            slot_length[k],
             score_scale,
         )
-        result = result.astype(jnp.bfloat16)
-        return result.transpose(1, 0, 2).reshape(NEW, group * HEAD)
-
-    n_hi = lax.axis_size("yhi")
-    n_core = lax.axis_size("core")
-    order = jnp.arange(slot_count, dtype=jnp.int32)
-    order = (order % n_hi) * n_core + order // n_hi
-    contexts = lax.map(attend, order)
-    context = contexts.reshape(tok_rows, group * HEAD)
-    partial = jnp.dot(context, full_out, preferred_element_type=jnp.float32).astype(jnp.bfloat16)
-    partial = lax.psum_scatter(partial, "core", scatter_dimension=0, tiled=True)
-    attn_out = lax.psum_scatter(partial, "yhi", scatter_dimension=0, tiled=True)
-    return (attn_out, new_kv)
+        context = result.astype(jnp.bfloat16).transpose(1, 0, 2).reshape(NEW, group * HEAD)
+        partial = jnp.dot(context, full_out, preferred_element_type=jnp.float32).astype(
+            jnp.bfloat16
+        )
+        if k:
+            partial = lax.ppermute(partial, TP_AXES, perm=[(s, (s + k) % n_tp) for s in range(n_tp)])
+        total = partial.astype(jnp.float32) if total is None else total + partial.astype(jnp.float32)
+    return (total.astype(jnp.bfloat16), new_kv)
 
 
 def solution(mesh):

time: 319 us -> 234 us (0.73)
  waiting for transfers between devices: 184 us -> 28.7 us
  blocking collectives: 42.2 us -> 69.3 us
  matrix products: 26.6 us -> 44.9 us
  starting transfers between devices: 0.24 us -> 12 us
  loops' own time: 10.8 us -> 0 us
  local copies, waits for them, and re-layouts: 21.4 us -> 29.4 us
  between operations: 14.3 us -> 22.2 us
  other arithmetic: 19.2 us -> 25.9 us
    all_gather x2, waiting for transfers between devices: 73.9 us -> 0.02 us  [staged_gather(): values = lax.all_gather(values, name, axis=axis, tiled=True)]
    reduce_scatter x2 -> x0, waiting for transfers between devices: 58.2 us -> none  [the longest x1 41.1 us: per_device(): attn_out = lax.psum_scatter(partial, 'yhi', scatter_dimension=0, tiled=True)]
    all_gather x2 -> x0, waiting for transfers between devices: 51.6 us -> none  [the longest x1 31.1 us: per_device(): lax.all_gather(lax.all_gather(normed, 'core', axis=0, tiled=True), 'yhi',...]
    ppermute x0 -> x6, waiting for transfers between devices: none -> 28.7 us  [the longest x3 28.7 us: per_device(): lax.ppermute(partial, TP_AXES, perm=[(s, (s + k) % n_tp) for s in range(n...]
    all_gather x4, blocking collectives: 42.2 us -> 69.3 us  [staged_gather(): values = lax.all_gather(values, name, axis=axis, tiled=True)]
    ppermute x0 -> x6, starting transfers between devices: none -> 11.9 us  [the longest x3 8.45 us: per_device(): lax.ppermute(normed, TP_AXES, perm=[(s, (s - k) % n_tp) for s in range(n_...]
    another operation x1 -> x0, loops' own time: 10.8 us -> none  [per_device(): contexts = lax.map(attend, order)]
    dot_general x8, matrix products: 7.71 us -> 16.4 us  [value_weighted_rows(): jnp.einsum(form, weights.astype(jnp.bfloat16), values, preferred_element_...]
  transfers between devices with their start and end apart: 6 -> 8, of which waited for: 5 -> 2; matrix products, arithmetic and copies ran while one was open for 18% -> 39% of each run, Pallas kernels for 0% -> 0%
where the time goes in v3:
time: 234 us; the launch traced here: 232 us
  blocking collectives  69.3 us (30%)
  matrix products  44.9 us (19%)
  local copies, waits for them, and re-layouts  29.4 us (13%)
  waiting for transfers between devices  28.7 us (12%)
  other arithmetic  25.9 us (11%)
  between operations  22.2 us (9%)
  starting transfers between devices  12 us (5%)
    all_gather x4, blocking collectives, staged_gather(): values = lax.all_gather(values, name, axis=axis, tiled=True)  69.3 us
    ppermute x3, waiting for transfers between devices, per_device(): lax.ppermute(partial, TP_AXES, perm=[(s, (s + k) % n_tp) for s in range(n...  28.7 us
    dot_general x8, matrix products, value_weighted_rows(): jnp.einsum(form, weights.astype(jnp.bfloat16), values, preferred_element_...  16.4 us
    gather x4, local copies, waits for them, and re-layouts, padded_attention(): cache = pool[page_row].reshape(-1, 2 * HEAD)  16.2 us
    dot_general x4, matrix products, per_device(): jnp.dot(context, full_out, preferred_element_type=jnp.float32)  13.4 us
    reduce_sum x8, other arithmetic, padded_attention(): total = cached_exp.sum(-1) + recent_exponent.sum(-1)  11 us
    ppermute x3, starting transfers between devices, per_device(): lax.ppermute(normed, TP_AXES, perm=[(s, (s - k) % n_tp) for s in range(n_...  8.45 us
    dot_general x1, matrix products, per_device(): jnp.dot(gathered, staged_gather(w_qkv, REQ_AXES, 0), preferred_element_ty...  8.36 us
  transfers between devices with their start and end apart: 8, of which 2 were waited for; matrix products, arithmetic and copies ran while one was open for 39% of the time, Pallas kernels for 0%

profile of v3, /device:TPU:1, one launch (start us, length us, event | category | flops | bytes accessed | tf_op | source)
XLA Modules:
  0.0 232.5 jit_solution(2098652944878820966)
XLA Ops:
  7.2 11.9 %all_gather.18 = bf16[256,768]{1,0:T(8,128)(2,1)S(1)} all-gather(bf16[64,768]{1,0:T(8,128)(2,1)} %param.10), channel_id=1, replica_groups=mesh['z'=8,'ylo'=2,'x'=4,'yhi'=2,'core'=2] {'x'}, dimensions={0}, use_global_device_ids=true | all-gather | bytes 491520 | tf_op jit(solution)/shard_map/all_gather | solution.py:71
  19.2 7.6 %all_gather.19 = bf16[512,768]{1,0:T(8,128)(2,1)} all-gather(bf16[256,768]{1,0:T(8,128)(2,1)S(1)} %all_gather.18), channel_id=1, replica_groups=mesh['z'=8,'ylo'=2,'x'=4,'yhi'=2,'core'=2] {'ylo'}, dimensions={0}, use_global_device_ids=true | all-gather | bytes 1179648 | tf_op jit(solution)/shard_map/all_gather | solution.py:71
  27.5 1.5 fusion.33
  29.1 2.5 %fusion.35 = bf16[128,4096]{1,0:T(8,128)(2,1)} fusion(bf16[128,4096]{1,0:T(8,128)(2,1)} %param.8, f32[4096]{0:T(1024)S(1)} %convert_element_type.102, f32[128]{0:T(128)S(1)} %add_rsqrt_fusion), kind=kLoop, calls=%fused_computation.55 | loop fusion | flops 2097152 | bytes 2114048 | tf_op jit(solution)/shard_map/convert_element_type | solution.py:78
  31.6 5.3 %collective-permute-start = (bf16[128,4096]{1,0:T(8,128)(2,1)}, bf16[128,4096]{1,0:T(8,128)(2,1)}, u32[]{:S(2)}, u32[]{:S(2)}) collective-permute-start(bf16[128,4096]{1,0:T(8,128)(2,1)} %fusion.35), channel_id=1, source_target_pairs={{0,3},{1,0},{2,1},{3,2},{4,7},{5,4},{6,5},{7,6},{8,11},{9,8},{10,9... | collective-permute-start | bytes 3145736 | tf_op jit(solution)/shard_map/ppermute | solution.py:84
  36.9 2.3 collective-permute-start.1
  40.1 10.5 %all_gather.21 = bf16[512,256]{0,1:T(8,128)(2,1)S(1)} all-gather(bf16[512,64]{0,1:T(8,128)(2,1)} %param.11), channel_id=1, replica_groups=mesh['z'=8,'ylo'=2,'x'=4,'yhi'=2,'core'=2] {'x'}, dimensions={1}, use_global_device_ids=true | all-gather | bytes 327680 | tf_op jit(solution)/shard_map/all_gather | solution.py:71
  50.6 39.3 %all_gather.22 = bf16[512,512]{0,1:T(8,128)(2,1)} all-gather(bf16[512,256]{0,1:T(8,128)(2,1)S(1)} %all_gather.21), channel_id=1, replica_groups=mesh['z'=8,'ylo'=2,'x'=4,'yhi'=2,'core'=2] {'ylo'}, dimensions={1}, use_global_device_ids=true | all-gather | bytes 786432 | tf_op jit(solution)/shard_map/all_gather | solution.py:71
  99.0 3.5 %gather_fusion.2 = bf16[24,128,256]{2,1,0:T(8,128)(2,1)S(1)} fusion(bf16[96,128,256]{2,1,0:T(8,128)(2,1)} %param.15, s32[1024]{0:T(1024)S(1)} %get-tuple-element.45), kind=kCustom, calls=%fused_computation.2 | custom fusion | bytes 3145824 | tf_op jit(solution)/shard_map/gather | solution.py:46
  102.4 4.7 %gather_fusion.3 = bf16[24,128,256]{2,1,0:T(8,128)(2,1)} fusion(bf16[96,128,256]{2,1,0:T(8,128)(2,1)} %param.15, s32[1024]{0:T(1024)S(1)} %get-tuple-element.44), kind=kCustom, calls=%fused_computation.3 | custom fusion | bytes 3145824 | tf_op jit(solution)/shard_map/gather | solution.py:46
  107.2 4.6 %gather_fusion.4 = bf16[24,128,256]{2,1,0:T(8,128)(2,1)} fusion(bf16[96,128,256]{2,1,0:T(8,128)(2,1)} %param.15, s32[1024]{0:T(1024)S(1)} %get-tuple-element.43), kind=kCustom, calls=%fused_computation.4 | custom fusion | bytes 3145824 | tf_op jit(solution)/shard_map/gather | solution.py:46
  111.8 3.4 %gather_fusion.5 = bf16[24,128,256]{2,1,0:T(8,128)(2,1)S(1)} fusion(bf16[96,128,256]{2,1,0:T(8,128)(2,1)} %param.15, s32[1024]{0:T(1024)S(1)} %get-tuple-element.42), kind=kCustom, calls=%fused_computation.5 | custom fusion | bytes 3145824 | tf_op jit(solution)/shard_map/gather | solution.py:46
  119.8 8.4 %fusion.36 = bf16[512,768]{1,0:T(8,128)(2,1)} fusion(bf16[4096,768]{1,0:T(8,128)(2,1)} %all-gather.3.cloned.1.call-done, bf16[128,4096]{1,0:T(8,128)(2,1)} %collective-permute-done.2, bf16[128,4096]{1,0:T(8,128)(2,1)} %collective-permute-done.1, bf16[128,4096]{1,0:T(8,128)(2,1)} %collective-permute-done, bf16[128,4096]{1,0:T(8,128)(2,1)} %fusion.35), kind=kOutput, calls=%fused_computation.57 | convolution fusion | flops 3238395904 | bytes 11272192 | tf_op jit(solution)/shard_map/dot_general | solution.py:89
  128.1 2.3 copy.47
  130.4 1.7 slice_bitcast_fusion.16
  132.1 1.9 slice.173
  134.0 1.3 subtract_convert_fusion.1
  135.2 1.0 copy.49
  136.2 1.7 copy.50
  138.0 2.0 copy.92
  140.0 1.1 convert_element_type.105
  141.1 1.4 subtract_convert_fusion
  142.6 1.1 fusion.136
  143.7 1.1 bitcast_reduce_fusion.3
  145.2 1.1 bitcast_reduce_fusion.2
  146.3 1.0 fusion.135
  147.8 1.1 bitcast_reduce_fusion.1
  149.2 1.0 bitcast_reduce_fusion
  150.9 2.2 fusion.7
  153.1 1.7 fusion.25
  154.9 1.6 fusion.56
  156.5 2.5 %fusion.5 = f32[4,128]{1,0:T(4,128)} fusion(f32[3072,128,4]{1,0,2:T(8,128)S(1)} %get-tuple-element.35, f32[4,128]{1,0:T(4,128)S(1)} %max.28, pred[3072]{0:T(1024)(128)(4,1)S(1)} %iota_compare_fusion.4), kind=kLoop, calls=%fused_computation.27 | loop fusion | flops 6290944 | bytes 6298624 | tf_op jit(solution)/shard_map/reduce_sum | solution.py:57
  159.0 2.0 fusion.9
  161.0 2.6 %fusion.11 = f32[4,128]{1,0:T(4,128)} fusion(f32[3072,128,4]{1,0,2:T(8,128)S(1)} %get-tuple-element.27, f32[4,128]{1,0:T(4,128)S(1)} %max.31, pred[3072]{0:T(1024)(128)(4,1)S(1)} %iota_compare_fusion.1), kind=kLoop, calls=%fused_computation.33 | loop fusion | flops 6290944 | bytes 6298624 | tf_op jit(solution)/shard_map/reduce_sum | solution.py:57
  163.5 2.5 %fusion.23 = f32[4,128,128]{1,2,0:T(8,128)} fusion(f32[3072,128,4]{1,0,2:T(8,128)S(1)} %get-tuple-element.31, f32[4,128]{1,0:T(4,128)S(1)} %max.30, pred[3072]{0:T(1024)(128)(4,1)S(1)} %iota_compare_fusion.2, bf16[3072,256]{1,0:T(8,128)(2,1)S(1)} %bitcast.236), kind=kOutput, calls=%fused_computation.44 | convolution fusion | flops 408944640 | bytes 7345152 | tf_op jit(solution)/shard_map/gnk,kd->gnd/dot_general | solution.py:38
  166.0 2.5 %fusion.21 = f32[4,128,128]{1,2,0:T(8,128)} fusion(f32[3072,128,4]{1,0,2:T(8,128)S(1)} %get-tuple-element.27, f32[4,128]{1,0:T(4,128)S(1)} %max.31, pred[3072]{0:T(1024)(128)(4,1)S(1)} %iota_compare_fusion.1, bf16[3072,256]{1,0:T(8,128)(2,1)S(1)} %bitcast.234), kind=kOutput, calls=%fused_computation.43 | convolution fusion | flops 408944640 | bytes 7345152 | tf_op jit(solution)/shard_map/gnk,kd->gnd/dot_general | solution.py:38
  168.5 3.9 %convolution_convert_fusion.2 = bf16[128,4096]{1,0:T(8,128)(2,1)S(1)} fusion(bf16[128,512]{0,1:T(8,128)(2,1)} %bitcast.246, bf16[512,4096]{0,1:T(8,128)(2,1)} %all-gather.5.cloned.1.call-done), kind=kOutput, calls=%fused_computation.24 | convolution fusion | flops 537395200 | bytes 5373952 | tf_op jit(solution)/shard_map/dot_general | solution.py:125
  172.4 2.2 collective-permute-start.3
  174.6 1.0 fusion.72
  175.6 1.3 fusion.57
  176.9 2.5 %convolution_convert_fusion.1 = bf16[128,4096]{1,0:T(8,128)(2,1)} fusion(bf16[128,512]{0,1:T(8,128)(2,1)S(1)} %bitcast.247, bf16[512,4096]{0,1:T(8,128)(2,1)S(1)} %copy-done.3), kind=kOutput, calls=%fused_computation.23 | convolution fusion | flops 537395200 | bytes 5373952 | tf_op jit(solution)/shard_map/dot_general | solution.py:125
  180.0 1.0 fusion.58
  181.0 2.5 %convolution_convert_fusion = bf16[128,4096]{1,0:T(8,128)(2,1)} fusion(bf16[128,512]{0,1:T(8,128)(2,1)S(1)} %bitcast.248, bf16[512,4096]{0,1:T(8,128)(2,1)S(1)} %copy-done.3), kind=kOutput, calls=%fused_computation.22 | convolution fusion | flops 537395200 | bytes 5373952 | tf_op jit(solution)/shard_map/dot_general | solution.py:125
  186.5 5.0 %fusion.27 = f32[4,128,128]{1,2,0:T(8,128)S(1)} fusion(f32[3072,128,4]{1,0,2:T(8,128)} %copy-done.5, f32[4,128]{1,0:T(4,128)S(1)} %copy-done.13, pred[3072]{0:T(1024)(128)(4,1)S(1)} %iota_compare_fusion.4, bf16[3072,256]{1,0:T(8,128)(2,1)S(1)} %bitcast.232), kind=kOutput, calls=%fused_computation.46 | convolution fusion | flops 408944640 | bytes 7345152 | tf_op jit(solution)/shard_map/gnk,kd->gnd/dot_general | solution.py:38
  191.5 1.0 fusion.55
  192.4 22.3 %collective-permute-done.4 = bf16[128,4096]{1,0:T(8,128)(2,1)} collective-permute-done((bf16[128,4096]{1,0:T(8,128)(2,1)}, bf16[128,4096]{1,0:T(8,128)(2,1)}, u32[]{:S(2)}, u32[]{:S(2)}) %collective-permute-start.4) | collective-permute-done | bytes 1048608 | tf_op jit(solution)/shard_map/ppermute | solution.py:129
  214.7 6.3 %collective-permute-done.5 = bf16[128,4096]{1,0:T(8,128)(2,1)} collective-permute-done((bf16[128,4096]{1,0:T(8,128)(2,1)}, bf16[128,4096]{1,0:T(8,128)(2,1)}, u32[]{:S(2)}, u32[]{:S(2)}) %collective-permute-start.5) | collective-permute-done | bytes 1048608 | tf_op jit(solution)/shard_map/ppermute | solution.py:129
  221.1 4.6 %add_convert_fusion = bf16[128,4096]{1,0:T(8,128)(2,1)} fusion(bf16[128,4096]{1,0:T(8,128)(2,1)} %collective-permute-done.5, bf16[128,4096]{1,0:T(8,128)(2,1)} %collective-permute-done.4, bf16[128,4096]{1,0:T(8,128)(2,1)} %collective-permute-done.3, bf16[128,512]{0,1:T(8,128)(2,1)S(1)} %bitcast.245, bf16[512,4096]{0,1:T(8,128)(2,1)S(1)} %copy-done.4), kind=kOutput, calls=%fused_computation.56 | convolution fusion | flops 541589504 | bytes 8519680 | tf_op jit(solution)/shard_map/dot_general | solution.py:125
  (94 shorter events, 13.2 us)
Async XLA Ops:
  7.2 88.5 %copy-start = (s32[256]{0:T(256)S(1)}, s32[256]{0:T(256)}, u32[]{:S(2)}) copy-start(s32[256]{0:T(256)} %param.13) | copy-start | bytes 3076
  7.2 91.7 %copy-start.20 = (s32[4,24]{1,0:T(4,128)S(1)}, s32[4,24]{1,0:T(4,128)}, u32[]{:S(2)}) copy-start(s32[4,24]{1,0:T(4,128)} %param.14) | copy-start | bytes 1156
  7.2 112.6 %all-gather.3.cloned.1.call-start = ((), (), s32[]{:S(2)}) async-start(), calls=%async_computation | async-start | bytes 7077888 | tf_op jit(solution)/shard_map/all_gather | solution.py:71
  26.8 141.7 %all-gather.5.cloned.1.call-start = ((), (), s32[]{:S(2)}) async-start(), calls=%async_computation.1 | async-start | bytes 4718592 | tf_op jit(solution)/shard_map/all_gather | solution.py:71
  31.6 88.1 %collective-permute-start = (bf16[128,4096]{1,0:T(8,128)(2,1)}, bf16[128,4096]{1,0:T(8,128)(2,1)}, u32[]{:S(2)}, u32[]{:S(2)}) collective-permute-start(bf16[128,4096]{1,0:T(8,128)(2,1)} %fusion.35), channel_id=1, source_target_pairs={{0,3},{1,0},{2,1},{3,2},{4,7},{5,4},{6,5},{7,6},{8,11},{9,8},{10,9... | collective-permute-start | bytes 3145736 | tf_op jit(solution)/shard_map/ppermute | solution.py:84
  36.9 82.8 %collective-permute-start.1 = (bf16[128,4096]{1,0:T(8,128)(2,1)}, bf16[128,4096]{1,0:T(8,128)(2,1)}, u32[]{:S(2)}, u32[]{:S(2)}) collective-permute-start(bf16[128,4096]{1,0:T(8,128)(2,1)} %fusion.35), channel_id=1, source_target_pairs={{0,2},{1,3},{2,0},{3,1},{4,6},{5,7},{6,4},{7,5},{8,10},{9,11},{10,... | collective-permute-start | bytes 3145736 | tf_op jit(solution)/shard_map/ppermute | solution.py:84
  39.2 80.5 %collective-permute-start.2 = (bf16[128,4096]{1,0:T(8,128)(2,1)}, bf16[128,4096]{1,0:T(8,128)(2,1)}, u32[]{:S(2)}, u32[]{:S(2)}) collective-permute-start(bf16[128,4096]{1,0:T(8,128)(2,1)} %fusion.35), channel_id=1, source_target_pairs={{0,1},{1,2},{2,3},{3,0},{4,5},{5,6},{6,7},{7,4},{8,9},{9,10},{10,1... | collective-permute-start | bytes 3145736 | tf_op jit(solution)/shard_map/ppermute | solution.py:84
  99.0 16.3 %copy-start.2 = (s32[256]{0:T(256)S(1)}, s32[256]{0:T(256)}, u32[]{:S(2)}) copy-start(s32[256]{0:T(256)} %param.12) | copy-start | bytes 3076
  142.6 2.2 copy-start.11
  143.6 6.6 %copy-start.8 = (f32[4,128,128]{1,2,0:T(8,128)}, f32[4,128,128]{1,2,0:T(8,128)S(1)}, u32[]{:S(2)}) copy-start(f32[4,128,128]{1,2,0:T(8,128)S(1)} %get-tuple-element.37) | copy-start | bytes 786436
  143.6 1.5 copy-start.7
  144.7 11.8 %copy-start.5 = (f32[3072,128,4]{1,0,2:T(8,128)}, f32[3072,128,4]{1,0,2:T(8,128)S(1)}, u32[]{:S(2)}) copy-start(f32[3072,128,4]{1,0,2:T(8,128)S(1)} %get-tuple-element.35) | copy-start | bytes 18874372
  144.8 11.7 %copy-start.12 = (f32[4,128]{1,0:T(4,128)}, f32[4,128]{1,0:T(4,128)S(1)}, u32[]{:S(2)}) copy-start(f32[4,128]{1,0:T(4,128)S(1)} %max.28) | copy-start | bytes 6148
  145.2 2.6 %copy-start.6 = (bf16[24,128,256]{2,1,0:T(8,128)(2,1)S(1)}, bf16[24,128,256]{2,1,0:T(8,128)(2,1)}, u32[]{:S(2)}) copy-start(bf16[24,128,256]{2,1,0:T(8,128)(2,1)} %gather_fusion.4) | copy-start | bytes 4718596
  148.9 14.7 %copy-start.16 = (f32[4,128]{1,0:T(4,128)}, f32[4,128]{1,0:T(4,128)S(1)}, u32[]{:S(2)}) copy-start(f32[4,128]{1,0:T(4,128)S(1)} %max.30) | copy-start | bytes 6148
  150.2 15.8 %copy-start.14 = (f32[4,128]{1,0:T(4,128)}, f32[4,128]{1,0:T(4,128)S(1)}, u32[]{:S(2)}) copy-start(f32[4,128]{1,0:T(4,128)S(1)} %max.31) | copy-start | bytes 6148
  166.0 8.6 %copy-start.17 = (f32[4,128]{1,0:T(4,128)S(1)}, f32[4,128]{1,0:T(4,128)}, u32[]{:S(2)}) copy-start(f32[4,128]{1,0:T(4,128)} %copy-done.16) | copy-start | bytes 6148
  168.5 11.4 %copy-start.15 = (f32[4,128]{1,0:T(4,128)S(1)}, f32[4,128]{1,0:T(4,128)}, u32[]{:S(2)}) copy-start(f32[4,128]{1,0:T(4,128)} %copy-done.14) | copy-start | bytes 6148
  168.5 11.5 %copy-start.19 = (f32[4,128]{1,0:T(4,128)S(1)}, f32[4,128]{1,0:T(4,128)}, u32[]{:S(2)}) copy-start(f32[4,128]{1,0:T(4,128)} %fusion.11) | copy-start | bytes 6148
  168.5 11.5 %copy-start.21 = (f32[4,128,128]{1,2,0:T(8,128)S(1)}, f32[4,128,128]{1,2,0:T(8,128)}, u32[]{:S(2)}) copy-start(f32[4,128,128]{1,2,0:T(8,128)} %fusion.21) | copy-start | bytes 786436
  168.5 8.4 %copy-start.3 = (bf16[512,4096]{0,1:T(8,128)(2,1)S(1)}, bf16[512,4096]{0,1:T(8,128)(2,1)}, u32[]{:S(2)}) copy-start(bf16[512,4096]{0,1:T(8,128)(2,1)} %all-gather.5.cloned.1.call-done) | copy-start | bytes 12582916
  172.4 20.0 %collective-permute-start.3 = (bf16[128,4096]{1,0:T(8,128)(2,1)S(1)}, bf16[128,4096]{1,0:T(8,128)(2,1)}, u32[]{:S(2)}, u32[]{:S(2)}) collective-permute-start(bf16[128,4096]{1,0:T(8,128)(2,1)S(1)} %convolution_convert_fusion.2), channel_id=1, source_target_pairs={{0,1},{1,2},{2,3},{3,0},{4,5},{5,6},{6,7},{7,4},{8,9},{9,10},{10,1... | collective-permute-start | bytes 3145736 | tf_op jit(solution)/shard_map/ppermute | solution.py:129
  176.9 7.3 %copy-start.10 = (bf16[512,128]{0,1:T(8,128)(2,1)S(1)}, bf16[512,128]{0,1:T(8,128)(2,1)}, u32[]{:S(2)}) copy-start(bf16[512,128]{0,1:T(8,128)(2,1)} %get-tuple-element.8) | copy-start | bytes 393220
  176.9 8.8 %copy-start.18 = (f32[4,128]{1,0:T(4,128)S(1)}, f32[4,128]{1,0:T(4,128)}, u32[]{:S(2)}) copy-start(f32[4,128]{1,0:T(4,128)} %fusion.68) | copy-start | bytes 6148
  176.9 9.5 %copy-start.13 = (f32[4,128]{1,0:T(4,128)S(1)}, f32[4,128]{1,0:T(4,128)}, u32[]{:S(2)}) copy-start(f32[4,128]{1,0:T(4,128)} %copy-done.12) | copy-start | bytes 6148
  179.4 35.3 %collective-permute-start.4 = (bf16[128,4096]{1,0:T(8,128)(2,1)}, bf16[128,4096]{1,0:T(8,128)(2,1)}, u32[]{:S(2)}, u32[]{:S(2)}) collective-permute-start(bf16[128,4096]{1,0:T(8,128)(2,1)} %convolution_convert_fusion.1), channel_id=1, source_target_pairs={{0,2},{1,3},{2,0},{3,1},{4,6},{5,7},{6,4},{7,5},{8,10},{9,11},{10,... | collective-permute-start | bytes 3145736 | tf_op jit(solution)/shard_map/ppermute | solution.py:129
  183.4 8.0 %copy-start.9 = (f32[4,128,128]{1,2,0:T(8,128)S(1)}, f32[4,128,128]{1,2,0:T(8,128)}, u32[]{:S(2)}) copy-start(f32[4,128,128]{1,2,0:T(8,128)} %copy-done.8) | copy-start | bytes 786436
  183.4 37.7 %collective-permute-start.5 = (bf16[128,4096]{1,0:T(8,128)(2,1)}, bf16[128,4096]{1,0:T(8,128)(2,1)}, u32[]{:S(2)}, u32[]{:S(2)}) collective-permute-start(bf16[128,4096]{1,0:T(8,128)(2,1)} %convolution_convert_fusion), channel_id=1, source_target_pairs={{0,3},{1,0},{2,1},{3,2},{4,7},{5,4},{6,5},{7,6},{8,11},{9,8},{10,9... | collective-permute-start | bytes 3145736 | tf_op jit(solution)/shard_map/ppermute | solution.py:129
  185.7 35.4 %copy-start.4 = (bf16[512,4096]{0,1:T(8,128)(2,1)S(1)}, bf16[512,4096]{0,1:T(8,128)(2,1)}, u32[]{:S(2)}) copy-start(bf16[512,4096]{0,1:T(8,128)(2,1)} %all-gather.5.cloned.1.call-done) | copy-start | bytes 12582916
  186.5 39.2 %copy-start.1 = (s32[256]{0:T(256)S(1)}, s32[256]{0:T(256)}, u32[]{:S(2)}) copy-start(s32[256]{0:T(256)} %param.13) | copy-start | bytes 3076
Sparse Core Ops, SparseCore 0:
  26.9 79.8 all-gather.2
  108.6 53.3 all-gather.4

commit v4 on v3

--- a/solution.py
+++ b/solution.py
@@ -109,11 +109,17 @@
     new_kv = lax.dynamic_slice_in_dim(doubled, ((slot_count - me) % slot_count) * NEW, tok_rows, 0)
     score_scale = 1.0 / math.sqrt(HEAD)
 
-    total = None
-    for k in range(slot_count):
+    arrived_parts = []
+    pending = None
+    for k in list(range(1, slot_count)) + [0]:
         rows = slice(k * NEW, (k + 1) * NEW)
+        query_rows = queries[rows]
+        if pending is not None:
+            query_rows, made = lax.optimization_barrier((query_rows, pending[1]))
+            sent_to = [(s, (s + pending[0]) % n_tp) for s in range(n_tp)]
+            arrived_parts.append(lax.ppermute(made, TP_AXES, perm=sent_to))
         result = padded_attention(
-            queries[rows],
+            query_rows,
             keys_new[rows],
             values_new[rows],
             pool,
@@ -125,9 +131,10 @@
         partial = jnp.dot(context, full_out, preferred_element_type=jnp.float32).astype(
             jnp.bfloat16
         )
-        if k:
-            partial = lax.ppermute(partial, TP_AXES, perm=[(s, (s + k) % n_tp) for s in range(n_tp)])
-        total = partial.astype(jnp.float32) if total is None else total + partial.astype(jnp.float32)
+        pending = (k, partial)
+    total = pending[1].astype(jnp.float32)
+    for part in arrived_parts:
+        total = total + part.astype(jnp.float32)
     return (total.astype(jnp.bfloat16), new_kv)
 
 

time: 234 us -> 245 us (1.047)
  waiting for transfers between devices: 28.7 us -> 70.8 us
  blocking collectives: 69.3 us -> 36.1 us
  starting transfers between devices: 12 us -> 17.5 us
    all_gather x4, blocking collectives: 69.3 us -> 36.1 us  [staged_gather(): values = lax.all_gather(values, name, axis=axis, tiled=True)]
    all_gather x2, waiting for transfers between devices: 0.02 us -> 27.6 us  [staged_gather(): values = lax.all_gather(values, name, axis=axis, tiled=True)]
    ppermute x3, waiting for transfers between devices: 0.01 us -> 13.7 us  [per_device(): lax.ppermute(normed, TP_AXES, perm=[(s, (s - k) % n_tp) for s in range(n_...]
    ppermute x3, starting transfers between devices: 3.47 us -> 6.26 us  [per_device(): arrived_parts.append(lax.ppermute(made, TP_AXES, perm=sent_to))]
    ppermute x3, starting transfers between devices: 8.45 us -> 11.2 us  [per_device(): lax.ppermute(normed, TP_AXES, perm=[(s, (s - k) % n_tp) for s in range(n_...]
    reduce_sum x8, other arithmetic: 11 us -> 8.37 us  [padded_attention(): total = cached_exp.sum(-1) + recent_exponent.sum(-1)]
  transfers between devices with their start and end apart: 8 -> 8, of which waited for: 2 -> 6; matrix products, arithmetic and copies ran while one was open for 39% -> 28% of each run, Pallas kernels for 0% -> 0%
where the time goes in v4:
time: 245 us; the launch traced here: 244 us
  waiting for transfers between devices  70.8 us (29%)
  matrix products  43.5 us (18%)
  blocking collectives  36.1 us (15%)
  local copies, waits for them, and re-layouts  29.7 us (12%)
  other arithmetic  23.7 us (10%)
  between operations  22.1 us (9%)
  starting transfers between devices  17.5 us (7%)
    all_gather x4, blocking collectives, staged_gather(): values = lax.all_gather(values, name, axis=axis, tiled=True)  36.1 us
    ppermute x3, waiting for transfers between devices, per_device(): arrived_parts.append(lax.ppermute(made, TP_AXES, perm=sent_to))  29.5 us
    all_gather x2, waiting for transfers between devices, staged_gather(): values = lax.all_gather(values, name, axis=axis, tiled=True)  27.6 us
    gather x4, local copies, waits for them, and re-layouts, padded_attention(): cache = pool[page_row].reshape(-1, 2 * HEAD)  17.6 us
    dot_general x8, matrix products, value_weighted_rows(): jnp.einsum(form, weights.astype(jnp.bfloat16), values, preferred_element_...  14.5 us
    ppermute x3, waiting for transfers between devices, per_device(): lax.ppermute(normed, TP_AXES, perm=[(s, (s - k) % n_tp) for s in range(n_...  13.7 us
    dot_general x4, matrix products, per_device(): jnp.dot(context, full_out, preferred_element_type=jnp.float32)  13.3 us
    ppermute x3, starting transfers between devices, per_device(): lax.ppermute(normed, TP_AXES, perm=[(s, (s - k) % n_tp) for s in range(n_...  11.2 us
  transfers between devices with their start and end apart: 8, of which 6 were waited for; matrix products, arithmetic and copies ran while one was open for 28% of the time, Pallas kernels for 0%

profile of v4, /device:TPU:1, one launch (start us, length us, event | category | flops | bytes accessed | tf_op | source)
XLA Modules:
  0.0 243.5 jit_solution(10309985985200323111)
XLA Ops:
  7.2 11.9 %all_gather.18 = bf16[256,768]{1,0:T(8,128)(2,1)S(1)} all-gather(bf16[64,768]{1,0:T(8,128)(2,1)} %param.10), channel_id=1, replica_groups=mesh['z'=8,'ylo'=2,'x'=4,'yhi'=2,'core'=2] {'x'}, dimensions={0}, use_global_device_ids=true | all-gather | bytes 491520 | tf_op jit(solution)/shard_map/all_gather | solution.py:71
  19.2 7.6 %all_gather.19 = bf16[512,768]{1,0:T(8,128)(2,1)} all-gather(bf16[256,768]{1,0:T(8,128)(2,1)S(1)} %all_gather.18), channel_id=1, replica_groups=mesh['z'=8,'ylo'=2,'x'=4,'yhi'=2,'core'=2] {'ylo'}, dimensions={0}, use_global_device_ids=true | all-gather | bytes 1179648 | tf_op jit(solution)/shard_map/all_gather | solution.py:71
  26.8 9.6 %all_gather.21 = bf16[512,256]{0,1:T(8,128)(2,1)S(1)} all-gather(bf16[512,64]{0,1:T(8,128)(2,1)} %param.11), channel_id=1, replica_groups=mesh['z'=8,'ylo'=2,'x'=4,'yhi'=2,'core'=2] {'x'}, dimensions={1}, use_global_device_ids=true | all-gather | bytes 327680 | tf_op jit(solution)/shard_map/all_gather | solution.py:71
  36.4 7.0 %all_gather.22 = bf16[512,512]{0,1:T(8,128)(2,1)} all-gather(bf16[512,256]{0,1:T(8,128)(2,1)S(1)} %all_gather.21), channel_id=1, replica_groups=mesh['z'=8,'ylo'=2,'x'=4,'yhi'=2,'core'=2] {'ylo'}, dimensions={1}, use_global_device_ids=true | all-gather | bytes 786432 | tf_op jit(solution)/shard_map/all_gather | solution.py:71
  43.5 1.6 fusion.33
  45.8 1.5 fusion.35
  47.3 10.5 %collective-permute-start.2 = (bf16[128,4096]{1,0:T(8,128)(2,1)S(1)}, bf16[128,4096]{1,0:T(8,128)(2,1)}, u32[]{:S(2)}, u32[]{:S(2)}) collective-permute-start(bf16[128,4096]{1,0:T(8,128)(2,1)S(1)} %fusion.35), channel_id=1, source_target_pairs={{0,1},{1,2},{2,3},{3,0},{4,5},{5,6},{6,7},{7,4},{8,9},{9,10},{10,1... | collective-permute-start | bytes 3145736 | tf_op jit(solution)/shard_map/ppermute | solution.py:84
  67.5 4.7 %gather_fusion.5 = bf16[24,128,256]{2,1,0:T(8,128)(2,1)} fusion(bf16[96,128,256]{2,1,0:T(8,128)(2,1)} %param.15, s32[1024]{0:T(1024)S(1)} %get-tuple-element.58), kind=kCustom, calls=%fused_computation.5 | custom fusion | bytes 3145824 | tf_op jit(solution)/shard_map/gather | solution.py:46
  72.2 4.8 %gather_fusion.4 = bf16[24,128,256]{2,1,0:T(8,128)(2,1)} fusion(bf16[96,128,256]{2,1,0:T(8,128)(2,1)} %param.15, s32[1024]{0:T(1024)S(1)} %get-tuple-element.59), kind=kCustom, calls=%fused_computation.4 | custom fusion | bytes 3145824 | tf_op jit(solution)/shard_map/gather | solution.py:46
  77.0 4.7 %gather_fusion.3 = bf16[24,128,256]{2,1,0:T(8,128)(2,1)} fusion(bf16[96,128,256]{2,1,0:T(8,128)(2,1)} %param.15, s32[1024]{0:T(1024)S(1)} %get-tuple-element.60), kind=kCustom, calls=%fused_computation.3 | custom fusion | bytes 3145824 | tf_op jit(solution)/shard_map/gather | solution.py:46
  81.7 3.5 %gather_fusion.2 = bf16[24,128,256]{2,1,0:T(8,128)(2,1)S(1)} fusion(bf16[96,128,256]{2,1,0:T(8,128)(2,1)} %param.15, s32[1024]{0:T(1024)S(1)} %get-tuple-element.61), kind=kCustom, calls=%fused_computation.2 | custom fusion | bytes 3145824 | tf_op jit(solution)/shard_map/gather | solution.py:46
  90.9 13.0 %collective-permute-done.1 = bf16[128,4096]{1,0:T(8,128)(2,1)} collective-permute-done((bf16[128,4096]{1,0:T(8,128)(2,1)S(1)}, bf16[128,4096]{1,0:T(8,128)(2,1)}, u32[]{:S(2)}, u32[]{:S(2)}) %collective-permute-start.1) | collective-permute-done | bytes 1048608 | tf_op jit(solution)/shard_map/ppermute | solution.py:84
  104.5 2.3 all-gather.3.cloned.1.call-done
  106.8 8.1 %fusion.36 = bf16[512,768]{1,0:T(8,128)(2,1)} fusion(bf16[4096,768]{1,0:T(8,128)(2,1)} %all-gather.3.cloned.1.call-done, bf16[128,4096]{1,0:T(8,128)(2,1)} %collective-permute-done.2, bf16[128,4096]{1,0:T(8,128)(2,1)} %collective-permute-done.1, bf16[128,4096]{1,0:T(8,128)(2,1)} %collective-permute-done, bf16[128,4096]{1,0:T(8,128)(2,1)S(1)} %fusion.35), kind=kOutput, calls=%fused_computation.57 | convolution fusion | flops 3238395904 | bytes 11272192 | tf_op jit(solution)/shard_map/dot_general | solution.py:89
  114.9 1.4 copy.47
  116.4 1.0 copy.92
  117.4 1.1 convert_element_type.105
  119.2 1.9 add_convert_fusion.2
  121.2 1.7 copy.50
  122.9 1.7 copy.49
  124.6 1.5 add_convert_fusion.1
  126.2 1.0 pad_maximum_fusion
  128.1 3.1 %bitcast_reduce_fusion.3 = (f32[4,128]{1,0:T(4,128)S(1)}, f32[3072,128,4]{1,0,2:T(8,128)S(1)}) fusion(pred[3072]{0:T(1024)(128)(4,1)S(1)} %iota_compare_fusion.1, bf16[128,4,128]{2,0,1:T(8,128)(2,1)S(1)} %get-tuple-element.20, bf16[3072,256]{1,0:T(8,128)(2,1)} %bitcast.243), kind=kOutput, calls=%fused_computation.16 | convolution fusion | flops 407371264 | bytes 7214080 | tf_op jit(solution)/shard_map/ngd,kd->gnk/dot_general | solution.py:49
  131.4 2.0 fusion.5
  133.4 1.7 fusion.27
  135.1 1.6 fusion.55
  136.7 25.3 %all-gather.5.cloned.1.call-done = bf16[512,4096]{0,1:T(8,128)(2,1)} async-done(((bf16[512,512]{0,1:T(8,128)(2,1)}), bf16[512,4096]{0,1:T(8,128)(2,1)}) %all-gather.5.cloned.1.call-update) | async-done | bytes 4194320 | tf_op jit(solution)/shard_map/all_gather | solution.py:71
  162.0 4.7 %convolution_convert_fusion.3 = bf16[128,4096]{1,0:T(8,128)(2,1)} fusion(bf16[128,512]{0,1:T(8,128)(2,1)} %bitcast.252, bf16[512,4096]{0,1:T(8,128)(2,1)} %all-gather.5.cloned.1.call-done), kind=kOutput, calls=%fused_computation.26 | convolution fusion | flops 537395200 | bytes 5373952 | tf_op jit(solution)/shard_map/dot_general | solution.py:131
  167.0 1.0 bitcast_reduce_fusion.2
  168.0 1.7 fusion.25
  169.8 2.0 fusion.7
  171.8 1.0 fusion.56
  172.8 1.5 convolution_convert_fusion.2
  174.6 1.0 bitcast_reduce_fusion.1
  175.6 1.7 fusion.23
  177.3 2.2 fusion.9
  179.6 1.0 fusion.57
  180.6 2.5 %convolution_convert_fusion.1 = bf16[128,4096]{1,0:T(8,128)(2,1)} fusion(bf16[128,512]{0,1:T(8,128)(2,1)S(1)} %bitcast.254, bf16[512,4096]{0,1:T(8,128)(2,1)S(1)} %copy-done.3), kind=kOutput, calls=%fused_computation.24 | convolution fusion | flops 537395200 | bytes 5373952 | tf_op jit(solution)/shard_map/dot_general | solution.py:131
  183.9 2.7 %collective-permute-start.4 = (bf16[128,4096]{1,0:T(8,128)(2,1)S(1)}, bf16[128,4096]{1,0:T(8,128)(2,1)}, u32[]{:S(2)}, u32[]{:S(2)}) collective-permute-start(bf16[128,4096]{1,0:T(8,128)(2,1)S(1)} %convolution_convert_fusion.2), channel_id=1, source_target_pairs={{0,2},{1,3},{2,0},{3,1},{4,6},{5,7},{6,4},{7,5},{8,10},{9,11},{10,... | collective-permute-start | bytes 3145736 | tf_op jit(solution)/shard_map/ppermute | solution.py:120
  186.6 2.7 %collective-permute-start.3 = (bf16[128,4096]{1,0:T(8,128)(2,1)}, bf16[128,4096]{1,0:T(8,128)(2,1)}, u32[]{:S(2)}, u32[]{:S(2)}) collective-permute-start(bf16[128,4096]{1,0:T(8,128)(2,1)} %convolution_convert_fusion.3), channel_id=1, source_target_pairs={{0,1},{1,2},{2,3},{3,0},{4,5},{5,6},{6,7},{7,4},{8,9},{9,10},{10,1... | collective-permute-start | bytes 3145736 | tf_op jit(solution)/shard_map/ppermute | solution.py:120
  189.5 1.0 bitcast_reduce_fusion
  190.5 2.6 %copy-done.5 = f32[3072,128,4]{1,0,2:T(8,128)} copy-done((f32[3072,128,4]{1,0,2:T(8,128)}, f32[3072,128,4]{1,0,2:T(8,128)S(1)}, u32[]{:S(2)}) %copy-start.5) | copy-done | bytes 6291480
  193.2 2.0 fusion.11
  196.8 4.8 %fusion.21 = f32[4,128,128]{1,2,0:T(8,128)S(1)} fusion(f32[3072,128,4]{1,0,2:T(8,128)} %copy-done.5, f32[4,128]{1,0:T(4,128)S(1)} %max.31, pred[3072]{0:T(1024)(128)(4,1)S(1)} %iota_compare_fusion.4, bf16[3072,256]{1,0:T(8,128)(2,1)S(1)} %bitcast.238), kind=kOutput, calls=%fused_computation.43 | convolution fusion | flops 408944640 | bytes 7345152 | tf_op jit(solution)/shard_map/gnk,kd->gnd/dot_general | solution.py:38
  201.6 1.0 fusion.58
  202.6 8.2 %collective-permute-done.5 = bf16[128,4096]{1,0:T(8,128)(2,1)} collective-permute-done((bf16[128,4096]{1,0:T(8,128)(2,1)}, bf16[128,4096]{1,0:T(8,128)(2,1)}, u32[]{:S(2)}, u32[]{:S(2)}) %collective-permute-start.5) | collective-permute-done | bytes 1048608 | tf_op jit(solution)/shard_map/ppermute | solution.py:120
  210.8 21.3 %collective-permute-done.3 = bf16[128,4096]{1,0:T(8,128)(2,1)} collective-permute-done((bf16[128,4096]{1,0:T(8,128)(2,1)}, bf16[128,4096]{1,0:T(8,128)(2,1)}, u32[]{:S(2)}, u32[]{:S(2)}) %collective-permute-start.3) | collective-permute-done | bytes 1048608 | tf_op jit(solution)/shard_map/ppermute | solution.py:120
  232.1 4.6 %add_convert_fusion = bf16[128,4096]{1,0:T(8,128)(2,1)} fusion(bf16[128,4096]{1,0:T(8,128)(2,1)} %collective-permute-done.5, bf16[128,4096]{1,0:T(8,128)(2,1)} %collective-permute-done.4, bf16[128,4096]{1,0:T(8,128)(2,1)} %collective-permute-done.3, bf16[128,512]{0,1:T(8,128)(2,1)S(1)} %bitcast.251, bf16[512,4096]{0,1:T(8,128)(2,1)S(1)} %copy-done.4), kind=kOutput, calls=%fused_computation.56 | convolution fusion | flops 541589504 | bytes 8519680 | tf_op jit(solution)/shard_map/dot_general | solution.py:131
  (82 shorter events, 14.2 us)
Async XLA Ops:
  7.2 57.1 %copy-start = (s32[256]{0:T(256)S(1)}, s32[256]{0:T(256)}, u32[]{:S(2)}) copy-start(s32[256]{0:T(256)} %param.13) | copy-start | bytes 3076
  7.2 60.3 %copy-start.15 = (s32[4,24]{1,0:T(4,128)S(1)}, s32[4,24]{1,0:T(4,128)}, u32[]{:S(2)}) copy-start(s32[4,24]{1,0:T(4,128)} %param.14) | copy-start | bytes 1156
  7.2 99.7 %all-gather.3.cloned.1.call-start = ((), (), s32[]{:S(2)}) async-start(), calls=%async_computation | async-start | bytes 7077888 | tf_op jit(solution)/shard_map/all_gather | solution.py:71
  26.8 135.2 %all-gather.5.cloned.1.call-start = ((), (), s32[]{:S(2)}) async-start(), calls=%async_computation.1 | async-start | bytes 4718592 | tf_op jit(solution)/shard_map/all_gather | solution.py:71
  47.3 43.5 %collective-permute-start.2 = (bf16[128,4096]{1,0:T(8,128)(2,1)S(1)}, bf16[128,4096]{1,0:T(8,128)(2,1)}, u32[]{:S(2)}, u32[]{:S(2)}) collective-permute-start(bf16[128,4096]{1,0:T(8,128)(2,1)S(1)} %fusion.35), channel_id=1, source_target_pairs={{0,1},{1,2},{2,3},{3,0},{4,5},{5,6},{6,7},{7,4},{8,9},{9,10},{10,1... | collective-permute-start | bytes 3145736 | tf_op jit(solution)/shard_map/ppermute | solution.py:84
  57.9 46.0 %collective-permute-start.1 = (bf16[128,4096]{1,0:T(8,128)(2,1)S(1)}, bf16[128,4096]{1,0:T(8,128)(2,1)}, u32[]{:S(2)}, u32[]{:S(2)}) collective-permute-start(bf16[128,4096]{1,0:T(8,128)(2,1)S(1)} %fusion.35), channel_id=1, source_target_pairs={{0,2},{1,3},{2,0},{3,1},{4,6},{5,7},{6,4},{7,5},{8,10},{9,11},{10,... | collective-permute-start | bytes 3145736 | tf_op jit(solution)/shard_map/ppermute | solution.py:84
  58.5 46.0 %collective-permute-start = (bf16[128,4096]{1,0:T(8,128)(2,1)S(1)}, bf16[128,4096]{1,0:T(8,128)(2,1)}, u32[]{:S(2)}, u32[]{:S(2)}) collective-permute-start(bf16[128,4096]{1,0:T(8,128)(2,1)S(1)} %fusion.35), channel_id=1, source_target_pairs={{0,3},{1,0},{2,1},{3,2},{4,7},{5,4},{6,5},{7,6},{8,11},{9,8},{10,9... | collective-permute-start | bytes 3145736 | tf_op jit(solution)/shard_map/ppermute | solution.py:84
  67.5 17.7 %copy-start.2 = (s32[256]{0:T(256)S(1)}, s32[256]{0:T(256)}, u32[]{:S(2)}) copy-start(s32[256]{0:T(256)} %param.12) | copy-start | bytes 3076
  116.3 15.0 %copy-start.9 = (bf16[512,768]{0,1:T(8,128)(2,1)}, bf16[512,768]{0,1:T(8,128)(2,1)S(1)}, u32[]{:S(2)}) copy-start(bf16[512,768]{0,1:T(8,128)(2,1)S(1)} %copy.47) | copy-start | bytes 2359300
  128.1 5.3 %copy-start.8 = (bf16[24,128,256]{2,1,0:T(8,128)(2,1)S(1)}, bf16[24,128,256]{2,1,0:T(8,128)(2,1)}, u32[]{:S(2)}) copy-start(bf16[24,128,256]{2,1,0:T(8,128)(2,1)} %gather_fusion.5) | copy-start | bytes 4718596
  133.4 33.4 %copy-start.12 = (bf16[128,4,128]{2,0,1:T(8,128)(2,1)S(1)}, bf16[128,4,128]{2,0,1:T(8,128)(2,1)}, u32[]{:S(2)}) copy-start(bf16[128,4,128]{2,0,1:T(8,128)(2,1)} %get-tuple-element.8) | copy-start | bytes 393220
  133.4 33.4 %copy-start.14 = (pred[128,128]{0,1:T(8,128)(4,1)S(1)}, pred[128,128]{0,1:T(8,128)(4,1)}, u32[]{:S(2)}) copy-start(pred[128,128]{0,1:T(8,128)(4,1)} %iota_compare_fusion) | copy-start | bytes 49156
  133.4 33.6 %copy-start.7 = (bf16[24,128,256]{2,1,0:T(8,128)(2,1)S(1)}, bf16[24,128,256]{2,1,0:T(8,128)(2,1)}, u32[]{:S(2)}) copy-start(bf16[24,128,256]{2,1,0:T(8,128)(2,1)} %gather_fusion.4) | copy-start | bytes 4718596
  169.7 3.1 %copy-start.3 = (bf16[512,4096]{0,1:T(8,128)(2,1)S(1)}, bf16[512,4096]{0,1:T(8,128)(2,1)}, u32[]{:S(2)}) copy-start(bf16[512,4096]{0,1:T(8,128)(2,1)} %all-gather.5.cloned.1.call-done) | copy-start | bytes 12582916
  169.7 4.6 %copy-start.11 = (bf16[128,4,128]{2,0,1:T(8,128)(2,1)S(1)}, bf16[128,4,128]{2,0,1:T(8,128)(2,1)}, u32[]{:S(2)}) copy-start(bf16[128,4,128]{2,0,1:T(8,128)(2,1)} %get-tuple-element.9) | copy-start | bytes 393220
  169.8 4.8 %copy-start.6 = (bf16[24,128,256]{2,1,0:T(8,128)(2,1)S(1)}, bf16[24,128,256]{2,1,0:T(8,128)(2,1)}, u32[]{:S(2)}) copy-start(bf16[24,128,256]{2,1,0:T(8,128)(2,1)} %gather_fusion.3) | copy-start | bytes 4718596
  177.3 12.0 %copy-start.10 = (bf16[128,4,128]{2,0,1:T(8,128)(2,1)S(1)}, bf16[128,4,128]{2,0,1:T(8,128)(2,1)}, u32[]{:S(2)}) copy-start(bf16[128,4,128]{2,0,1:T(8,128)(2,1)} %get-tuple-element.10) | copy-start | bytes 393220
  183.0 27.8 %collective-permute-start.5 = (bf16[128,4096]{1,0:T(8,128)(2,1)}, bf16[128,4096]{1,0:T(8,128)(2,1)}, u32[]{:S(2)}, u32[]{:S(2)}) collective-permute-start(bf16[128,4096]{1,0:T(8,128)(2,1)} %convolution_convert_fusion.1), channel_id=1, source_target_pairs={{0,3},{1,0},{2,1},{3,2},{4,7},{5,4},{6,5},{7,6},{8,11},{9,8},{10,9... | collective-permute-start | bytes 3145736 | tf_op jit(solution)/shard_map/ppermute | solution.py:120
  183.9 26.9 %collective-permute-start.4 = (bf16[128,4096]{1,0:T(8,128)(2,1)S(1)}, bf16[128,4096]{1,0:T(8,128)(2,1)}, u32[]{:S(2)}, u32[]{:S(2)}) collective-permute-start(bf16[128,4096]{1,0:T(8,128)(2,1)S(1)} %convolution_convert_fusion.2), channel_id=1, source_target_pairs={{0,2},{1,3},{2,0},{3,1},{4,6},{5,7},{6,4},{7,5},{8,10},{9,11},{10,... | collective-permute-start | bytes 3145736 | tf_op jit(solution)/shard_map/ppermute | solution.py:120
  186.6 45.6 %collective-permute-start.3 = (bf16[128,4096]{1,0:T(8,128)(2,1)}, bf16[128,4096]{1,0:T(8,128)(2,1)}, u32[]{:S(2)}, u32[]{:S(2)}) collective-permute-start(bf16[128,4096]{1,0:T(8,128)(2,1)} %convolution_convert_fusion.3), channel_id=1, source_target_pairs={{0,1},{1,2},{2,3},{3,0},{4,5},{5,6},{6,7},{7,4},{8,9},{9,10},{10,1... | collective-permute-start | bytes 3145736 | tf_op jit(solution)/shard_map/ppermute | solution.py:120
  189.5 5.7 %copy-start.13 = (bf16[512,128]{0,1:T(8,128)(2,1)S(1)}, bf16[512,128]{0,1:T(8,128)(2,1)}, u32[]{:S(2)}) copy-start(bf16[512,128]{0,1:T(8,128)(2,1)} %get-tuple-element.24) | copy-start | bytes 393220
  190.5 2.7 %copy-start.5 = (f32[3072,128,4]{1,0,2:T(8,128)}, f32[3072,128,4]{1,0,2:T(8,128)S(1)}, u32[]{:S(2)}) copy-start(f32[3072,128,4]{1,0,2:T(8,128)S(1)} %get-tuple-element.55) | copy-start | bytes 18874372
  196.8 35.4 %copy-start.4 = (bf16[512,4096]{0,1:T(8,128)(2,1)S(1)}, bf16[512,4096]{0,1:T(8,128)(2,1)}, u32[]{:S(2)}) copy-start(bf16[512,4096]{0,1:T(8,128)(2,1)} %all-gather.5.cloned.1.call-done) | copy-start | bytes 12582916
  196.8 39.9 %copy-start.1 = (s32[256]{0:T(256)S(1)}, s32[256]{0:T(256)}, u32[]{:S(2)}) copy-start(s32[256]{0:T(256)} %param.13) | copy-start | bytes 3076
Sparse Core Ops, SparseCore 0:
  26.9 79.8 all-gather.2
  108.6 53.3 all-gather.4

commit v5 on v3

--- a/solution.py
+++ b/solution.py
@@ -72,6 +72,31 @@
     return values
 
 
+def blocks_to_z_first(values, axis, sizes):
+    shape = values.shape
+    split = shape[:axis] + tuple(sizes) + (-1,) + shape[axis + 1:]
+    order = tuple(range(axis)) + (axis + 2, axis + 1, axis) + tuple(range(axis + 3, len(split)))
+    return values.reshape(split).transpose(order).reshape(shape)
+
+
+def project_over_x(tokens, w_part):
+    sizes = tuple(lax.axis_size(name) for name in REQ_AXES)
+    n_x = sizes[-1]
+    mine = lax.axis_index("x")
+    held = lax.all_gather(lax.all_gather(w_part, "z", axis=0, tiled=True), "ylo", axis=0, tiled=True)
+    ordered = blocks_to_z_first(tokens, 1, sizes)
+    width = held.shape[0]
+    total = None
+    for k in range(n_x):
+        block = held
+        if k:
+            block = lax.ppermute(held, "x", perm=[(s, (s - k) % n_x) for s in range(n_x)])
+        features = lax.dynamic_slice_in_dim(ordered, ((mine + k) % n_x) * width, width, 1)
+        term = jnp.dot(features, block, preferred_element_type=jnp.float32)
+        total = term if total is None else total + term
+    return total
+
+
 def per_device(hidden, norm_gain, w_qkv, w_out, lengths, deal, pages, pool):
     states = hidden.astype(jnp.float32)
     mean_square = jnp.mean(states * states, axis=1, keepdims=True)
@@ -86,10 +111,17 @@
     ]
     gathered = jnp.concatenate(arrived, 0)
     tok_rows = gathered.shape[0]
-    projected = jnp.dot(
-        gathered,
-        staged_gather(w_qkv, REQ_AXES, 0),
-        preferred_element_type=jnp.float32,
+    cut = w_qkv.shape[1] // 2
+    projected = jnp.concatenate(
+        [
+            jnp.dot(
+                gathered,
+                staged_gather(w_qkv[:, :cut], REQ_AXES, 0),
+                preferred_element_type=jnp.float32,
+            ),
+            project_over_x(gathered, w_qkv[:, cut:]),
+        ],
+        1,
     ).astype(jnp.bfloat16)
     full_out = staged_gather(w_out, REQ_AXES, 1)
     group = QH // KVH

time: 234 us -> 269 us (1.15)
  blocking collectives: 69.3 us -> 100 us
  waiting for transfers between devices: 28.7 us -> 50.6 us
  matrix products: 44.9 us -> 31.4 us
  other arithmetic: 25.9 us -> 16.5 us
  starting transfers between devices: 12 us -> 20 us
  local copies, waits for them, and re-layouts: 29.4 us -> 26.6 us
    all_gather x0 -> x2, blocking collectives: none -> 51.2 us  [the longest x1 26.1 us: project_over_x(): lax.all_gather(lax.all_gather(w_part, 'z', axis=0, tiled=True), 'ylo', ax...]
    all_gather x4, blocking collectives: 69.3 us -> 49.3 us  [staged_gather(): values = lax.all_gather(values, name, axis=axis, tiled=True)]
    ppermute x3, waiting for transfers between devices: 28.7 us -> 40.3 us  [per_device(): lax.ppermute(partial, TP_AXES, perm=[(s, (s + k) % n_tp) for s in range(n...]
    ppermute x0 -> x3, waiting for transfers between devices: none -> 10.2 us  [project_over_x(): lax.ppermute(held, 'x', perm=[(s, (s - k) % n_x) for s in range(n_x)])]
    dot_general x8, matrix products: 16.4 us -> 7.7 us  [value_weighted_rows(): jnp.einsum(form, weights.astype(jnp.bfloat16), values, preferred_element_...]
    ppermute x0 -> x3, starting transfers between devices: none -> 4.18 us  [project_over_x(): lax.ppermute(held, 'x', perm=[(s, (s - k) % n_x) for s in range(n_x)])]
    dot_general x4, matrix products: 13.4 us -> 9.57 us  [per_device(): jnp.dot(context, full_out, preferred_element_type=jnp.float32)]
    ppermute x3, starting transfers between devices: 3.47 us -> 6.33 us  [per_device(): lax.ppermute(partial, TP_AXES, perm=[(s, (s + k) % n_tp) for s in range(n...]
  transfers between devices with their start and end apart: 8 -> 11, of which waited for: 2 -> 4; matrix products, arithmetic and copies ran while one was open for 39% -> 25% of each run, Pallas kernels for 0% -> 0%
where the time goes in v5:
time: 269 us; the launch traced here: 268 us
  blocking collectives  100 us (37%)
  waiting for transfers between devices  50.6 us (19%)
  matrix products  31.4 us (12%)
  local copies, waits for them, and re-layouts  26.6 us (10%)
  between operations  22.4 us (8%)
  starting transfers between devices  20 us (7%)
  other arithmetic  16.5 us (6%)
    all_gather x4, blocking collectives, staged_gather(): values = lax.all_gather(values, name, axis=axis, tiled=True)  49.3 us
    ppermute x3, waiting for transfers between devices, per_device(): lax.ppermute(partial, TP_AXES, perm=[(s, (s + k) % n_tp) for s in range(n...  40.3 us
    all_gather x1, blocking collectives, project_over_x(): lax.all_gather(lax.all_gather(w_part, 'z', axis=0, tiled=True), 'ylo', ax...  26.1 us
    all_gather x1, blocking collectives, project_over_x(): lax.all_gather(w_part, 'z', axis=0, tiled=True)  25.1 us
    gather x4, local copies, waits for them, and re-layouts, padded_attention(): cache = pool[page_row].reshape(-1, 2 * HEAD)  18.8 us
    ppermute x3, waiting for transfers between devices, project_over_x(): lax.ppermute(held, 'x', perm=[(s, (s - k) % n_x) for s in range(n_x)])  10.2 us
    dot_general x4, matrix products, per_device(): jnp.dot(context, full_out, preferred_element_type=jnp.float32)  9.57 us
    ppermute x3, starting transfers between devices, per_device(): lax.ppermute(normed, TP_AXES, perm=[(s, (s - k) % n_tp) for s in range(n_...  9.37 us
  transfers between devices with their start and end apart: 11, of which 4 were waited for; matrix products, arithmetic and copies ran while one was open for 25% of the time, Pallas kernels for 0%

profile of v5, /device:TPU:1, one launch (start us, length us, event | category | flops | bytes accessed | tf_op | source)
XLA Modules:
  0.0 267.9 jit_solution(8615293015832120575)
XLA Ops:
  7.2 0.8 fusion.133
  8.1 10.5 %all_gather.24 = bf16[256,384]{1,0:T(8,128)(2,1)S(1)} all-gather(bf16[64,384]{1,0:T(8,128)(2,1)S(1)} %get-tuple-element.14), channel_id=1, replica_groups=mesh['z'=8,'ylo'=2,'x'=4,'yhi'=2,'core'=2] {'x'}, dimensions={0}, use_global_device_ids=true | all-gather | bytes 245760 | tf_op jit(solution)/shard_map/all_gather | solution.py:71
  18.6 5.3 %all_gather.25 = bf16[512,384]{1,0:T(8,128)(2,1)} all-gather(bf16[256,384]{1,0:T(8,128)(2,1)S(1)} %all_gather.24), channel_id=1, replica_groups=mesh['z'=8,'ylo'=2,'x'=4,'yhi'=2,'core'=2] {'ylo'}, dimensions={0}, use_global_device_ids=true | all-gather | bytes 589824 | tf_op jit(solution)/shard_map/all_gather | solution.py:71
  23.9 1.6 copy.48
  25.5 0.7 convert_element_type.101
  26.8 0.7 fusion.27
  27.5 6.1 %collective-permute-start = (bf16[128,4096]{0,1:T(8,128)(2,1)S(1)}, bf16[128,4096]{0,1:T(8,128)(2,1)S(1)}, u32[]{:S(2)}, u32[]{:S(2)}) collective-permute-start(bf16[128,4096]{0,1:T(8,128)(2,1)S(1)} %fusion.27), channel_id=1, source_target_pairs={{0,3},{1,0},{2,1},{3,2},{4,7},{5,4},{6,5},{7,6},{8,11},{9,8},{10,9... | collective-permute-start | bytes 3145736 | tf_op jit(solution)/shard_map/ppermute | solution.py:109
  33.6 1.5 collective-permute-start.1
  35.2 1.7 collective-permute-start.2
  36.9 25.1 %all_gather.27 = bf16[512,384]{1,0:T(8,128)(2,1)S(1)} all-gather(bf16[64,384]{1,0:T(8,128)(2,1)S(1)} %get-tuple-element.15), channel_id=1, replica_groups=mesh['z'=8,'ylo'=2,'x'=4,'yhi'=2,'core'=2] {'z'}, dimensions={0}, use_global_device_ids=true | all-gather | bytes 442368 | tf_op jit(solution)/shard_map/all_gather | solution.py:86
  61.9 26.1 %all_gather.28 = bf16[1024,384]{1,0:T(8,128)(2,1)S(1)} all-gather(bf16[512,384]{1,0:T(8,128)(2,1)S(1)} %all_gather.27), channel_id=1, replica_groups=mesh['z'=8,'ylo'=2,'x'=4,'yhi'=2,'core'=2] {'ylo'}, dimensions={0}, use_global_device_ids=true | all-gather | bytes 1179648 | tf_op jit(solution)/shard_map/all_gather | solution.py:86
  88.0 2.1 collective-permute-start.3
  90.2 26.3 %all_gather.29 = bf16[512,256]{0,1:T(8,128)(2,1)S(1)} all-gather(bf16[512,64]{0,1:T(8,128)(2,1)S(1)} %copy-done.10), channel_id=1, replica_groups=mesh['z'=8,'ylo'=2,'x'=4,'yhi'=2,'core'=2] {'x'}, dimensions={1}, use_global_device_ids=true | all-gather | bytes 327680 | tf_op jit(solution)/shard_map/all_gather | solution.py:71
  116.4 7.3 %all_gather.30 = bf16[512,512]{0,1:T(8,128)(2,1)} all-gather(bf16[512,256]{0,1:T(8,128)(2,1)S(1)} %all_gather.29), channel_id=1, replica_groups=mesh['z'=8,'ylo'=2,'x'=4,'yhi'=2,'core'=2] {'ylo'}, dimensions={1}, use_global_device_ids=true | all-gather | bytes 786432 | tf_op jit(solution)/shard_map/all_gather | solution.py:71
  132.9 4.6 %gather_fusion.2 = bf16[24,128,256]{2,1,0:T(8,128)(2,1)} fusion(bf16[96,128,256]{2,1,0:T(8,128)(2,1)} %param.15, s32[1024]{0:T(1024)S(1)} %get-tuple-element.49), kind=kCustom, calls=%fused_computation.2 | custom fusion | bytes 3145824 | tf_op jit(solution)/shard_map/gather | solution.py:46
  137.5 4.8 %gather_fusion.3 = bf16[24,128,256]{2,1,0:T(8,128)(2,1)} fusion(bf16[96,128,256]{2,1,0:T(8,128)(2,1)} %param.15, s32[1024]{0:T(1024)S(1)} %get-tuple-element.48), kind=kCustom, calls=%fused_computation.3 | custom fusion | bytes 3145824 | tf_op jit(solution)/shard_map/gather | solution.py:46
  142.3 4.7 %gather_fusion.4 = bf16[24,128,256]{2,1,0:T(8,128)(2,1)} fusion(bf16[96,128,256]{2,1,0:T(8,128)(2,1)} %param.15, s32[1024]{0:T(1024)S(1)} %get-tuple-element.47), kind=kCustom, calls=%fused_computation.4 | custom fusion | bytes 3145824 | tf_op jit(solution)/shard_map/gather | solution.py:46
  147.0 4.8 %gather_fusion.5 = bf16[24,128,256]{2,1,0:T(8,128)(2,1)} fusion(bf16[96,128,256]{2,1,0:T(8,128)(2,1)} %param.15, s32[1024]{0:T(1024)S(1)} %get-tuple-element.46), kind=kCustom, calls=%fused_computation.5 | custom fusion | bytes 3145824 | tf_op jit(solution)/shard_map/gather | solution.py:46
  155.7 2.1 collective-permute-start.4
  157.8 1.8 pad_maximum_fusion
  160.7 1.8 fusion.50
  162.5 1.8 convolution_add_fusion.1
  164.2 10.2 %collective-permute-done.4 = bf16[1024,384]{1,0:T(8,128)(2,1)S(1)} collective-permute-done((bf16[1024,384]{1,0:T(8,128)(2,1)S(1)}, bf16[1024,384]{1,0:T(8,128)(2,1)S(1)}, u32[]{:S(2)}, u32[]{:S(2)}) %collective-permute-start.4) | collective-permute-done | bytes 786464 | tf_op jit(solution)/shard_map/ppermute | solution.py:93
  175.7 0.7 fusion.63
  176.4 0.8 copy.74
  177.2 4.5 %convolution_convert_fusion.4 = bf16[512,384]{0,1:T(8,128)(2,1)S(1)} fusion(bf16[4096,384]{1,0:T(8,128)(2,1)} %all-gather.3.cloned.1.call-done, bf16[128,4096]{0,1:T(8,128)(2,1)} %collective-permute-done.2, bf16[128,4096]{0,1:T(8,128)(2,1)} %collective-permute-done.1, bf16[128,4096]{0,1:T(8,128)(2,1)S(1)} %collective-permute-done, ...), kind=kOutput, calls=%fused_computation.54 | convolution fusion | flops 1627586560 | bytes 7733248 | tf_op jit(solution)/shard_map/dot_general | solution.py:117
  182.3 1.0 bitcast_reduce_fusion.3
  183.5 1.0 bitcast_reduce_fusion.2
  184.8 1.1 copy-done.8
  185.9 1.0 bitcast_reduce_fusion.1
  187.4 1.0 bitcast_reduce_fusion
  188.6 2.0 fusion.7
  190.6 2.2 fusion.9
  192.8 2.0 fusion.11
  194.8 1.7 fusion.17
  196.8 1.7 fusion.15
  198.7 1.7 fusion.13
  200.7 2.0 fusion.5
  202.7 3.9 %convolution_convert_fusion.2 = bf16[128,4096]{1,0:T(8,128)(2,1)S(1)} fusion(bf16[128,512]{0,1:T(8,128)(2,1)S(1)} %bitcast.255, bf16[512,4096]{0,1:T(8,128)(2,1)} %all-gather.5.cloned.1.call-done), kind=kOutput, calls=%fused_computation.24 | convolution fusion | flops 537395200 | bytes 5373952 | tf_op jit(solution)/shard_map/dot_general | solution.py:157
  206.6 3.5 %collective-permute-start.6 = (bf16[128,4096]{1,0:T(8,128)(2,1)S(1)}, bf16[128,4096]{1,0:T(8,128)(2,1)S(1)}, u32[]{:S(2)}, u32[]{:S(2)}) collective-permute-start(bf16[128,4096]{1,0:T(8,128)(2,1)S(1)} %convolution_convert_fusion.2), channel_id=1, source_target_pairs={{0,1},{1,2},{2,3},{3,0},{4,5},{5,6},{6,7},{7,4},{8,9},{9,10},{10,1... | collective-permute-start | bytes 3145736 | tf_op jit(solution)/shard_map/ppermute | solution.py:161
  210.1 1.5 convolution_convert_fusion.1
  211.6 2.8 %collective-permute-start.7 = (bf16[128,4096]{1,0:T(8,128)(2,1)S(1)}, bf16[128,4096]{1,0:T(8,128)(2,1)S(1)}, u32[]{:S(2)}, u32[]{:S(2)}) collective-permute-start(bf16[128,4096]{1,0:T(8,128)(2,1)S(1)} %convolution_convert_fusion.1), channel_id=1, source_target_pairs={{0,2},{1,3},{2,0},{3,1},{4,6},{5,7},{6,4},{7,5},{8,10},{9,11},{10,... | collective-permute-start | bytes 3145736 | tf_op jit(solution)/shard_map/ppermute | solution.py:161
  214.4 1.5 convolution_convert_fusion
  216.2 1.7 fusion.19
  218.1 12.5 %collective-permute-done.6 = bf16[128,4096]{1,0:T(8,128)(2,1)S(1)} collective-permute-done((bf16[128,4096]{1,0:T(8,128)(2,1)S(1)}, bf16[128,4096]{1,0:T(8,128)(2,1)S(1)}, u32[]{:S(2)}, u32[]{:S(2)}) %collective-permute-start.6) | collective-permute-done | bytes 1048608 | tf_op jit(solution)/shard_map/ppermute | solution.py:161
  230.6 25.3 %collective-permute-done.7 = bf16[128,4096]{1,0:T(8,128)(2,1)S(1)} collective-permute-done((bf16[128,4096]{1,0:T(8,128)(2,1)S(1)}, bf16[128,4096]{1,0:T(8,128)(2,1)S(1)}, u32[]{:S(2)}, u32[]{:S(2)}) %collective-permute-start.7) | collective-permute-done | bytes 1048608 | tf_op jit(solution)/shard_map/ppermute | solution.py:161
  255.9 2.5 collective-permute-done.8
  258.4 2.6 add_convert_fusion
  (90 shorter events, 11.0 us)
Async XLA Ops:
  7.2 122.4 %copy-start = (s32[256]{0:T(256)S(1)}, s32[256]{0:T(256)}, u32[]{:S(2)}) copy-start(s32[256]{0:T(256)} %param.13) | copy-start | bytes 3076
  7.2 83.0 %copy-start.10 = (bf16[512,64]{0,1:T(8,128)(2,1)S(1)}, bf16[512,64]{0,1:T(8,128)(2,1)}, u32[]{:S(2)}) copy-start(bf16[512,64]{0,1:T(8,128)(2,1)} %param.11) | copy-start | bytes 196612
  7.2 125.6 %copy-start.11 = (s32[4,24]{1,0:T(4,128)S(1)}, s32[4,24]{1,0:T(4,128)}, u32[]{:S(2)}) copy-start(s32[4,24]{1,0:T(4,128)} %param.14) | copy-start | bytes 1156
  7.2 170.0 %all-gather.3.cloned.1.call-start = ((), (), s32[]{:S(2)}) async-start(), calls=%async_computation | async-start | bytes 3538944 | tf_op jit(solution)/shard_map/all_gather | solution.py:71
  23.9 178.8 %all-gather.5.cloned.1.call-start = ((), (), s32[]{:S(2)}) async-start(), calls=%async_computation.1 | async-start | bytes 4718592 | tf_op jit(solution)/shard_map/all_gather | solution.py:71
  27.5 128.2 %collective-permute-start = (bf16[128,4096]{0,1:T(8,128)(2,1)S(1)}, bf16[128,4096]{0,1:T(8,128)(2,1)S(1)}, u32[]{:S(2)}, u32[]{:S(2)}) collective-permute-start(bf16[128,4096]{0,1:T(8,128)(2,1)S(1)} %fusion.27), channel_id=1, source_target_pairs={{0,3},{1,0},{2,1},{3,2},{4,7},{5,4},{6,5},{7,6},{8,11},{9,8},{10,9... | collective-permute-start | bytes 3145736 | tf_op jit(solution)/shard_map/ppermute | solution.py:109
  33.6 124.1 %collective-permute-start.1 = (bf16[128,4096]{0,1:T(8,128)(2,1)S(1)}, bf16[128,4096]{0,1:T(8,128)(2,1)}, u32[]{:S(2)}, u32[]{:S(2)}) collective-permute-start(bf16[128,4096]{0,1:T(8,128)(2,1)S(1)} %fusion.27), channel_id=1, source_target_pairs={{0,2},{1,3},{2,0},{3,1},{4,6},{5,7},{6,4},{7,5},{8,10},{9,11},{10,... | collective-permute-start | bytes 3145736 | tf_op jit(solution)/shard_map/ppermute | solution.py:109
  35.2 122.6 %collective-permute-start.2 = (bf16[128,4096]{0,1:T(8,128)(2,1)S(1)}, bf16[128,4096]{0,1:T(8,128)(2,1)}, u32[]{:S(2)}, u32[]{:S(2)}) collective-permute-start(bf16[128,4096]{0,1:T(8,128)(2,1)S(1)} %fusion.27), channel_id=1, source_target_pairs={{0,1},{1,2},{2,3},{3,0},{4,5},{5,6},{6,7},{7,4},{8,9},{9,10},{10,1... | collective-permute-start | bytes 3145736 | tf_op jit(solution)/shard_map/ppermute | solution.py:109
  88.0 74.4 %collective-permute-start.3 = (bf16[1024,384]{1,0:T(8,128)(2,1)S(1)}, bf16[1024,384]{1,0:T(8,128)(2,1)}, u32[]{:S(2)}, u32[]{:S(2)}) collective-permute-start(bf16[1024,384]{1,0:T(8,128)(2,1)S(1)} %all_gather.28), channel_id=1, source_target_pairs={{0,12},{4,0},{8,4},{12,8},{1,13},{5,1},{9,5},{13,9},{2,14},{6,2},{... | collective-permute-start | bytes 2359304 | tf_op jit(solution)/shard_map/ppermute | solution.py:93
  90.2 70.5 %collective-permute-start.5 = (bf16[1024,384]{1,0:T(8,128)(2,1)S(1)}, bf16[1024,384]{1,0:T(8,128)(2,1)}, u32[]{:S(2)}, u32[]{:S(2)}) collective-permute-start(bf16[1024,384]{1,0:T(8,128)(2,1)S(1)} %all_gather.28), channel_id=1, source_target_pairs={{0,4},{4,8},{8,12},{12,0},{1,5},{5,9},{9,13},{13,1},{2,6},{6,10},{... | collective-permute-start | bytes 2359304 | tf_op jit(solution)/shard_map/ppermute | solution.py:93
  132.9 18.8 %copy-start.2 = (s32[256]{0:T(256)S(1)}, s32[256]{0:T(256)}, u32[]{:S(2)}) copy-start(s32[256]{0:T(256)} %param.12) | copy-start | bytes 3076
  155.7 18.7 %collective-permute-start.4 = (bf16[1024,384]{1,0:T(8,128)(2,1)S(1)}, bf16[1024,384]{1,0:T(8,128)(2,1)S(1)}, u32[]{:S(2)}, u32[]{:S(2)}) collective-permute-start(bf16[1024,384]{1,0:T(8,128)(2,1)S(1)} %all_gather.28), channel_id=1, source_target_pairs={{0,8},{4,12},{8,0},{12,4},{1,9},{5,13},{9,1},{13,5},{2,10},{6,14},... | collective-permute-start | bytes 2359304 | tf_op jit(solution)/shard_map/ppermute | solution.py:93
  177.2 5.0 %copy-start.5 = (bf16[24,128,256]{2,1,0:T(8,128)(2,1)S(1)}, bf16[24,128,256]{2,1,0:T(8,128)(2,1)}, u32[]{:S(2)}) copy-start(bf16[24,128,256]{2,1,0:T(8,128)(2,1)} %gather_fusion.2) | copy-start | bytes 4718596
  182.0 1.5 copy-start.9
  183.3 17.4 %copy-start.4 = (f32[3072,128,4]{1,0,2:T(8,128)}, f32[3072,128,4]{1,0,2:T(8,128)S(1)}, u32[]{:S(2)}) copy-start(f32[3072,128,4]{1,0,2:T(8,128)S(1)} %get-tuple-element.39) | copy-start | bytes 18874372
  183.3 2.6 copy-start.8
  184.5 2.9 %copy-start.7 = (bf16[24,128,256]{2,1,0:T(8,128)(2,1)S(1)}, bf16[24,128,256]{2,1,0:T(8,128)(2,1)}, u32[]{:S(2)}) copy-start(bf16[24,128,256]{2,1,0:T(8,128)(2,1)} %gather_fusion.5) | copy-start | bytes 4718596
  202.7 7.4 %copy-start.3 = (bf16[512,4096]{0,1:T(8,128)(2,1)S(1)}, bf16[512,4096]{0,1:T(8,128)(2,1)}, u32[]{:S(2)}) copy-start(bf16[512,4096]{0,1:T(8,128)(2,1)} %all-gather.5.cloned.1.call-done) | copy-start | bytes 12582916
  202.7 13.4 %slice-start = ((s8[6291456]{0:T(1024)(128)(4,1)}), s8[4194304]{0:T(1024)(128)(4,1)S(1)}, s32[]{:S(2)}) async-start(s8[6291456]{0:T(1024)(128)(4,1)} %bitcast.232), calls=%async_computation.2 | async-start | bytes 8388608
  206.6 9.5 %copy-start.6 = (bf16[24,128,256]{2,1,0:T(8,128)(2,1)S(1)}, bf16[24,128,256]{2,1,0:T(8,128)(2,1)}, u32[]{:S(2)}) copy-start(bf16[24,128,256]{2,1,0:T(8,128)(2,1)} %gather_fusion.2) | copy-start | bytes 4718596
  206.6 24.0 %collective-permute-start.6 = (bf16[128,4096]{1,0:T(8,128)(2,1)S(1)}, bf16[128,4096]{1,0:T(8,128)(2,1)S(1)}, u32[]{:S(2)}, u32[]{:S(2)}) collective-permute-start(bf16[128,4096]{1,0:T(8,128)(2,1)S(1)} %convolution_convert_fusion.2), channel_id=1, source_target_pairs={{0,1},{1,2},{2,3},{3,0},{4,5},{5,6},{6,7},{7,4},{8,9},{9,10},{10,1... | collective-permute-start | bytes 3145736 | tf_op jit(solution)/shard_map/ppermute | solution.py:161
  210.1 6.0 %slice-start.1 = ((s8[6291456]{0:T(1024)(128)(4,1)}), s8[2097152]{0:T(1024)(128)(4,1)S(1)}, s32[]{:S(2)}) async-start(s8[6291456]{0:T(1024)(128)(4,1)} %bitcast.232), calls=%async_computation.3 | async-start | bytes 4194304
  211.6 44.3 %collective-permute-start.7 = (bf16[128,4096]{1,0:T(8,128)(2,1)S(1)}, bf16[128,4096]{1,0:T(8,128)(2,1)S(1)}, u32[]{:S(2)}, u32[]{:S(2)}) collective-permute-start(bf16[128,4096]{1,0:T(8,128)(2,1)S(1)} %convolution_convert_fusion.1), channel_id=1, source_target_pairs={{0,2},{1,3},{2,0},{3,1},{4,6},{5,7},{6,4},{7,5},{8,10},{9,11},{10,... | collective-permute-start | bytes 3145736 | tf_op jit(solution)/shard_map/ppermute | solution.py:161
  215.9 42.5 %collective-permute-start.8 = (bf16[128,4096]{1,0:T(8,128)(2,1)S(1)}, bf16[128,4096]{1,0:T(8,128)(2,1)S(1)}, u32[]{:S(2)}, u32[]{:S(2)}) collective-permute-start(bf16[128,4096]{1,0:T(8,128)(2,1)S(1)} %convolution_convert_fusion), channel_id=1, source_target_pairs={{0,3},{1,0},{2,1},{3,2},{4,7},{5,4},{6,5},{7,6},{8,11},{9,8},{10,9... | collective-permute-start | bytes 3145736 | tf_op jit(solution)/shard_map/ppermute | solution.py:161
  216.1 44.9 %copy-start.1 = (s32[256]{0:T(256)S(1)}, s32[256]{0:T(256)}, u32[]{:S(2)}) copy-start(s32[256]{0:T(256)} %param.13) | copy-start | bytes 3076
Sparse Core Ops, SparseCore 0:
  24.0 54.1 all-gather.2
  123.9 57.2 all-gather.4

commit v6 on v3

--- a/solution.py
+++ b/solution.py
@@ -67,9 +67,8 @@
 
 
 def staged_gather(values, axes, axis):
-    for name in reversed(axes):
-        values = lax.all_gather(values, name, axis=axis, tiled=True)
-    return values
+    values = lax.all_gather(values, axes[1:], axis=axis, tiled=True)
+    return lax.all_gather(values, axes[0], axis=axis, tiled=True)
 
 
 def per_device(hidden, norm_gain, w_qkv, w_out, lengths, deal, pages, pool):

time: 234 us -> 239 us (1.021)
  waiting for transfers between devices: 28.7 us -> 46.4 us
  blocking collectives: 69.3 us -> 53.5 us
  starting transfers between devices: 12 us -> 14.9 us
    all_gather x2, waiting for transfers between devices: 0.02 us -> 17.1 us  [staged_gather(): return lax.all_gather(values, axes[0], axis=axis, tiled=True)]
    all_gather x4 -> x2, blocking collectives: 69.3 us -> 53.5 us  [staged_gather(): values = lax.all_gather(values, axes[1:], axis=axis, tiled=True)]
    ppermute x3, starting transfers between devices: 8.45 us -> 10.9 us  [per_device(): lax.ppermute(normed, TP_AXES, perm=[(s, (s - k) % n_tp) for s in range(n_...]
  transfers between devices with their start and end apart: 8 -> 8, of which waited for: 2 -> 5; matrix products, arithmetic and copies ran while one was open for 39% -> 38% of each run, Pallas kernels for 0% -> 0%
where the time goes in v6:
time: 239 us; the launch traced here: 237 us
  blocking collectives  53.5 us (22%)
  waiting for transfers between devices  46.4 us (19%)
  matrix products  44.9 us (19%)
  local copies, waits for them, and re-layouts  29.6 us (12%)
  other arithmetic  25.9 us (11%)
  between operations  22.2 us (9%)
  starting transfers between devices  14.9 us (6%)
    all_gather x2, blocking collectives, staged_gather(): values = lax.all_gather(values, axes[1:], axis=axis, tiled=True)  53.5 us
    ppermute x3, waiting for transfers between devices, per_device(): lax.ppermute(partial, TP_AXES, perm=[(s, (s + k) % n_tp) for s in range(n...  29.3 us
    all_gather x2, waiting for transfers between devices, staged_gather(): return lax.all_gather(values, axes[0], axis=axis, tiled=True)  17.1 us
    gather x4, local copies, waits for them, and re-layouts, padded_attention(): cache = pool[page_row].reshape(-1, 2 * HEAD)  16.4 us
    dot_general x8, matrix products, value_weighted_rows(): jnp.einsum(form, weights.astype(jnp.bfloat16), values, preferred_element_...  16.4 us
    dot_general x4, matrix products, per_device(): jnp.dot(context, full_out, preferred_element_type=jnp.float32)  13.4 us
    reduce_sum x8, other arithmetic, padded_attention(): total = cached_exp.sum(-1) + recent_exponent.sum(-1)  11 us
    ppermute x3, starting transfers between devices, per_device(): lax.ppermute(normed, TP_AXES, perm=[(s, (s - k) % n_tp) for s in range(n_...  10.9 us
  transfers between devices with their start and end apart: 8, of which 5 were waited for; matrix products, arithmetic and copies ran while one was open for 38% of the time, Pallas kernels for 0%

profile of v6, /device:TPU:1, one launch (start us, length us, event | category | flops | bytes accessed | tf_op | source)
XLA Modules:
  0.0 237.3 jit_solution(6862516870036267233)
XLA Ops:
  7.2 27.4 %all_gather.12 = bf16[512,768]{1,0:T(8,128)(2,1)} all-gather(bf16[64,768]{1,0:T(8,128)(2,1)} %param.10), channel_id=1, replica_groups=mesh['z'=8,'ylo'=2,'x'=4,'yhi'=2,'core'=2] {'ylo','x'}, dimensions={0}, use_global_device_ids=true | all-gather | bytes 884736 | tf_op jit(solution)/shard_map/all_gather | solution.py:70
  35.4 1.5 fusion.33
  36.9 2.5 %fusion.35 = bf16[128,4096]{1,0:T(8,128)(2,1)} fusion(bf16[128,4096]{1,0:T(8,128)(2,1)} %param.8, f32[4096]{0:T(1024)S(1)} %convert_element_type.102, f32[128]{0:T(128)S(1)} %add_rsqrt_fusion), kind=kLoop, calls=%fused_computation.55 | loop fusion | flops 2097152 | bytes 2114048 | tf_op jit(solution)/shard_map/convert_element_type | solution.py:77
  39.4 7.7 %collective-permute-start = (bf16[128,4096]{1,0:T(8,128)(2,1)}, bf16[128,4096]{1,0:T(8,128)(2,1)}, u32[]{:S(2)}, u32[]{:S(2)}) collective-permute-start(bf16[128,4096]{1,0:T(8,128)(2,1)} %fusion.35), channel_id=1, source_target_pairs={{0,3},{1,0},{2,1},{3,2},{4,7},{5,4},{6,5},{7,6},{8,11},{9,8},{10,9... | collective-permute-start | bytes 3145736 | tf_op jit(solution)/shard_map/ppermute | solution.py:83
  47.2 1.3 collective-permute-start.1
  48.5 1.9 collective-permute-start.2
  50.3 26.1 %all_gather.14 = bf16[512,512]{0,1:T(8,128)(2,1)} all-gather(bf16[512,64]{0,1:T(8,128)(2,1)} %param.11), channel_id=1, replica_groups=mesh['z'=8,'ylo'=2,'x'=4,'yhi'=2,'core'=2] {'ylo','x'}, dimensions={1}, use_global_device_ids=true | all-gather | bytes 589824 | tf_op jit(solution)/shard_map/all_gather | solution.py:70
  85.5 3.5 %gather_fusion.2 = bf16[24,128,256]{2,1,0:T(8,128)(2,1)S(1)} fusion(bf16[96,128,256]{2,1,0:T(8,128)(2,1)} %param.15, s32[1024]{0:T(1024)S(1)} %get-tuple-element.45), kind=kCustom, calls=%fused_computation.2 | custom fusion | bytes 3145824 | tf_op jit(solution)/shard_map/gather | solution.py:46
  89.0 4.8 %gather_fusion.3 = bf16[24,128,256]{2,1,0:T(8,128)(2,1)} fusion(bf16[96,128,256]{2,1,0:T(8,128)(2,1)} %param.15, s32[1024]{0:T(1024)S(1)} %get-tuple-element.44), kind=kCustom, calls=%fused_computation.3 | custom fusion | bytes 3145824 | tf_op jit(solution)/shard_map/gather | solution.py:46
  93.8 4.7 %gather_fusion.4 = bf16[24,128,256]{2,1,0:T(8,128)(2,1)} fusion(bf16[96,128,256]{2,1,0:T(8,128)(2,1)} %param.15, s32[1024]{0:T(1024)S(1)} %get-tuple-element.43), kind=kCustom, calls=%fused_computation.4 | custom fusion | bytes 3145824 | tf_op jit(solution)/shard_map/gather | solution.py:46
  98.5 3.5 %gather_fusion.5 = bf16[24,128,256]{2,1,0:T(8,128)(2,1)S(1)} fusion(bf16[96,128,256]{2,1,0:T(8,128)(2,1)} %param.15, s32[1024]{0:T(1024)S(1)} %get-tuple-element.42), kind=kCustom, calls=%fused_computation.5 | custom fusion | bytes 3145824 | tf_op jit(solution)/shard_map/gather | solution.py:46
  106.5 10.6 %all-gather.3.cloned.1.call-done = bf16[4096,768]{1,0:T(8,128)(2,1)} async-done(((bf16[512,768]{1,0:T(8,128)(2,1)}), bf16[4096,768]{1,0:T(8,128)(2,1)}) %all-gather.3.cloned.1.call-update) | async-done | bytes 6291472 | tf_op jit(solution)/shard_map/all_gather | solution.py:71
  117.1 8.4 %fusion.36 = bf16[512,768]{1,0:T(8,128)(2,1)} fusion(bf16[4096,768]{1,0:T(8,128)(2,1)} %all-gather.3.cloned.1.call-done, bf16[128,4096]{1,0:T(8,128)(2,1)} %collective-permute-done.2, bf16[128,4096]{1,0:T(8,128)(2,1)} %collective-permute-done.1, bf16[128,4096]{1,0:T(8,128)(2,1)} %collective-permute-done, bf16[128,4096]{1,0:T(8,128)(2,1)} %fusion.35), kind=kOutput, calls=%fused_computation.57 | convolution fusion | flops 3238395904 | bytes 11272192 | tf_op jit(solution)/shard_map/dot_general | solution.py:88
  125.4 2.3 copy.47
  127.7 1.7 slice_bitcast_fusion.16
  129.4 1.9 slice.173
  131.2 1.3 subtract_convert_fusion.1
  132.5 1.0 copy.49
  133.5 1.7 copy.50
  135.3 2.0 copy.92
  137.3 1.1 convert_element_type.105
  138.4 1.4 subtract_convert_fusion
  139.8 1.1 fusion.136
  140.9 1.1 bitcast_reduce_fusion.3
  142.4 1.1 bitcast_reduce_fusion.2
  143.5 1.0 fusion.135
  145.1 1.1 bitcast_reduce_fusion.1
  146.5 1.0 bitcast_reduce_fusion
  148.2 2.2 fusion.7
  150.4 1.7 fusion.25
  152.1 1.6 fusion.56
  153.8 2.5 %fusion.5 = f32[4,128]{1,0:T(4,128)} fusion(f32[3072,128,4]{1,0,2:T(8,128)S(1)} %get-tuple-element.35, f32[4,128]{1,0:T(4,128)S(1)} %max.28, pred[3072]{0:T(1024)(128)(4,1)S(1)} %iota_compare_fusion.4), kind=kLoop, calls=%fused_computation.27 | loop fusion | flops 6290944 | bytes 6298624 | tf_op jit(solution)/shard_map/reduce_sum | solution.py:57
  156.3 2.0 fusion.9
  158.2 2.6 %fusion.11 = f32[4,128]{1,0:T(4,128)} fusion(f32[3072,128,4]{1,0,2:T(8,128)S(1)} %get-tuple-element.27, f32[4,128]{1,0:T(4,128)S(1)} %max.31, pred[3072]{0:T(1024)(128)(4,1)S(1)} %iota_compare_fusion.1), kind=kLoop, calls=%fused_computation.33 | loop fusion | flops 6290944 | bytes 6298624 | tf_op jit(solution)/shard_map/reduce_sum | solution.py:57
  160.8 2.5 %fusion.23 = f32[4,128,128]{1,2,0:T(8,128)} fusion(f32[3072,128,4]{1,0,2:T(8,128)S(1)} %get-tuple-element.31, f32[4,128]{1,0:T(4,128)S(1)} %max.30, pred[3072]{0:T(1024)(128)(4,1)S(1)} %iota_compare_fusion.2, bf16[3072,256]{1,0:T(8,128)(2,1)S(1)} %bitcast.236), kind=kOutput, calls=%fused_computation.44 | convolution fusion | flops 408944640 | bytes 7345152 | tf_op jit(solution)/shard_map/gnk,kd->gnd/dot_general | solution.py:38
  163.3 2.5 %fusion.21 = f32[4,128,128]{1,2,0:T(8,128)} fusion(f32[3072,128,4]{1,0,2:T(8,128)S(1)} %get-tuple-element.27, f32[4,128]{1,0:T(4,128)S(1)} %max.31, pred[3072]{0:T(1024)(128)(4,1)S(1)} %iota_compare_fusion.1, bf16[3072,256]{1,0:T(8,128)(2,1)S(1)} %bitcast.234), kind=kOutput, calls=%fused_computation.43 | convolution fusion | flops 408944640 | bytes 7345152 | tf_op jit(solution)/shard_map/gnk,kd->gnd/dot_general | solution.py:38
  165.7 6.5 %all-gather.5.cloned.1.call-done = bf16[512,4096]{0,1:T(8,128)(2,1)} async-done(((bf16[512,512]{0,1:T(8,128)(2,1)}), bf16[512,4096]{0,1:T(8,128)(2,1)}) %all-gather.5.cloned.1.call-update) | async-done | bytes 4194320 | tf_op jit(solution)/shard_map/all_gather | solution.py:71
  172.2 3.9 %convolution_convert_fusion.2 = bf16[128,4096]{1,0:T(8,128)(2,1)S(1)} fusion(bf16[128,512]{0,1:T(8,128)(2,1)} %bitcast.246, bf16[512,4096]{0,1:T(8,128)(2,1)} %all-gather.5.cloned.1.call-done), kind=kOutput, calls=%fused_computation.24 | convolution fusion | flops 537395200 | bytes 5373952 | tf_op jit(solution)/shard_map/dot_general | solution.py:124
  176.1 3.5 %collective-permute-start.3 = (bf16[128,4096]{1,0:T(8,128)(2,1)S(1)}, bf16[128,4096]{1,0:T(8,128)(2,1)}, u32[]{:S(2)}, u32[]{:S(2)}) collective-permute-start(bf16[128,4096]{1,0:T(8,128)(2,1)S(1)} %convolution_convert_fusion.2), channel_id=1, source_target_pairs={{0,1},{1,2},{2,3},{3,0},{4,5},{5,6},{6,7},{7,4},{8,9},{9,10},{10,1... | collective-permute-start | bytes 3145736 | tf_op jit(solution)/shard_map/ppermute | solution.py:128
  179.7 1.0 fusion.72
  180.7 1.3 fusion.57
  182.0 2.5 %convolution_convert_fusion.1 = bf16[128,4096]{1,0:T(8,128)(2,1)} fusion(bf16[128,512]{0,1:T(8,128)(2,1)S(1)} %bitcast.247, bf16[512,4096]{0,1:T(8,128)(2,1)S(1)} %copy-done.3), kind=kOutput, calls=%fused_computation.23 | convolution fusion | flops 537395200 | bytes 5373952 | tf_op jit(solution)/shard_map/dot_general | solution.py:124
  185.8 2.5 %convolution_convert_fusion = bf16[128,4096]{1,0:T(8,128)(2,1)} fusion(bf16[128,512]{0,1:T(8,128)(2,1)S(1)} %bitcast.248, bf16[512,4096]{0,1:T(8,128)(2,1)S(1)} %copy-done.3), kind=kOutput, calls=%fused_computation.22 | convolution fusion | flops 537395200 | bytes 5373952 | tf_op jit(solution)/shard_map/dot_general | solution.py:124
  190.7 5.0 %fusion.27 = f32[4,128,128]{1,2,0:T(8,128)S(1)} fusion(f32[3072,128,4]{1,0,2:T(8,128)} %copy-done.5, f32[4,128]{1,0:T(4,128)S(1)} %copy-done.13, pred[3072]{0:T(1024)(128)(4,1)S(1)} %iota_compare_fusion.4, bf16[3072,256]{1,0:T(8,128)(2,1)S(1)} %bitcast.232), kind=kOutput, calls=%fused_computation.46 | convolution fusion | flops 408944640 | bytes 7345152 | tf_op jit(solution)/shard_map/gnk,kd->gnd/dot_general | solution.py:38
  195.7 1.0 fusion.55
  197.1 23.3 %collective-permute-done.4 = bf16[128,4096]{1,0:T(8,128)(2,1)} collective-permute-done((bf16[128,4096]{1,0:T(8,128)(2,1)}, bf16[128,4096]{1,0:T(8,128)(2,1)}, u32[]{:S(2)}, u32[]{:S(2)}) %collective-permute-start.4) | collective-permute-done | bytes 1048608 | tf_op jit(solution)/shard_map/ppermute | solution.py:128
  220.3 5.6 %collective-permute-done.5 = bf16[128,4096]{1,0:T(8,128)(2,1)} collective-permute-done((bf16[128,4096]{1,0:T(8,128)(2,1)}, bf16[128,4096]{1,0:T(8,128)(2,1)}, u32[]{:S(2)}, u32[]{:S(2)}) %collective-permute-start.5) | collective-permute-done | bytes 1048608 | tf_op jit(solution)/shard_map/ppermute | solution.py:128
  225.9 4.6 %add_convert_fusion = bf16[128,4096]{1,0:T(8,128)(2,1)} fusion(bf16[128,4096]{1,0:T(8,128)(2,1)} %collective-permute-done.5, bf16[128,4096]{1,0:T(8,128)(2,1)} %collective-permute-done.4, bf16[128,4096]{1,0:T(8,128)(2,1)} %collective-permute-done.3, bf16[128,512]{0,1:T(8,128)(2,1)S(1)} %bitcast.245, bf16[512,4096]{0,1:T(8,128)(2,1)S(1)} %copy-done.4), kind=kOutput, calls=%fused_computation.56 | convolution fusion | flops 541589504 | bytes 8519680 | tf_op jit(solution)/shard_map/dot_general | solution.py:124
  (92 shorter events, 12.8 us)
Async XLA Ops:
  7.2 75.1 %copy-start = (s32[256]{0:T(256)S(1)}, s32[256]{0:T(256)}, u32[]{:S(2)}) copy-start(s32[256]{0:T(256)} %param.13) | copy-start | bytes 3076
  7.2 78.2 %copy-start.20 = (s32[4,24]{1,0:T(4,128)S(1)}, s32[4,24]{1,0:T(4,128)}, u32[]{:S(2)}) copy-start(s32[4,24]{1,0:T(4,128)} %param.14) | copy-start | bytes 1156
  7.2 109.9 %all-gather.3.cloned.1.call-start = ((), (), s32[]{:S(2)}) async-start(), calls=%async_computation | async-start | bytes 7077888 | tf_op jit(solution)/shard_map/all_gather | solution.py:71
  34.6 137.6 %all-gather.5.cloned.1.call-start = ((), (), s32[]{:S(2)}) async-start(), calls=%async_computation.1 | async-start | bytes 4718592 | tf_op jit(solution)/shard_map/all_gather | solution.py:71
  39.4 67.0 %collective-permute-start = (bf16[128,4096]{1,0:T(8,128)(2,1)}, bf16[128,4096]{1,0:T(8,128)(2,1)}, u32[]{:S(2)}, u32[]{:S(2)}) collective-permute-start(bf16[128,4096]{1,0:T(8,128)(2,1)} %fusion.35), channel_id=1, source_target_pairs={{0,3},{1,0},{2,1},{3,2},{4,7},{5,4},{6,5},{7,6},{8,11},{9,8},{10,9... | collective-permute-start | bytes 3145736 | tf_op jit(solution)/shard_map/ppermute | solution.py:83
  47.2 59.3 %collective-permute-start.1 = (bf16[128,4096]{1,0:T(8,128)(2,1)}, bf16[128,4096]{1,0:T(8,128)(2,1)}, u32[]{:S(2)}, u32[]{:S(2)}) collective-permute-start(bf16[128,4096]{1,0:T(8,128)(2,1)} %fusion.35), channel_id=1, source_target_pairs={{0,2},{1,3},{2,0},{3,1},{4,6},{5,7},{6,4},{7,5},{8,10},{9,11},{10,... | collective-permute-start | bytes 3145736 | tf_op jit(solution)/shard_map/ppermute | solution.py:83
  48.5 58.0 %collective-permute-start.2 = (bf16[128,4096]{1,0:T(8,128)(2,1)}, bf16[128,4096]{1,0:T(8,128)(2,1)}, u32[]{:S(2)}, u32[]{:S(2)}) collective-permute-start(bf16[128,4096]{1,0:T(8,128)(2,1)} %fusion.35), channel_id=1, source_target_pairs={{0,1},{1,2},{2,3},{3,0},{4,5},{5,6},{6,7},{7,4},{8,9},{9,10},{10,1... | collective-permute-start | bytes 3145736 | tf_op jit(solution)/shard_map/ppermute | solution.py:83
  85.5 16.5 %copy-start.2 = (s32[256]{0:T(256)S(1)}, s32[256]{0:T(256)}, u32[]{:S(2)}) copy-start(s32[256]{0:T(256)} %param.12) | copy-start | bytes 3076
  139.8 2.2 copy-start.11
  140.9 6.6 %copy-start.8 = (f32[4,128,128]{1,2,0:T(8,128)}, f32[4,128,128]{1,2,0:T(8,128)S(1)}, u32[]{:S(2)}) copy-start(f32[4,128,128]{1,2,0:T(8,128)S(1)} %get-tuple-element.37) | copy-start | bytes 786436
  140.9 1.5 copy-start.7
  142.0 11.8 %copy-start.5 = (f32[3072,128,4]{1,0,2:T(8,128)}, f32[3072,128,4]{1,0,2:T(8,128)S(1)}, u32[]{:S(2)}) copy-start(f32[3072,128,4]{1,0,2:T(8,128)S(1)} %get-tuple-element.35) | copy-start | bytes 18874372
  142.0 11.7 %copy-start.12 = (f32[4,128]{1,0:T(4,128)}, f32[4,128]{1,0:T(4,128)S(1)}, u32[]{:S(2)}) copy-start(f32[4,128]{1,0:T(4,128)S(1)} %max.28) | copy-start | bytes 6148
  142.4 2.6 %copy-start.6 = (bf16[24,128,256]{2,1,0:T(8,128)(2,1)S(1)}, bf16[24,128,256]{2,1,0:T(8,128)(2,1)}, u32[]{:S(2)}) copy-start(bf16[24,128,256]{2,1,0:T(8,128)(2,1)} %gather_fusion.4) | copy-start | bytes 4718596
  146.1 14.7 %copy-start.16 = (f32[4,128]{1,0:T(4,128)}, f32[4,128]{1,0:T(4,128)S(1)}, u32[]{:S(2)}) copy-start(f32[4,128]{1,0:T(4,128)S(1)} %max.30) | copy-start | bytes 6148
  147.5 15.8 %copy-start.14 = (f32[4,128]{1,0:T(4,128)}, f32[4,128]{1,0:T(4,128)S(1)}, u32[]{:S(2)}) copy-start(f32[4,128]{1,0:T(4,128)S(1)} %max.31) | copy-start | bytes 6148
  163.3 16.4 %copy-start.17 = (f32[4,128]{1,0:T(4,128)S(1)}, f32[4,128]{1,0:T(4,128)}, u32[]{:S(2)}) copy-start(f32[4,128]{1,0:T(4,128)} %copy-done.16) | copy-start | bytes 6148
  165.7 19.0 %copy-start.15 = (f32[4,128]{1,0:T(4,128)S(1)}, f32[4,128]{1,0:T(4,128)}, u32[]{:S(2)}) copy-start(f32[4,128]{1,0:T(4,128)} %copy-done.14) | copy-start | bytes 6148
  165.7 19.0 %copy-start.19 = (f32[4,128]{1,0:T(4,128)S(1)}, f32[4,128]{1,0:T(4,128)}, u32[]{:S(2)}) copy-start(f32[4,128]{1,0:T(4,128)} %fusion.11) | copy-start | bytes 6148
  165.7 19.1 %copy-start.21 = (f32[4,128,128]{1,2,0:T(8,128)S(1)}, f32[4,128,128]{1,2,0:T(8,128)}, u32[]{:S(2)}) copy-start(f32[4,128,128]{1,2,0:T(8,128)} %fusion.21) | copy-start | bytes 786436
  172.2 9.7 %copy-start.3 = (bf16[512,4096]{0,1:T(8,128)(2,1)S(1)}, bf16[512,4096]{0,1:T(8,128)(2,1)}, u32[]{:S(2)}) copy-start(bf16[512,4096]{0,1:T(8,128)(2,1)} %all-gather.5.cloned.1.call-done) | copy-start | bytes 12582916
  176.1 20.9 %collective-permute-start.3 = (bf16[128,4096]{1,0:T(8,128)(2,1)S(1)}, bf16[128,4096]{1,0:T(8,128)(2,1)}, u32[]{:S(2)}, u32[]{:S(2)}) collective-permute-start(bf16[128,4096]{1,0:T(8,128)(2,1)S(1)} %convolution_convert_fusion.2), channel_id=1, source_target_pairs={{0,1},{1,2},{2,3},{3,0},{4,5},{5,6},{6,7},{7,4},{8,9},{9,10},{10,1... | collective-permute-start | bytes 3145736 | tf_op jit(solution)/shard_map/ppermute | solution.py:128
  182.0 6.5 %copy-start.10 = (bf16[512,128]{0,1:T(8,128)(2,1)S(1)}, bf16[512,128]{0,1:T(8,128)(2,1)}, u32[]{:S(2)}) copy-start(bf16[512,128]{0,1:T(8,128)(2,1)} %get-tuple-element.8) | copy-start | bytes 393220
  182.0 7.9 %copy-start.18 = (f32[4,128]{1,0:T(4,128)S(1)}, f32[4,128]{1,0:T(4,128)}, u32[]{:S(2)}) copy-start(f32[4,128]{1,0:T(4,128)} %fusion.68) | copy-start | bytes 6148
  182.0 8.7 %copy-start.13 = (f32[4,128]{1,0:T(4,128)S(1)}, f32[4,128]{1,0:T(4,128)}, u32[]{:S(2)}) copy-start(f32[4,128]{1,0:T(4,128)} %copy-done.12) | copy-start | bytes 6148
  184.5 35.8 %collective-permute-start.4 = (bf16[128,4096]{1,0:T(8,128)(2,1)}, bf16[128,4096]{1,0:T(8,128)(2,1)}, u32[]{:S(2)}, u32[]{:S(2)}) collective-permute-start(bf16[128,4096]{1,0:T(8,128)(2,1)} %convolution_convert_fusion.1), channel_id=1, source_target_pairs={{0,2},{1,3},{2,0},{3,1},{4,6},{5,7},{6,4},{7,5},{8,10},{9,11},{10,... | collective-permute-start | bytes 3145736 | tf_op jit(solution)/shard_map/ppermute | solution.py:128
  188.2 7.4 %copy-start.9 = (f32[4,128,128]{1,2,0:T(8,128)S(1)}, f32[4,128,128]{1,2,0:T(8,128)}, u32[]{:S(2)}) copy-start(f32[4,128,128]{1,2,0:T(8,128)} %copy-done.8) | copy-start | bytes 786436
  188.2 37.7 %collective-permute-start.5 = (bf16[128,4096]{1,0:T(8,128)(2,1)}, bf16[128,4096]{1,0:T(8,128)(2,1)}, u32[]{:S(2)}, u32[]{:S(2)}) collective-permute-start(bf16[128,4096]{1,0:T(8,128)(2,1)} %convolution_convert_fusion), channel_id=1, source_target_pairs={{0,3},{1,0},{2,1},{3,2},{4,7},{5,4},{6,5},{7,6},{8,11},{9,8},{10,9... | collective-permute-start | bytes 3145736 | tf_op jit(solution)/shard_map/ppermute | solution.py:128
  189.9 36.0 %copy-start.4 = (bf16[512,4096]{0,1:T(8,128)(2,1)S(1)}, bf16[512,4096]{0,1:T(8,128)(2,1)}, u32[]{:S(2)}) copy-start(bf16[512,4096]{0,1:T(8,128)(2,1)} %all-gather.5.cloned.1.call-done) | copy-start | bytes 12582916
  190.7 39.8 %copy-start.1 = (s32[256]{0:T(256)S(1)}, s32[256]{0:T(256)}, u32[]{:S(2)}) copy-start(s32[256]{0:T(256)} %param.13) | copy-start | bytes 3076
Sparse Core Ops, SparseCore 0:
  34.8 82.2 all-gather.2
  118.8 53.3 all-gather.4

commit v7 on v3

--- a/solution.py
+++ b/solution.py
@@ -109,7 +109,7 @@
     new_kv = lax.dynamic_slice_in_dim(doubled, ((slot_count - me) % slot_count) * NEW, tok_rows, 0)
     score_scale = 1.0 / math.sqrt(HEAD)
 
-    total = None
+    contexts = []
     for k in range(slot_count):
         rows = slice(k * NEW, (k + 1) * NEW)
         result = padded_attention(
@@ -121,13 +121,15 @@
             slot_length[k],
             score_scale,
         )
-        context = result.astype(jnp.bfloat16).transpose(1, 0, 2).reshape(NEW, group * HEAD)
-        partial = jnp.dot(context, full_out, preferred_element_type=jnp.float32).astype(
-            jnp.bfloat16
-        )
-        if k:
-            partial = lax.ppermute(partial, TP_AXES, perm=[(s, (s + k) % n_tp) for s in range(n_tp)])
-        total = partial.astype(jnp.float32) if total is None else total + partial.astype(jnp.float32)
+        contexts.append(result.astype(jnp.bfloat16).transpose(1, 0, 2).reshape(NEW, group * HEAD))
+    partials = jnp.dot(
+        jnp.concatenate(contexts, 0), full_out, preferred_element_type=jnp.float32
+    ).astype(jnp.bfloat16)
+    total = partials[:NEW].astype(jnp.float32)
+    for k in range(1, slot_count):
+        sent_to = [(s, (s + k) % n_tp) for s in range(n_tp)]
+        arrived_part = lax.ppermute(partials[k * NEW:(k + 1) * NEW], TP_AXES, perm=sent_to)
+        total = total + arrived_part.astype(jnp.float32)
     return (total.astype(jnp.bfloat16), new_kv)
 
 

time: 234 us -> 238 us (1.017)
  waiting for transfers between devices: 28.7 us -> 43.4 us
  matrix products: 44.9 us -> 32 us
  local copies, waits for them, and re-layouts: 29.4 us -> 32.4 us
    ppermute x3, waiting for transfers between devices: 28.7 us -> 43.3 us  [per_device(): lax.ppermute(partials[k * NEW:(k + 1) * NEW], TP_AXES, perm=sent_to)]
    dot_general x4 -> x1, matrix products: 13.4 us -> 4.62 us  [per_device(): jnp.dot(jnp.concatenate(contexts, 0), full_out, preferred_element_type=jn...]
    dot_general x8, matrix products: 16.4 us -> 11.5 us  [value_weighted_rows(): jnp.einsum(form, weights.astype(jnp.bfloat16), values, preferred_element_...]
    convert_element_type x0 -> x1, other arithmetic: none -> 2.85 us  [per_device(): return (total.astype(jnp.bfloat16), new_kv)]
    reduce_sum x8, other arithmetic: 11 us -> 8.41 us  [padded_attention(): total = cached_exp.sum(-1) + recent_exponent.sum(-1)]
    unnamed x46 -> x20, local copies, waits for them, and re-layouts: 3.65 us -> 4.86 us
  transfers between devices with their start and end apart: 8 -> 8, of which waited for: 2 -> 3; matrix products, arithmetic and copies ran while one was open for 39% -> 33% of each run, Pallas kernels for 0% -> 0%
where the time goes in v7:
time: 238 us; the launch traced here: 237 us
  blocking collectives  69.3 us (29%)
  waiting for transfers between devices  43.4 us (18%)
  local copies, waits for them, and re-layouts  32.4 us (14%)
  matrix products  32 us (13%)
  other arithmetic  26.1 us (11%)
  between operations  22.1 us (9%)
  starting transfers between devices  11.9 us (5%)
    all_gather x4, blocking collectives, staged_gather(): values = lax.all_gather(values, name, axis=axis, tiled=True)  69.3 us
    ppermute x3, waiting for transfers between devices, per_device(): lax.ppermute(partials[k * NEW:(k + 1) * NEW], TP_AXES, perm=sent_to)  43.3 us
    gather x4, local copies, waits for them, and re-layouts, padded_attention(): cache = pool[page_row].reshape(-1, 2 * HEAD)  16.2 us
    dot_general x8, matrix products, value_weighted_rows(): jnp.einsum(form, weights.astype(jnp.bfloat16), values, preferred_element_...  11.5 us
    ppermute x3, starting transfers between devices, per_device(): lax.ppermute(normed, TP_AXES, perm=[(s, (s - k) % n_tp) for s in range(n_...  8.45 us
    reduce_sum x8, other arithmetic, padded_attention(): total = cached_exp.sum(-1) + recent_exponent.sum(-1)  8.41 us
    dot_general x1, matrix products, per_device(): jnp.dot(gathered, staged_gather(w_qkv, REQ_AXES, 0), preferred_element_ty...  8.36 us
    unnamed x20, local copies, waits for them, and re-layouts  4.86 us
  transfers between devices with their start and end apart: 8, of which 3 were waited for; matrix products, arithmetic and copies ran while one was open for 33% of the time, Pallas kernels for 0%

profile of v7, /device:TPU:1, one launch (start us, length us, event | category | flops | bytes accessed | tf_op | source)
XLA Modules:
  0.0 237.2 jit_solution(7441791836424287945)
XLA Ops:
  7.2 11.9 %all_gather.18 = bf16[256,768]{1,0:T(8,128)(2,1)S(1)} all-gather(bf16[64,768]{1,0:T(8,128)(2,1)} %param.10), channel_id=1, replica_groups=mesh['z'=8,'ylo'=2,'x'=4,'yhi'=2,'core'=2] {'x'}, dimensions={0}, use_global_device_ids=true | all-gather | bytes 491520 | tf_op jit(solution)/shard_map/all_gather | solution.py:71
  19.2 7.6 %all_gather.19 = bf16[512,768]{1,0:T(8,128)(2,1)} all-gather(bf16[256,768]{1,0:T(8,128)(2,1)S(1)} %all_gather.18), channel_id=1, replica_groups=mesh['z'=8,'ylo'=2,'x'=4,'yhi'=2,'core'=2] {'ylo'}, dimensions={0}, use_global_device_ids=true | all-gather | bytes 1179648 | tf_op jit(solution)/shard_map/all_gather | solution.py:71
  27.5 1.5 fusion.32
  29.1 2.5 %fusion.34 = bf16[128,4096]{1,0:T(8,128)(2,1)} fusion(bf16[128,4096]{1,0:T(8,128)(2,1)} %param.8, f32[4096]{0:T(1024)S(1)} %convert_element_type.93, f32[128]{0:T(128)S(1)} %add_rsqrt_fusion), kind=kLoop, calls=%fused_computation.51 | loop fusion | flops 2097152 | bytes 2114048 | tf_op jit(solution)/shard_map/convert_element_type | solution.py:78
  31.6 5.3 %collective-permute-start = (bf16[128,4096]{1,0:T(8,128)(2,1)}, bf16[128,4096]{1,0:T(8,128)(2,1)}, u32[]{:S(2)}, u32[]{:S(2)}) collective-permute-start(bf16[128,4096]{1,0:T(8,128)(2,1)} %fusion.34), channel_id=1, source_target_pairs={{0,3},{1,0},{2,1},{3,2},{4,7},{5,4},{6,5},{7,6},{8,11},{9,8},{10,9... | collective-permute-start | bytes 3145736 | tf_op jit(solution)/shard_map/ppermute | solution.py:84
  36.9 2.3 collective-permute-start.1
  40.1 10.5 %all_gather.21 = bf16[512,256]{0,1:T(8,128)(2,1)S(1)} all-gather(bf16[512,64]{0,1:T(8,128)(2,1)} %param.11), channel_id=1, replica_groups=mesh['z'=8,'ylo'=2,'x'=4,'yhi'=2,'core'=2] {'x'}, dimensions={1}, use_global_device_ids=true | all-gather | bytes 327680 | tf_op jit(solution)/shard_map/all_gather | solution.py:71
  50.6 39.3 %all_gather.22 = bf16[512,512]{0,1:T(8,128)(2,1)} all-gather(bf16[512,256]{0,1:T(8,128)(2,1)S(1)} %all_gather.21), channel_id=1, replica_groups=mesh['z'=8,'ylo'=2,'x'=4,'yhi'=2,'core'=2] {'ylo'}, dimensions={1}, use_global_device_ids=true | all-gather | bytes 786432 | tf_op jit(solution)/shard_map/all_gather | solution.py:71
  99.0 4.7 %gather_fusion.2 = bf16[24,128,256]{2,1,0:T(8,128)(2,1)} fusion(bf16[96,128,256]{2,1,0:T(8,128)(2,1)} %param.15, s32[1024]{0:T(1024)S(1)} %get-tuple-element.48), kind=kCustom, calls=%fused_computation.2 | custom fusion | bytes 3145824 | tf_op jit(solution)/shard_map/gather | solution.py:46
  103.7 4.6 %gather_fusion.3 = bf16[24,128,256]{2,1,0:T(8,128)(2,1)} fusion(bf16[96,128,256]{2,1,0:T(8,128)(2,1)} %param.15, s32[1024]{0:T(1024)S(1)} %get-tuple-element.47), kind=kCustom, calls=%fused_computation.3 | custom fusion | bytes 3145824 | tf_op jit(solution)/shard_map/gather | solution.py:46
  108.3 3.4 %gather_fusion.4 = bf16[24,128,256]{2,1,0:T(8,128)(2,1)S(1)} fusion(bf16[96,128,256]{2,1,0:T(8,128)(2,1)} %param.15, s32[1024]{0:T(1024)S(1)} %get-tuple-element.46), kind=kCustom, calls=%fused_computation.4 | custom fusion | bytes 3145824 | tf_op jit(solution)/shard_map/gather | solution.py:46
  111.8 3.4 %gather_fusion.5 = bf16[24,128,256]{2,1,0:T(8,128)(2,1)S(1)} fusion(bf16[96,128,256]{2,1,0:T(8,128)(2,1)} %param.15, s32[1024]{0:T(1024)S(1)} %get-tuple-element.45), kind=kCustom, calls=%fused_computation.5 | custom fusion | bytes 3145824 | tf_op jit(solution)/shard_map/gather | solution.py:46
  119.7 8.4 %fusion.35 = bf16[512,768]{1,0:T(8,128)(2,1)} fusion(bf16[4096,768]{1,0:T(8,128)(2,1)} %all-gather.3.cloned.1.call-done, bf16[128,4096]{1,0:T(8,128)(2,1)} %collective-permute-done.2, bf16[128,4096]{1,0:T(8,128)(2,1)} %collective-permute-done.1, bf16[128,4096]{1,0:T(8,128)(2,1)} %collective-permute-done, bf16[128,4096]{1,0:T(8,128)(2,1)} %fusion.34), kind=kOutput, calls=%fused_computation.53 | convolution fusion | flops 3238395904 | bytes 11272192 | tf_op jit(solution)/shard_map/dot_general | solution.py:89
  128.1 2.3 copy.47
  130.4 1.6 slice_bitcast_fusion.16
  132.0 1.9 slice.189
  133.9 1.3 subtract_convert_fusion.1
  135.2 1.0 copy.49
  136.2 1.7 copy.50
  137.9 2.1 copy.92
  140.0 1.2 convert_element_type.96
  141.2 1.4 subtract_convert_fusion
  142.6 1.0 fusion.145
  143.6 1.0 fusion.144
  144.7 1.1 fusion.143
  145.8 1.1 bitcast_reduce_fusion.3
  146.9 1.1 bitcast_reduce_fusion.2
  148.0 1.1 bitcast_reduce_fusion.1
  149.4 1.0 bitcast_reduce_fusion
  150.7 2.2 fusion.4
  152.9 2.0 fusion.6
  154.9 2.0 fusion.8
  156.9 2.0 fusion.10
  158.9 1.7 fusion.26
  161.6 1.7 fusion.24
  163.3 1.6 fusion.55
  165.0 1.7 fusion.22
  166.7 1.0 fusion.56
  167.7 1.7 fusion.20
  170.5 4.6 %convolution_convert_fusion = bf16[512,4096]{1,0:T(8,128)(2,1)S(1)} fusion(bf16[512,4096]{0,1:T(8,128)(2,1)} %all-gather.5.cloned.1.call-done, bf16[128,512]{0,1:T(8,128)(2,1)S(1)} %bitcast.241, bf16[128,512]{0,1:T(8,128)(2,1)S(1)} %bitcast.240, bf16[128,512]{0,1:T(8,128)(2,1)S(1)} %bitcast.239, bf16[128,512]{0,1:T(8,128)(2,1)S(1)} %bitcast.238), kind=kOutput, calls=%fused_computation.22 | convolution fusion | flops 2151677952 | bytes 8912896 | tf_op jit(solution)/shard_map/dot_general | solution.py:125
  175.1 1.9 copy-done.3
  177.0 1.8 fusion.139
  178.8 2.2 collective-permute-start.3
  182.2 1.2 fusion.71
  184.3 18.6 %collective-permute-done.3 = bf16[128,4096]{1,0:T(8,128)(2,1)S(1)} collective-permute-done((bf16[128,4096]{1,0:T(8,128)(2,1)}, bf16[128,4096]{1,0:T(8,128)(2,1)S(1)}, u32[]{:S(2)}, u32[]{:S(2)}) %collective-permute-start.3) | collective-permute-done | bytes 1048608 | tf_op jit(solution)/shard_map/ppermute | solution.py:131
  202.9 23.4 %collective-permute-done.4 = bf16[128,4096]{1,0:T(8,128)(2,1)S(1)} collective-permute-done((bf16[128,4096]{1,0:T(8,128)(2,1)}, bf16[128,4096]{1,0:T(8,128)(2,1)S(1)}, u32[]{:S(2)}, u32[]{:S(2)}) %collective-permute-start.4) | collective-permute-done | bytes 1048608 | tf_op jit(solution)/shard_map/ppermute | solution.py:131
  226.2 1.3 collective-permute-done.5
  227.6 2.8 %add_convert_fusion = bf16[128,4096]{1,0:T(8,128)(2,1)} fusion(bf16[128,4096]{1,0:T(8,128)(2,1)S(1)} %collective-permute-done.5, bf16[128,4096]{1,0:T(8,128)(2,1)S(1)} %collective-permute-done.4, bf16[128,4096]{1,0:T(8,128)(2,1)S(1)} %collective-permute-done.3, bf16[512,4096]{1,0:T(8,128)(2,1)} %copy-done.3), kind=kLoop, calls=%fused_computation.52 | loop fusion | flops 4194304 | bytes 5242880 | tf_op jit(solution)/shard_map/convert_element_type | solution.py:133
  (67 shorter events, 12.2 us)
Async XLA Ops:
  7.2 88.5 %copy-start = (s32[256]{0:T(256)S(1)}, s32[256]{0:T(256)}, u32[]{:S(2)}) copy-start(s32[256]{0:T(256)} %param.13) | copy-start | bytes 3076
  7.2 91.7 %copy-start.7 = (s32[4,24]{1,0:T(4,128)S(1)}, s32[4,24]{1,0:T(4,128)}, u32[]{:S(2)}) copy-start(s32[4,24]{1,0:T(4,128)} %param.14) | copy-start | bytes 1156
  7.2 112.5 %all-gather.3.cloned.1.call-start = ((), (), s32[]{:S(2)}) async-start(), calls=%async_computation | async-start | bytes 7077888 | tf_op jit(solution)/shard_map/all_gather | solution.py:71
  26.8 143.7 %all-gather.5.cloned.1.call-start = ((), (), s32[]{:S(2)}) async-start(), calls=%async_computation.1 | async-start | bytes 4718592 | tf_op jit(solution)/shard_map/all_gather | solution.py:71
  31.6 88.1 %collective-permute-start = (bf16[128,4096]{1,0:T(8,128)(2,1)}, bf16[128,4096]{1,0:T(8,128)(2,1)}, u32[]{:S(2)}, u32[]{:S(2)}) collective-permute-start(bf16[128,4096]{1,0:T(8,128)(2,1)} %fusion.34), channel_id=1, source_target_pairs={{0,3},{1,0},{2,1},{3,2},{4,7},{5,4},{6,5},{7,6},{8,11},{9,8},{10,9... | collective-permute-start | bytes 3145736 | tf_op jit(solution)/shard_map/ppermute | solution.py:84
  36.9 82.8 %collective-permute-start.1 = (bf16[128,4096]{1,0:T(8,128)(2,1)}, bf16[128,4096]{1,0:T(8,128)(2,1)}, u32[]{:S(2)}, u32[]{:S(2)}) collective-permute-start(bf16[128,4096]{1,0:T(8,128)(2,1)} %fusion.34), channel_id=1, source_target_pairs={{0,2},{1,3},{2,0},{3,1},{4,6},{5,7},{6,4},{7,5},{8,10},{9,11},{10,... | collective-permute-start | bytes 3145736 | tf_op jit(solution)/shard_map/ppermute | solution.py:84
  39.2 80.5 %collective-permute-start.2 = (bf16[128,4096]{1,0:T(8,128)(2,1)}, bf16[128,4096]{1,0:T(8,128)(2,1)}, u32[]{:S(2)}, u32[]{:S(2)}) collective-permute-start(bf16[128,4096]{1,0:T(8,128)(2,1)} %fusion.34), channel_id=1, source_target_pairs={{0,1},{1,2},{2,3},{3,0},{4,5},{5,6},{6,7},{7,4},{8,9},{9,10},{10,1... | collective-permute-start | bytes 3145736 | tf_op jit(solution)/shard_map/ppermute | solution.py:84
  99.0 16.3 %copy-start.2 = (s32[256]{0:T(256)S(1)}, s32[256]{0:T(256)}, u32[]{:S(2)}) copy-start(s32[256]{0:T(256)} %param.12) | copy-start | bytes 3076
  140.0 5.8 %copy-start.5 = (bf16[24,128,256]{2,1,0:T(8,128)(2,1)S(1)}, bf16[24,128,256]{2,1,0:T(8,128)(2,1)}, u32[]{:S(2)}) copy-start(bf16[24,128,256]{2,1,0:T(8,128)(2,1)} %gather_fusion.2) | copy-start | bytes 4718596
  144.6 2.2 copy-start.4
  148.0 1.2 copy-start.6
  166.7 3.8 %copy-start.8 = (bf16[128,4,128]{0,2,1:T(8,128)(2,1)S(1)}, bf16[128,4,128]{0,2,1:T(8,128)(2,1)}, u32[]{:S(2)}) copy-start(bf16[128,4,128]{0,2,1:T(8,128)(2,1)} %fusion.55) | copy-start | bytes 393220
  170.5 59.9 %copy-start.1 = (s32[256]{0:T(256)S(1)}, s32[256]{0:T(256)}, u32[]{:S(2)}) copy-start(s32[256]{0:T(256)} %param.13) | copy-start | bytes 3076
  175.1 1.9 copy-start.3
  178.8 24.0 %collective-permute-start.3 = (bf16[128,4096]{1,0:T(8,128)(2,1)}, bf16[128,4096]{1,0:T(8,128)(2,1)S(1)}, u32[]{:S(2)}, u32[]{:S(2)}) collective-permute-start(bf16[128,4096]{1,0:T(8,128)(2,1)} %get-tuple-element.6), channel_id=1, source_target_pairs={{0,1},{1,2},{2,3},{3,0},{4,5},{5,6},{6,7},{7,4},{8,9},{9,10},{10,1... | collective-permute-start | bytes 3145736 | tf_op jit(solution)/shard_map/ppermute | solution.py:131
  181.0 45.2 %collective-permute-start.4 = (bf16[128,4096]{1,0:T(8,128)(2,1)}, bf16[128,4096]{1,0:T(8,128)(2,1)S(1)}, u32[]{:S(2)}, u32[]{:S(2)}) collective-permute-start(bf16[128,4096]{1,0:T(8,128)(2,1)} %get-tuple-element.8), channel_id=1, source_target_pairs={{0,2},{1,3},{2,0},{3,1},{4,6},{5,7},{6,4},{7,5},{8,10},{9,11},{10,... | collective-permute-start | bytes 3145736 | tf_op jit(solution)/shard_map/ppermute | solution.py:131
  181.5 46.1 %collective-permute-start.5 = (bf16[128,4096]{1,0:T(8,128)(2,1)}, bf16[128,4096]{1,0:T(8,128)(2,1)S(1)}, u32[]{:S(2)}, u32[]{:S(2)}) collective-permute-start(bf16[128,4096]{1,0:T(8,128)(2,1)} %get-tuple-element.7), channel_id=1, source_target_pairs={{0,3},{1,0},{2,1},{3,2},{4,7},{5,4},{6,5},{7,6},{8,11},{9,8},{10,9... | collective-permute-start | bytes 3145736 | tf_op jit(solution)/shard_map/ppermute | solution.py:131
Sparse Core Ops, SparseCore 0:
  26.9 79.8 all-gather.2
  108.6 53.3 all-gather.4

commit v8 on v7

--- a/solution.py
+++ b/solution.py
@@ -122,14 +122,22 @@
             score_scale,
         )
         contexts.append(result.astype(jnp.bfloat16).transpose(1, 0, 2).reshape(NEW, group * HEAD))
-    partials = jnp.dot(
-        jnp.concatenate(contexts, 0), full_out, preferred_element_type=jnp.float32
-    ).astype(jnp.bfloat16)
-    total = partials[:NEW].astype(jnp.float32)
-    for k in range(1, slot_count):
-        sent_to = [(s, (s + k) % n_tp) for s in range(n_tp)]
-        arrived_part = lax.ppermute(partials[k * NEW:(k + 1) * NEW], TP_AXES, perm=sent_to)
-        total = total + arrived_part.astype(jnp.float32)
+    stepped = jnp.concatenate(contexts, 0)
+    stepped = jnp.concatenate([stepped, stepped], 0)
+    in_order = lax.dynamic_slice_in_dim(stepped, ((slot_count - me) % slot_count) * NEW, tok_rows, 0)
+    partials = jnp.dot(in_order, full_out, preferred_element_type=jnp.float32).astype(jnp.bfloat16)
+    n_hi = lax.axis_size("yhi")
+    n_core = lax.axis_size("core")
+    partials = partials.reshape(n_hi, n_core, NEW, partials.shape[-1])
+    core = lax.axis_index("core")
+    hi = lax.axis_index("yhi")
+    kept = lax.dynamic_index_in_dim(partials, core, 1, keepdims=False)
+    given = lax.dynamic_index_in_dim(partials, 1 - core, 1, keepdims=False)
+    taken = lax.ppermute(given, "core", perm=[(0, 1), (1, 0)])
+    pair_sum = kept.astype(jnp.float32) + taken.astype(jnp.float32)
+    mine = lax.dynamic_index_in_dim(pair_sum, hi, 0, keepdims=False)
+    theirs = lax.dynamic_index_in_dim(pair_sum, 1 - hi, 0, keepdims=False).astype(jnp.bfloat16)
+    total = mine + lax.ppermute(theirs, "yhi", perm=[(0, 1), (1, 0)]).astype(jnp.float32)
     return (total.astype(jnp.bfloat16), new_kv)
 
 

time: 238 us -> 230 us (0.966)
  waiting for transfers between devices: 43.4 us -> 26.3 us
  local copies, waits for them, and re-layouts: 32.4 us -> 38.5 us
  other arithmetic: 26.1 us -> 28.6 us
    ppermute x3 -> x2, waiting for transfers between devices: 43.3 us -> 26.3 us  [the longest x1 22 us: per_device(): lax.ppermute(theirs, 'yhi', perm=[(0, 1), (1, 0)]).astype(jnp.float32)]
    unnamed x20 -> x27, local copies, waits for them, and re-layouts: 4.86 us -> 11.8 us
    add x0 -> x1, other arithmetic: none -> 2.94 us  [per_device(): pair_sum = kept.astype(jnp.float32) + taken.astype(jnp.float32)]
  transfers between devices with their start and end apart: 8 -> 7, of which waited for: 3 -> 2; matrix products, arithmetic and copies ran while one was open for 33% -> 37% of each run, Pallas kernels for 0% -> 0%
where the time goes in v8:
time: 230 us; the launch traced here: 228 us
  blocking collectives  69.3 us (30%)
  local copies, waits for them, and re-layouts  38.5 us (17%)
  matrix products  32 us (14%)
  other arithmetic  28.6 us (12%)
  waiting for transfers between devices  26.3 us (11%)
  between operations  22.1 us (10%)
  starting transfers between devices  11.3 us (5%)
    all_gather x4, blocking collectives, staged_gather(): values = lax.all_gather(values, name, axis=axis, tiled=True)  69.3 us
    ppermute x1, waiting for transfers between devices, per_device(): lax.ppermute(theirs, 'yhi', perm=[(0, 1), (1, 0)]).astype(jnp.float32)  22 us
    gather x4, local copies, waits for them, and re-layouts, padded_attention(): cache = pool[page_row].reshape(-1, 2 * HEAD)  16.2 us
    unnamed x27, local copies, waits for them, and re-layouts  11.8 us
    dot_general x8, matrix products, value_weighted_rows(): jnp.einsum(form, weights.astype(jnp.bfloat16), values, preferred_element_...  10.8 us
    reduce_sum x8, other arithmetic, padded_attention(): total = cached_exp.sum(-1) + recent_exponent.sum(-1)  8.65 us
    ppermute x3, starting transfers between devices, per_device(): lax.ppermute(normed, TP_AXES, perm=[(s, (s - k) % n_tp) for s in range(n_...  8.45 us
    dot_general x1, matrix products, per_device(): jnp.dot(gathered, staged_gather(w_qkv, REQ_AXES, 0), preferred_element_ty...  8.36 us
  transfers between devices with their start and end apart: 7, of which 2 were waited for; matrix products, arithmetic and copies ran while one was open for 37% of the time, Pallas kernels for 0%

profile of v8, /device:TPU:1, one launch (start us, length us, event | category | flops | bytes accessed | tf_op | source)
XLA Modules:
  0.0 228.2 jit_solution(10451933454933105496)
XLA Ops:
  7.2 11.9 %all_gather.18 = bf16[256,768]{1,0:T(8,128)(2,1)S(1)} all-gather(bf16[64,768]{1,0:T(8,128)(2,1)} %param.10), channel_id=1, replica_groups=mesh['z'=8,'ylo'=2,'x'=4,'yhi'=2,'core'=2] {'x'}, dimensions={0}, use_global_device_ids=true | all-gather | bytes 491520 | tf_op jit(solution)/shard_map/all_gather | solution.py:71
  19.2 7.6 %all_gather.19 = bf16[512,768]{1,0:T(8,128)(2,1)} all-gather(bf16[256,768]{1,0:T(8,128)(2,1)S(1)} %all_gather.18), channel_id=1, replica_groups=mesh['z'=8,'ylo'=2,'x'=4,'yhi'=2,'core'=2] {'ylo'}, dimensions={0}, use_global_device_ids=true | all-gather | bytes 1179648 | tf_op jit(solution)/shard_map/all_gather | solution.py:71
  27.5 1.5 fusion.32
  29.1 2.5 %fusion.34 = bf16[128,4096]{1,0:T(8,128)(2,1)} fusion(bf16[128,4096]{1,0:T(8,128)(2,1)} %param.8, f32[4096]{0:T(1024)S(1)} %convert_element_type.99, f32[128]{0:T(128)S(1)} %add_rsqrt_fusion), kind=kLoop, calls=%fused_computation.52 | loop fusion | flops 2097152 | bytes 2114048 | tf_op jit(solution)/shard_map/convert_element_type | solution.py:78
  31.6 5.3 %collective-permute-start = (bf16[128,4096]{1,0:T(8,128)(2,1)}, bf16[128,4096]{1,0:T(8,128)(2,1)}, u32[]{:S(2)}, u32[]{:S(2)}) collective-permute-start(bf16[128,4096]{1,0:T(8,128)(2,1)} %fusion.34), channel_id=1, source_target_pairs={{0,3},{1,0},{2,1},{3,2},{4,7},{5,4},{6,5},{7,6},{8,11},{9,8},{10,9... | collective-permute-start | bytes 3145736 | tf_op jit(solution)/shard_map/ppermute | solution.py:84
  36.9 2.3 collective-permute-start.1
  40.1 10.5 %all_gather.21 = bf16[512,256]{0,1:T(8,128)(2,1)S(1)} all-gather(bf16[512,64]{0,1:T(8,128)(2,1)} %param.11), channel_id=1, replica_groups=mesh['z'=8,'ylo'=2,'x'=4,'yhi'=2,'core'=2] {'x'}, dimensions={1}, use_global_device_ids=true | all-gather | bytes 327680 | tf_op jit(solution)/shard_map/all_gather | solution.py:71
  50.6 39.3 %all_gather.22 = bf16[512,512]{0,1:T(8,128)(2,1)} all-gather(bf16[512,256]{0,1:T(8,128)(2,1)S(1)} %all_gather.21), channel_id=1, replica_groups=mesh['z'=8,'ylo'=2,'x'=4,'yhi'=2,'core'=2] {'ylo'}, dimensions={1}, use_global_device_ids=true | all-gather | bytes 786432 | tf_op jit(solution)/shard_map/all_gather | solution.py:71
  99.0 3.5 %gather_fusion.5 = bf16[24,128,256]{2,1,0:T(8,128)(2,1)S(1)} fusion(bf16[96,128,256]{2,1,0:T(8,128)(2,1)} %param.15, s32[1024]{0:T(1024)S(1)} %get-tuple-element.42), kind=kCustom, calls=%fused_computation.5 | custom fusion | bytes 3145824 | tf_op jit(solution)/shard_map/gather | solution.py:46
  102.5 3.4 %gather_fusion.4 = bf16[24,128,256]{2,1,0:T(8,128)(2,1)S(1)} fusion(bf16[96,128,256]{2,1,0:T(8,128)(2,1)} %param.15, s32[1024]{0:T(1024)S(1)} %get-tuple-element.43), kind=kCustom, calls=%fused_computation.4 | custom fusion | bytes 3145824 | tf_op jit(solution)/shard_map/gather | solution.py:46
  105.9 4.7 %gather_fusion.3 = bf16[24,128,256]{2,1,0:T(8,128)(2,1)} fusion(bf16[96,128,256]{2,1,0:T(8,128)(2,1)} %param.15, s32[1024]{0:T(1024)S(1)} %get-tuple-element.44), kind=kCustom, calls=%fused_computation.3 | custom fusion | bytes 3145824 | tf_op jit(solution)/shard_map/gather | solution.py:46
  110.6 4.6 %gather_fusion.2 = bf16[24,128,256]{2,1,0:T(8,128)(2,1)} fusion(bf16[96,128,256]{2,1,0:T(8,128)(2,1)} %param.15, s32[1024]{0:T(1024)S(1)} %get-tuple-element.45), kind=kCustom, calls=%fused_computation.2 | custom fusion | bytes 3145824 | tf_op jit(solution)/shard_map/gather | solution.py:46
  119.7 8.4 %fusion.36 = bf16[512,768]{1,0:T(8,128)(2,1)} fusion(bf16[4096,768]{1,0:T(8,128)(2,1)} %all-gather.3.cloned.1.call-done, bf16[128,4096]{1,0:T(8,128)(2,1)} %collective-permute-done.2, bf16[128,4096]{1,0:T(8,128)(2,1)} %collective-permute-done.1, bf16[128,4096]{1,0:T(8,128)(2,1)} %collective-permute-done, bf16[128,4096]{1,0:T(8,128)(2,1)} %fusion.34), kind=kOutput, calls=%fused_computation.57 | convolution fusion | flops 3238395904 | bytes 11272192 | tf_op jit(solution)/shard_map/dot_general | solution.py:89
  128.1 2.3 %copy.49 = bf16[512,768]{0,1:T(8,128)(2,1)} copy(bf16[512,768]{1,0:T(8,128)(2,1)} %fusion.36) | data formatting | bytes 1572864 | tf_op jit(solution)/shard_map/convert_element_type | solution.py:93
  130.4 1.6 slice_bitcast_fusion.16
  132.1 1.9 slice.173
  133.9 1.3 add_convert_fusion.1
  135.2 1.0 copy.51
  136.2 1.7 copy.52
  138.0 2.0 copy.95
  140.0 1.1 convert_element_type.102
  141.1 1.4 add_convert_fusion
  142.6 1.0 fusion.139
  143.7 1.0 fusion.138
  144.7 1.0 fusion.137
  146.6 1.0 bitcast_reduce_fusion
  147.6 1.1 bitcast_reduce_fusion.1
  149.0 1.1 bitcast_reduce_fusion.2
  150.2 1.1 bitcast_reduce_fusion.3
  151.3 2.2 fusion.4
  153.6 1.7 fusion.26
  155.3 1.0 fusion.55
  157.0 2.0 fusion.6
  159.0 1.7 fusion.24
  160.7 1.0 fusion.56
  162.4 2.0 fusion.8
  164.4 1.7 fusion.22
  167.9 2.2 fusion.10
  170.1 1.7 fusion.20
  171.9 1.0 fusion.58
  176.1 4.8 %convolution_convert_fusion = bf16[512,4096]{1,0:T(8,128)(2,1)S(1)} fusion(bf16[512,4096]{0,1:T(8,128)(2,1)} %all-gather.5.cloned.1.call-done, bf16[1024,512]{0,1:T(8,128)(2,1)} %constant_dynamic-update-slice_fusion, s32[]{:T(128)S(6)} %select_n.177), kind=kOutput, calls=%fused_computation.22 | convolution fusion | flops 2149580800 | bytes 8912900 | tf_op jit(solution)/shard_map/dot_general | solution.py:128
  180.9 1.9 copy-done.4
  183.1 4.3 %collective-permute-done.3 = bf16[2,128,4096]{2,1,0:T(8,128)(2,1)} collective-permute-done((bf16[2,128,4096]{2,1,0:T(8,128)(2,1)S(1)}, bf16[2,128,4096]{2,1,0:T(8,128)(2,1)}, u32[]{:S(2)}, u32[]{:S(2)}) %collective-permute-start.3) | collective-permute-done | bytes 2097184 | tf_op jit(solution)/shard_map/ppermute | solution.py:136
  187.4 2.9 %convert_add_fusion = f32[2,128,4096]{2,1,0:T(8,128)S(1)} fusion(bf16[2,128,4096]{2,1,0:T(8,128)(2,1)} %collective-permute-done.3, bf16[2,2,128,4096]{3,2,1,0:T(8,128)(2,1)} %bitcast.231, s32[]{:T(128)S(6)} %select_n.178), kind=kLoop, calls=%fused_computation.39 | loop fusion | flops 3145728 | bytes 8388612 | tf_op jit(solution)/shard_map/add | solution.py:137
  190.3 1.9 copy-done.3
  192.4 2.7 %collective-permute-start.4 = (bf16[128,4096]{1,0:T(8,128)(2,1)S(1)}, bf16[128,4096]{1,0:T(8,128)(2,1)S(1)}, u32[]{:S(2)}, u32[]{:S(2)}) collective-permute-start(bf16[128,4096]{1,0:T(8,128)(2,1)S(1)} %fusion.59), channel_id=1, source_target_pairs={{0,2},{2,0},{1,3},{3,1},{4,6},{6,4},{5,7},{7,5},{8,10},{10,8},{9,1... | collective-permute-start | bytes 3145736 | tf_op jit(solution)/shard_map/ppermute | solution.py:140
  196.6 22.0 %collective-permute-done.4 = bf16[128,4096]{1,0:T(8,128)(2,1)S(1)} collective-permute-done((bf16[128,4096]{1,0:T(8,128)(2,1)S(1)}, bf16[128,4096]{1,0:T(8,128)(2,1)S(1)}, u32[]{:S(2)}, u32[]{:S(2)}) %collective-permute-start.4) | collective-permute-done | bytes 1048608 | tf_op jit(solution)/shard_map/ppermute | solution.py:140
  218.6 2.8 %fusion.35 = bf16[128,4096]{1,0:T(8,128)(2,1)} fusion(bf16[128,4096]{1,0:T(8,128)(2,1)S(1)} %collective-permute-done.4, f32[2,128,4096]{2,1,0:T(8,128)} %copy-done.3, s32[]{:T(128)S(6)} %select_n.180), kind=kLoop, calls=%fused_computation.54 | loop fusion | flops 1572864 | bytes 4194308 | tf_op jit(solution)/shard_map/convert_element_type | solution.py:141
  (75 shorter events, 17.4 us)
Async XLA Ops:
  7.2 88.5 %copy-start = (s32[256]{0:T(256)S(1)}, s32[256]{0:T(256)}, u32[]{:S(2)}) copy-start(s32[256]{0:T(256)} %param.13) | copy-start | bytes 3076
  7.2 91.7 %copy-start.8 = (s32[4,24]{1,0:T(4,128)S(1)}, s32[4,24]{1,0:T(4,128)}, u32[]{:S(2)}) copy-start(s32[4,24]{1,0:T(4,128)} %param.14) | copy-start | bytes 1156
  7.2 112.5 %all-gather.3.cloned.1.call-start = ((), (), s32[]{:S(2)}) async-start(), calls=%async_computation | async-start | bytes 7077888 | tf_op jit(solution)/shard_map/all_gather | solution.py:71
  26.8 149.4 %all-gather.5.cloned.1.call-start = ((), (), s32[]{:S(2)}) async-start(), calls=%async_computation.1 | async-start | bytes 4718592 | tf_op jit(solution)/shard_map/all_gather | solution.py:71
  31.6 88.1 %collective-permute-start = (bf16[128,4096]{1,0:T(8,128)(2,1)}, bf16[128,4096]{1,0:T(8,128)(2,1)}, u32[]{:S(2)}, u32[]{:S(2)}) collective-permute-start(bf16[128,4096]{1,0:T(8,128)(2,1)} %fusion.34), channel_id=1, source_target_pairs={{0,3},{1,0},{2,1},{3,2},{4,7},{5,4},{6,5},{7,6},{8,11},{9,8},{10,9... | collective-permute-start | bytes 3145736 | tf_op jit(solution)/shard_map/ppermute | solution.py:84
  36.9 82.8 %collective-permute-start.1 = (bf16[128,4096]{1,0:T(8,128)(2,1)}, bf16[128,4096]{1,0:T(8,128)(2,1)}, u32[]{:S(2)}, u32[]{:S(2)}) collective-permute-start(bf16[128,4096]{1,0:T(8,128)(2,1)} %fusion.34), channel_id=1, source_target_pairs={{0,2},{1,3},{2,0},{3,1},{4,6},{5,7},{6,4},{7,5},{8,10},{9,11},{10,... | collective-permute-start | bytes 3145736 | tf_op jit(solution)/shard_map/ppermute | solution.py:84
  39.2 80.5 %collective-permute-start.2 = (bf16[128,4096]{1,0:T(8,128)(2,1)}, bf16[128,4096]{1,0:T(8,128)(2,1)}, u32[]{:S(2)}, u32[]{:S(2)}) collective-permute-start(bf16[128,4096]{1,0:T(8,128)(2,1)} %fusion.34), channel_id=1, source_target_pairs={{0,1},{1,2},{2,3},{3,0},{4,5},{5,6},{6,7},{7,4},{8,9},{9,10},{10,1... | collective-permute-start | bytes 3145736 | tf_op jit(solution)/shard_map/ppermute | solution.py:84
  99.0 16.3 %copy-start.2 = (s32[256]{0:T(256)S(1)}, s32[256]{0:T(256)}, u32[]{:S(2)}) copy-start(s32[256]{0:T(256)} %param.12) | copy-start | bytes 3076
  147.6 1.4 copy-start.5
  148.7 1.5 copy-start.6
  180.9 1.9 copy-start.4
  183.0 12.1 %copy-start.7 = (bf16[512,128]{0,1:T(8,128)(2,1)S(1)}, bf16[512,128]{0,1:T(8,128)(2,1)}, u32[]{:S(2)}) copy-start(bf16[512,128]{0,1:T(8,128)(2,1)} %get-tuple-element.8) | copy-start | bytes 393220
  183.0 4.4 %collective-permute-start.3 = (bf16[2,128,4096]{2,1,0:T(8,128)(2,1)S(1)}, bf16[2,128,4096]{2,1,0:T(8,128)(2,1)}, u32[]{:S(2)}, u32[]{:S(2)}) collective-permute-start(bf16[2,128,4096]{2,1,0:T(8,128)(2,1)S(1)} %dynamic-slice_bitcast_fusion), channel_id=1, source_target_pairs={{0,1},{1,0},{2,3},{3,2},{4,5},{5,4},{6,7},{7,6},{8,9},{9,8},{10,11... | collective-permute-start | bytes 6291464 | tf_op jit(solution)/shard_map/ppermute | solution.py:136
  183.1 38.3 %copy-start.1 = (s32[256]{0:T(256)S(1)}, s32[256]{0:T(256)}, u32[]{:S(2)}) copy-start(s32[256]{0:T(256)} %param.13) | copy-start | bytes 3076
  190.3 1.9 copy-start.3
  192.4 26.2 %collective-permute-start.4 = (bf16[128,4096]{1,0:T(8,128)(2,1)S(1)}, bf16[128,4096]{1,0:T(8,128)(2,1)S(1)}, u32[]{:S(2)}, u32[]{:S(2)}) collective-permute-start(bf16[128,4096]{1,0:T(8,128)(2,1)S(1)} %fusion.59), channel_id=1, source_target_pairs={{0,2},{2,0},{1,3},{3,1},{4,6},{6,4},{5,7},{7,5},{8,10},{10,8},{9,1... | collective-permute-start | bytes 3145736 | tf_op jit(solution)/shard_map/ppermute | solution.py:140
Sparse Core Ops, SparseCore 0:
  26.9 79.8 all-gather.2
  108.6 53.3 all-gather.4

commit v9 on v8

--- a/solution.py
+++ b/solution.py
@@ -72,6 +72,19 @@
     return values
 
 
+def z_first_gather(values, axis):
+    for name in REQ_AXES:
+        values = lax.all_gather(values, name, axis=axis, tiled=True)
+    return values
+
+
+def blocks_to_z_first(values, axis, sizes):
+    shape = values.shape
+    split = shape[:axis] + tuple(sizes) + (-1,) + shape[axis + 1:]
+    order = tuple(range(axis)) + (axis + 2, axis + 1, axis) + tuple(range(axis + 3, len(split)))
+    return values.reshape(split).transpose(order).reshape(shape)
+
+
 def per_device(hidden, norm_gain, w_qkv, w_out, lengths, deal, pages, pool):
     states = hidden.astype(jnp.float32)
     mean_square = jnp.mean(states * states, axis=1, keepdims=True)
@@ -86,9 +99,10 @@
     ]
     gathered = jnp.concatenate(arrived, 0)
     tok_rows = gathered.shape[0]
+    req_sizes = tuple(lax.axis_size(name) for name in REQ_AXES)
     projected = jnp.dot(
-        gathered,
-        staged_gather(w_qkv, REQ_AXES, 0),
+        blocks_to_z_first(gathered, 1, req_sizes),
+        z_first_gather(w_qkv, 0),
         preferred_element_type=jnp.float32,
     ).astype(jnp.bfloat16)
     full_out = staged_gather(w_out, REQ_AXES, 1)

time: 230 us -> 264 us (1.15)
  waiting for transfers between devices: 26.3 us -> 64.6 us
  blocking collectives: 69.3 us -> 76.5 us
  starting transfers between devices: 11.3 us -> 7.51 us
  matrix products: 32 us -> 28.4 us
    all_gather x0 -> x2, waiting for transfers between devices: none -> 36.9 us  [z_first_gather(): values = lax.all_gather(values, name, axis=axis, tiled=True)]
    all_gather x0 -> x1, blocking collectives: none -> 27.6 us  [z_first_gather(): values = lax.all_gather(values, name, axis=axis, tiled=True)]
    all_gather x4 -> x2, blocking collectives: 69.3 us -> 48.9 us  [staged_gather(): values = lax.all_gather(values, name, axis=axis, tiled=True)]
    dot_general x8, matrix products: 10.8 us -> 7.72 us  [value_weighted_rows(): jnp.einsum(form, weights.astype(jnp.bfloat16), values, preferred_element_...]
    unnamed x27 -> x38, local copies, waits for them, and re-layouts: 11.8 us -> 11.7 us
  transfers between devices with their start and end apart: 7 -> 8, of which waited for: 2 -> 3; matrix products, arithmetic and copies ran while one was open for 37% -> 30% of each run, Pallas kernels for 0% -> 0%
where the time goes in v9:
time: 264 us
  blocking collectives  76.5 us (29%)
  waiting for transfers between devices  64.6 us (24%)
  local copies, waits for them, and re-layouts  38.3 us (15%)
  matrix products  28.4 us (11%)
  other arithmetic  26.3 us (10%)
  between operations  22 us (8%)
  starting transfers between devices  7.51 us (3%)
    all_gather x2, blocking collectives, staged_gather(): values = lax.all_gather(values, name, axis=axis, tiled=True)  48.9 us
    all_gather x2, waiting for transfers between devices, z_first_gather(): values = lax.all_gather(values, name, axis=axis, tiled=True)  36.9 us
    all_gather x1, blocking collectives, z_first_gather(): values = lax.all_gather(values, name, axis=axis, tiled=True)  27.6 us
    ppermute x1, waiting for transfers between devices, per_device(): lax.ppermute(theirs, 'yhi', perm=[(0, 1), (1, 0)]).astype(jnp.float32)  23.5 us
    gather x4, local copies, waits for them, and re-layouts, padded_attention(): cache = pool[page_row].reshape(-1, 2 * HEAD)  18.6 us
    unnamed x38, local copies, waits for them, and re-layouts  11.7 us
    reduce_sum x8, other arithmetic, padded_attention(): total = cached_exp.sum(-1) + recent_exponent.sum(-1)  8.64 us
    dot_general x8, matrix products, value_weighted_rows(): jnp.einsum(form, weights.astype(jnp.bfloat16), values, preferred_element_...  7.72 us
  transfers between devices with their start and end apart: 8, of which 3 were waited for; matrix products, arithmetic and copies ran while one was open for 30% of the time, Pallas kernels for 0%

profile of v9, /device:TPU:1, one launch (start us, length us, event | category | flops | bytes accessed | tf_op | source)
XLA Modules:
  0.0 263.6 jit_solution(13294485414172633888)
XLA Ops:
  7.2 27.6 %all_gather.18 = bf16[512,768]{1,0:T(8,128)(2,1)} all-gather(bf16[64,768]{1,0:T(8,128)(2,1)} %param.10), channel_id=1, replica_groups=mesh['z'=8,'ylo'=2,'x'=4,'yhi'=2,'core'=2] {'z'}, dimensions={0}, use_global_device_ids=true | all-gather | bytes 884736 | tf_op jit(solution)/shard_map/all_gather | solution.py:77
  34.9 36.9 %all-gather.4.cloned.1.call-done = bf16[1024,768]{1,0:T(8,128)(2,1)} async-done(((bf16[512,768]{1,0:T(8,128)(2,1)}), bf16[1024,768]{1,0:T(8,128)(2,1)}) %all-gather.4.cloned.1.call-update) | async-done | bytes 1572880 | tf_op jit(solution)/shard_map/all_gather | solution.py:77
  71.8 1.6 copy.51
  73.4 0.7 convert_element_type.99
  74.7 0.7 fusion.26
  75.4 0.9 collective-permute-start
  76.3 2.4 collective-permute-start.1
  78.8 2.7 %collective-permute-start.2 = (bf16[128,4096]{0,1:T(8,128)(2,1)S(1)}, bf16[128,4096]{0,1:T(8,128)(2,1)}, u32[]{:S(2)}, u32[]{:S(2)}) collective-permute-start(bf16[128,4096]{0,1:T(8,128)(2,1)S(1)} %fusion.26), channel_id=1, source_target_pairs={{0,1},{1,2},{2,3},{3,0},{4,5},{5,6},{6,7},{7,4},{8,9},{9,10},{10,1... | collective-permute-start | bytes 3145736 | tf_op jit(solution)/shard_map/ppermute | solution.py:97
  81.5 10.3 %all_gather.21 = bf16[512,256]{0,1:T(8,128)(2,1)S(1)} all-gather(bf16[512,64]{0,1:T(8,128)(2,1)S(1)} %copy-done.10), channel_id=1, replica_groups=mesh['z'=8,'ylo'=2,'x'=4,'yhi'=2,'core'=2] {'x'}, dimensions={1}, use_global_device_ids=true | all-gather | bytes 327680 | tf_op jit(solution)/shard_map/all_gather | solution.py:71
  91.7 38.6 %all_gather.22 = bf16[512,512]{0,1:T(8,128)(2,1)} all-gather(bf16[512,256]{0,1:T(8,128)(2,1)S(1)} %all_gather.21), channel_id=1, replica_groups=mesh['z'=8,'ylo'=2,'x'=4,'yhi'=2,'core'=2] {'ylo'}, dimensions={1}, use_global_device_ids=true | all-gather | bytes 786432 | tf_op jit(solution)/shard_map/all_gather | solution.py:71
  139.6 4.7 %gather_fusion.5 = bf16[24,128,256]{2,1,0:T(8,128)(2,1)} fusion(bf16[96,128,256]{2,1,0:T(8,128)(2,1)} %param.15, s32[1024]{0:T(1024)S(1)} %get-tuple-element.42), kind=kCustom, calls=%fused_computation.5 | custom fusion | bytes 3145824 | tf_op jit(solution)/shard_map/gather | solution.py:46
  144.2 4.6 %gather_fusion.4 = bf16[24,128,256]{2,1,0:T(8,128)(2,1)} fusion(bf16[96,128,256]{2,1,0:T(8,128)(2,1)} %param.15, s32[1024]{0:T(1024)S(1)} %get-tuple-element.43), kind=kCustom, calls=%fused_computation.4 | custom fusion | bytes 3145824 | tf_op jit(solution)/shard_map/gather | solution.py:46
  148.8 4.7 %gather_fusion.3 = bf16[24,128,256]{2,1,0:T(8,128)(2,1)} fusion(bf16[96,128,256]{2,1,0:T(8,128)(2,1)} %param.15, s32[1024]{0:T(1024)S(1)} %get-tuple-element.44), kind=kCustom, calls=%fused_computation.3 | custom fusion | bytes 3145824 | tf_op jit(solution)/shard_map/gather | solution.py:46
  153.5 4.6 %gather_fusion.2 = bf16[24,128,256]{2,1,0:T(8,128)(2,1)} fusion(bf16[96,128,256]{2,1,0:T(8,128)(2,1)} %param.15, s32[1024]{0:T(1024)S(1)} %get-tuple-element.45), kind=kCustom, calls=%fused_computation.2 | custom fusion | bytes 3145824 | tf_op jit(solution)/shard_map/gather | solution.py:46
  163.8 1.9 pad_maximum_fusion
  165.7 2.6 copy.52
  168.3 7.6 %convolution_convert_fusion.1 = bf16[512,768]{1,0:T(8,128)(2,1)S(1)} fusion(bf16[512,4096]{0,1:T(8,128)(2,1)} %bitcast.236, bf16[4096,768]{1,0:T(8,128)(2,1)} %all-gather.6.cloned.1.call-done), kind=kOutput, calls=%fused_computation.50 | convolution fusion | flops 3221618688 | bytes 11272192 | tf_op jit(solution)/shard_map/dot_general | solution.py:103
  176.2 0.7 slice_bitcast_fusion.16
  177.5 0.8 copy.55
  178.3 0.8 copy.56
  179.5 1.6 add_convert_fusion
  181.2 1.0 fusion.127
  182.2 1.0 fusion.126
  183.3 1.1 fusion.125
  184.4 0.9 fusion.128
  185.3 1.0 bitcast_reduce_fusion
  186.4 1.1 bitcast_reduce_fusion.1
  187.8 1.1 bitcast_reduce_fusion.2
  189.0 1.1 bitcast_reduce_fusion.3
  190.1 2.2 fusion.4
  192.3 1.7 fusion.18
  195.0 2.0 fusion.6
  197.0 1.7 fusion.16
  198.9 0.7 constant_dynamic-update-slice_fusion.6
  199.7 2.0 fusion.8
  201.7 1.7 fusion.14
  204.3 2.2 fusion.10
  206.6 1.7 fusion.12
  208.5 0.7 constant_dynamic-update-slice_fusion.4
  211.9 4.8 %convolution_convert_fusion = bf16[512,4096]{1,0:T(8,128)(2,1)S(1)} fusion(bf16[512,4096]{0,1:T(8,128)(2,1)} %all-gather.8.cloned.1.call-done, bf16[1024,512]{0,1:T(8,128)(2,1)} %constant_dynamic-update-slice_fusion, s32[]{:T(128)S(6)} %select_n.177), kind=kOutput, calls=%fused_computation.22 | convolution fusion | flops 2149580800 | bytes 8912900 | tf_op jit(solution)/shard_map/dot_general | solution.py:142
  216.6 1.9 copy-done.4
  218.9 4.2 %collective-permute-done.3 = bf16[2,128,4096]{2,1,0:T(8,128)(2,1)} collective-permute-done((bf16[2,128,4096]{2,1,0:T(8,128)(2,1)S(1)}, bf16[2,128,4096]{2,1,0:T(8,128)(2,1)}, u32[]{:S(2)}, u32[]{:S(2)}) %collective-permute-start.3) | collective-permute-done | bytes 2097184 | tf_op jit(solution)/shard_map/ppermute | solution.py:150
  223.1 2.9 %convert_add_fusion = f32[2,128,4096]{2,1,0:T(8,128)S(1)} fusion(bf16[2,128,4096]{2,1,0:T(8,128)(2,1)} %collective-permute-done.3, bf16[2,2,128,4096]{3,2,1,0:T(8,128)(2,1)} %bitcast.238, s32[]{:T(128)S(6)} %select_n.178), kind=kLoop, calls=%fused_computation.32 | loop fusion | flops 3145728 | bytes 8388612 | tf_op jit(solution)/shard_map/add | solution.py:151
  226.1 1.9 copy-done.3
  228.1 1.2 collective-permute-start.4
  229.9 0.8 copy.74
  230.8 23.5 %collective-permute-done.4 = bf16[128,4096]{1,0:T(8,128)(2,1)S(1)} collective-permute-done((bf16[128,4096]{1,0:T(8,128)(2,1)S(1)}, bf16[128,4096]{1,0:T(8,128)(2,1)S(1)}, u32[]{:S(2)}, u32[]{:S(2)}) %collective-permute-start.4) | collective-permute-done | bytes 1048608 | tf_op jit(solution)/shard_map/ppermute | solution.py:154
  254.3 2.8 %fusion.27 = bf16[128,4096]{1,0:T(8,128)(2,1)} fusion(bf16[128,4096]{1,0:T(8,128)(2,1)S(1)} %collective-permute-done.4, f32[2,128,4096]{2,1,0:T(8,128)} %copy-done.3, s32[]{:T(128)S(6)} %select_n.180), kind=kLoop, calls=%fused_computation.47 | loop fusion | flops 1572864 | bytes 4194308 | tf_op jit(solution)/shard_map/convert_element_type | solution.py:155
  (90 shorter events, 15.6 us)
Async XLA Ops:
  7.2 129.1 %copy-start = (s32[256]{0:T(256)S(1)}, s32[256]{0:T(256)}, u32[]{:S(2)}) copy-start(s32[256]{0:T(256)} %param.13) | copy-start | bytes 3076
  7.2 74.3 %copy-start.10 = (bf16[512,64]{0,1:T(8,128)(2,1)S(1)}, bf16[512,64]{0,1:T(8,128)(2,1)}, u32[]{:S(2)}) copy-start(bf16[512,64]{0,1:T(8,128)(2,1)} %param.11) | copy-start | bytes 196612
  7.2 132.3 %copy-start.12 = (s32[4,24]{1,0:T(4,128)S(1)}, s32[4,24]{1,0:T(4,128)}, u32[]{:S(2)}) copy-start(s32[4,24]{1,0:T(4,128)} %param.14) | copy-start | bytes 1156
  7.2 64.5 %all-gather.4.cloned.1.call-start = ((), (), s32[]{:S(2)}) async-start(), calls=%async_computation | async-start | bytes 2359296 | tf_op jit(solution)/shard_map/all_gather | solution.py:77
  34.8 133.4 %all-gather.6.cloned.1.call-start = ((), (), s32[]{:S(2)}) async-start(), calls=%async_computation.1 | async-start | bytes 7864320 | tf_op jit(solution)/shard_map/all_gather | solution.py:77
  71.8 140.1 %all-gather.8.cloned.1.call-start = ((), (), s32[]{:S(2)}) async-start(), calls=%async_computation.2 | async-start | bytes 4718592 | tf_op jit(solution)/shard_map/all_gather | solution.py:71
  75.4 88.4 %collective-permute-start = (bf16[128,4096]{0,1:T(8,128)(2,1)S(1)}, bf16[128,4096]{0,1:T(8,128)(2,1)S(1)}, u32[]{:S(2)}, u32[]{:S(2)}) collective-permute-start(bf16[128,4096]{0,1:T(8,128)(2,1)S(1)} %fusion.26), channel_id=1, source_target_pairs={{0,3},{1,0},{2,1},{3,2},{4,7},{5,4},{6,5},{7,6},{8,11},{9,8},{10,9... | collective-permute-start | bytes 3145736 | tf_op jit(solution)/shard_map/ppermute | solution.py:97
  76.3 87.5 %collective-permute-start.1 = (bf16[128,4096]{0,1:T(8,128)(2,1)S(1)}, bf16[128,4096]{0,1:T(8,128)(2,1)S(1)}, u32[]{:S(2)}, u32[]{:S(2)}) collective-permute-start(bf16[128,4096]{0,1:T(8,128)(2,1)S(1)} %fusion.26), channel_id=1, source_target_pairs={{0,2},{1,3},{2,0},{3,1},{4,6},{5,7},{6,4},{7,5},{8,10},{9,11},{10,... | collective-permute-start | bytes 3145736 | tf_op jit(solution)/shard_map/ppermute | solution.py:97
  78.8 85.0 %collective-permute-start.2 = (bf16[128,4096]{0,1:T(8,128)(2,1)S(1)}, bf16[128,4096]{0,1:T(8,128)(2,1)}, u32[]{:S(2)}, u32[]{:S(2)}) collective-permute-start(bf16[128,4096]{0,1:T(8,128)(2,1)S(1)} %fusion.26), channel_id=1, source_target_pairs={{0,1},{1,2},{2,3},{3,0},{4,5},{5,6},{6,7},{7,4},{8,9},{9,10},{10,1... | collective-permute-start | bytes 3145736 | tf_op jit(solution)/shard_map/ppermute | solution.py:97
  139.5 18.6 %copy-start.2 = (s32[256]{0:T(256)S(1)}, s32[256]{0:T(256)}, u32[]{:S(2)}) copy-start(s32[256]{0:T(256)} %param.12) | copy-start | bytes 3076
  168.2 8.6 %copy-start.11 = (f32[512]{0:T(512)S(1)}, f32[512]{0:T(512)}, u32[]{:S(2)}) copy-start(f32[512]{0:T(512)} %convert_bitcast_fusion) | copy-start | bytes 6148
  168.2 8.7 %copy-start.13 = (f32[64]{0:T(128)S(1)}, f32[64]{0:T(128)}, u32[]{:S(2)}) copy-start(f32[64]{0:T(128)} %negate_power_fusion) | copy-start | bytes 772
  179.2 6.2 %copy-start.5 = (bf16[24,128,256]{2,1,0:T(8,128)(2,1)S(1)}, bf16[24,128,256]{2,1,0:T(8,128)(2,1)}, u32[]{:S(2)}) copy-start(bf16[24,128,256]{2,1,0:T(8,128)(2,1)} %gather_fusion.5) | copy-start | bytes 4718596
  183.2 3.1 %copy-start.6 = (bf16[24,128,256]{2,1,0:T(8,128)(2,1)S(1)}, bf16[24,128,256]{2,1,0:T(8,128)(2,1)}, u32[]{:S(2)}) copy-start(bf16[24,128,256]{2,1,0:T(8,128)(2,1)} %gather_fusion.4) | copy-start | bytes 4718596
  186.3 1.4 copy-start.7
  187.4 1.5 copy-start.8
  216.6 1.9 copy-start.4
  218.7 10.6 %copy-start.9 = (bf16[512,128]{0,1:T(8,128)(2,1)S(1)}, bf16[512,128]{0,1:T(8,128)(2,1)}, u32[]{:S(2)}) copy-start(bf16[512,128]{0,1:T(8,128)(2,1)} %get-tuple-element.8) | copy-start | bytes 393220
  218.7 4.4 %collective-permute-start.3 = (bf16[2,128,4096]{2,1,0:T(8,128)(2,1)S(1)}, bf16[2,128,4096]{2,1,0:T(8,128)(2,1)}, u32[]{:S(2)}, u32[]{:S(2)}) collective-permute-start(bf16[2,128,4096]{2,1,0:T(8,128)(2,1)S(1)} %dynamic-slice_bitcast_fusion), channel_id=1, source_target_pairs={{0,1},{1,0},{2,3},{3,2},{4,5},{5,4},{6,7},{7,6},{8,9},{9,8},{10,11... | collective-permute-start | bytes 6291464 | tf_op jit(solution)/shard_map/ppermute | solution.py:150
  218.9 38.2 %copy-start.1 = (s32[256]{0:T(256)S(1)}, s32[256]{0:T(256)}, u32[]{:S(2)}) copy-start(s32[256]{0:T(256)} %param.13) | copy-start | bytes 3076
  226.0 1.9 copy-start.3
  228.1 26.2 %collective-permute-start.4 = (bf16[128,4096]{1,0:T(8,128)(2,1)S(1)}, bf16[128,4096]{1,0:T(8,128)(2,1)S(1)}, u32[]{:S(2)}, u32[]{:S(2)}) collective-permute-start(bf16[128,4096]{1,0:T(8,128)(2,1)S(1)} %fusion.48), channel_id=1, source_target_pairs={{0,2},{2,0},{1,3},{3,1},{4,6},{6,4},{5,7},{7,5},{8,10},{10,8},{9,1... | collective-permute-start | bytes 3145736 | tf_op jit(solution)/shard_map/ppermute | solution.py:154
Sparse Core Ops, SparseCore 0:
  35.0 36.7 all-gather.3
  73.5 69.1 all-gather.5
  144.5 55.4 all-gather.7

commit v10 on v3

--- a/solution.py
+++ b/solution.py
@@ -81,7 +81,7 @@
     n_tp = lax.axis_size(TP_AXES)
     me = lax.axis_index(TP_AXES)
     arrived = [normed] + [
-        lax.ppermute(normed, TP_AXES, perm=[(s, (s - k) % n_tp) for s in range(n_tp)])
+        lax.ppermute(normed, TP_AXES, perm=[(s, s ^ k) for s in range(n_tp)])
         for k in range(1, n_tp)
     ]
     gathered = jnp.concatenate(arrived, 0)
@@ -96,7 +96,7 @@
     heads_here = w_qkv.shape[1] // ((group + 2) * HEAD)
     assert heads_here == 1 and pool.shape[2] == 2 * HEAD
     slot_count = tok_rows // NEW
-    step_slot = (me + jnp.arange(slot_count, dtype=jnp.int32)) % slot_count
+    step_slot = jnp.bitwise_xor(me, jnp.arange(slot_count, dtype=jnp.int32))
     slot_ids = lax.axis_index(REQ_AXES) * slot_count + step_slot
     slot_length = lengths[deal[slot_ids]]
     position = jnp.repeat(slot_length, NEW) + jnp.tile(jnp.arange(NEW, dtype=jnp.int32), slot_count)
@@ -105,12 +105,10 @@
     keys_new = rotate(projected[:, group].astype(jnp.float32), position).astype(jnp.bfloat16)
     values_new = projected[:, group + 1]
     stepped_kv = jnp.concatenate([keys_new, values_new], 1)
-    doubled = jnp.concatenate([stepped_kv, stepped_kv], 0)
-    new_kv = lax.dynamic_slice_in_dim(doubled, ((slot_count - me) % slot_count) * NEW, tok_rows, 0)
+    new_kv = jnp.take(stepped_kv.reshape(slot_count, NEW, -1), step_slot, axis=0).reshape(tok_rows, -1)
     score_scale = 1.0 / math.sqrt(HEAD)
 
-    total = None
-    for k in range(slot_count):
+    def context_of(k):
         rows = slice(k * NEW, (k + 1) * NEW)
         result = padded_attention(
             queries[rows],
@@ -121,13 +119,17 @@
             slot_length[k],
             score_scale,
         )
-        context = result.astype(jnp.bfloat16).transpose(1, 0, 2).reshape(NEW, group * HEAD)
-        partial = jnp.dot(context, full_out, preferred_element_type=jnp.float32).astype(
-            jnp.bfloat16
-        )
-        if k:
-            partial = lax.ppermute(partial, TP_AXES, perm=[(s, (s + k) % n_tp) for s in range(n_tp)])
-        total = partial.astype(jnp.float32) if total is None else total + partial.astype(jnp.float32)
+        return result.astype(jnp.bfloat16).transpose(1, 0, 2).reshape(NEW, group * HEAD)
+
+    def pair_sum_of(first, second):
+        both = jnp.concatenate([context_of(first), context_of(second)], 0)
+        shares = jnp.dot(both, full_out, preferred_element_type=jnp.float32).astype(jnp.bfloat16)
+        taken = lax.ppermute(shares[NEW:], "core", perm=[(0, 1), (1, 0)])
+        return shares[:NEW].astype(jnp.float32) + taken.astype(jnp.float32)
+
+    theirs = pair_sum_of(2, 3).astype(jnp.bfloat16)
+    crossed = lax.ppermute(theirs, "yhi", perm=[(0, 1), (1, 0)])
+    total = pair_sum_of(0, 1) + crossed.astype(jnp.float32)
     return (total.astype(jnp.bfloat16), new_kv)
 
 

time: 234 us -> 211 us (0.902)
  matrix products: 44.9 us -> 26.9 us
  other arithmetic: 25.9 us -> 22 us
  local copies, waits for them, and re-layouts: 29.4 us -> 26.5 us
  waiting for transfers between devices: 28.7 us -> 31.5 us
    all_gather x2, waiting for transfers between devices: 0.02 us -> 12.8 us  [staged_gather(): values = lax.all_gather(values, name, axis=axis, tiled=True)]
    ppermute x6, waiting for transfers between devices: 28.7 us -> 18.8 us  [the longest x1 18.7 us: per_device(): crossed = lax.ppermute(theirs, 'yhi', perm=[(0, 1), (1, 0)])]
    dot_general x8, matrix products: 16.4 us -> 7.72 us  [value_weighted_rows(): jnp.einsum(form, weights.astype(jnp.bfloat16), values, preferred_element_...]
    dot_general x4 -> x2, matrix products: 13.4 us -> 4.98 us  [pair_sum_of(): jnp.dot(both, full_out, preferred_element_type=jnp.float32)]
    convert_element_type x0 -> x3, other arithmetic: none -> 3.36 us  [the longest x1 3.03 us: per_device(): return (total.astype(jnp.bfloat16), new_kv)]
    unnamed x46 -> x20, local copies, waits for them, and re-layouts: 3.65 us -> 0.47 us
    slice x2 -> x6, local copies, waits for them, and re-layouts: 1.29 us -> 4.15 us  [the longest x2 1.69 us: per_device(): values_new = projected[:, group + 1]]
    reduce_sum x8, other arithmetic: 11 us -> 8.4 us  [padded_attention(): total = cached_exp.sum(-1) + recent_exponent.sum(-1)]
  transfers between devices with their start and end apart: 8 -> 8, of which waited for: 2 -> 2; matrix products, arithmetic and copies ran while one was open for 39% -> 33% of each run, Pallas kernels for 0% -> 0%
where the time goes in v10:
time: 211 us
  blocking collectives  69.4 us (33%)
  waiting for transfers between devices  31.5 us (15%)
  matrix products  26.9 us (13%)
  local copies, waits for them, and re-layouts  26.5 us (13%)
  between operations  22.1 us (10%)
  other arithmetic  22 us (10%)
  starting transfers between devices  12.1 us (6%)
    all_gather x4, blocking collectives, staged_gather(): values = lax.all_gather(values, name, axis=axis, tiled=True)  69.4 us
    ppermute x1, waiting for transfers between devices, per_device(): crossed = lax.ppermute(theirs, 'yhi', perm=[(0, 1), (1, 0)])  18.7 us
    gather x4, local copies, waits for them, and re-layouts, padded_attention(): cache = pool[page_row].reshape(-1, 2 * HEAD)  18.7 us
    all_gather x2, waiting for transfers between devices, staged_gather(): values = lax.all_gather(values, name, axis=axis, tiled=True)  12.8 us
    reduce_sum x8, other arithmetic, padded_attention(): total = cached_exp.sum(-1) + recent_exponent.sum(-1)  8.4 us
    ppermute x3, starting transfers between devices, per_device(): lax.ppermute(normed, TP_AXES, perm=[(s, s ^ k) for s in range(n_tp)])  8.26 us
    dot_general x8, matrix products, value_weighted_rows(): jnp.einsum(form, weights.astype(jnp.bfloat16), values, preferred_element_...  7.72 us
    dot_general x1, matrix products, per_device(): jnp.dot(gathered, staged_gather(w_qkv, REQ_AXES, 0), preferred_element_ty...  6.87 us
  transfers between devices with their start and end apart: 8, of which 2 were waited for; matrix products, arithmetic and copies ran while one was open for 33% of the time, Pallas kernels for 0%

profile of v10, /device:TPU:1, one launch (start us, length us, event | category | flops | bytes accessed | tf_op | source)
XLA Modules:
  0.0 210.6 jit_solution(15139840923590275020)
XLA Ops:
  7.2 11.9 %all_gather.18 = bf16[256,768]{1,0:T(8,128)(2,1)S(1)} all-gather(bf16[64,768]{1,0:T(8,128)(2,1)} %param.10), channel_id=1, replica_groups=mesh['z'=8,'ylo'=2,'x'=4,'yhi'=2,'core'=2] {'x'}, dimensions={0}, use_global_device_ids=true | all-gather | bytes 491520 | tf_op jit(solution)/shard_map/all_gather | solution.py:71
  19.2 7.6 %all_gather.19 = bf16[512,768]{1,0:T(8,128)(2,1)} all-gather(bf16[256,768]{1,0:T(8,128)(2,1)S(1)} %all_gather.18), channel_id=1, replica_groups=mesh['z'=8,'ylo'=2,'x'=4,'yhi'=2,'core'=2] {'ylo'}, dimensions={0}, use_global_device_ids=true | all-gather | bytes 1179648 | tf_op jit(solution)/shard_map/all_gather | solution.py:71
  26.8 0.7 convert_element_type.103
  27.5 1.5 fusion.32
  29.1 1.6 fusion.34
  30.6 7.6 %collective-permute-start.2 = (bf16[128,4096]{1,0:T(8,128)(2,1)S(1)}, bf16[128,4096]{1,0:T(8,128)(2,1)S(1)}, u32[]{:S(2)}, u32[]{:S(2)}) collective-permute-start(bf16[128,4096]{1,0:T(8,128)(2,1)S(1)} %fusion.34), channel_id=1, source_target_pairs={{0,3},{1,2},{2,1},{3,0},{4,7},{5,6},{6,5},{7,4},{8,11},{9,10},{10,... | collective-permute-start | bytes 3145736 | tf_op jit(solution)/shard_map/ppermute | solution.py:84
  38.2 0.7 collective-permute-start.1
  38.9 10.6 %all_gather.21 = bf16[512,256]{0,1:T(8,128)(2,1)S(1)} all-gather(bf16[512,64]{0,1:T(8,128)(2,1)} %param.11), channel_id=1, replica_groups=mesh['z'=8,'ylo'=2,'x'=4,'yhi'=2,'core'=2] {'x'}, dimensions={1}, use_global_device_ids=true | all-gather | bytes 327680 | tf_op jit(solution)/shard_map/all_gather | solution.py:71
  49.5 39.3 %all_gather.22 = bf16[512,512]{0,1:T(8,128)(2,1)} all-gather(bf16[512,256]{0,1:T(8,128)(2,1)S(1)} %all_gather.21), channel_id=1, replica_groups=mesh['z'=8,'ylo'=2,'x'=4,'yhi'=2,'core'=2] {'ylo'}, dimensions={1}, use_global_device_ids=true | all-gather | bytes 786432 | tf_op jit(solution)/shard_map/all_gather | solution.py:71
  88.8 0.7 fusion.133
  94.6 0.6 gather_fusion
  97.8 4.7 %gather_fusion.5 = bf16[24,128,256]{2,1,0:T(8,128)(2,1)} fusion(bf16[96,128,256]{2,1,0:T(8,128)(2,1)} %param.15, s32[1024]{0:T(1024)S(1)} %get-tuple-element.40), kind=kCustom, calls=%fused_computation.5 | custom fusion | bytes 3145824 | tf_op jit(solution)/shard_map/gather | solution.py:46
  102.5 4.6 %gather_fusion.4 = bf16[24,128,256]{2,1,0:T(8,128)(2,1)} fusion(bf16[96,128,256]{2,1,0:T(8,128)(2,1)} %param.15, s32[1024]{0:T(1024)S(1)} %get-tuple-element.41), kind=kCustom, calls=%fused_computation.4 | custom fusion | bytes 3145824 | tf_op jit(solution)/shard_map/gather | solution.py:46
  107.1 4.7 %gather_fusion.3 = bf16[24,128,256]{2,1,0:T(8,128)(2,1)} fusion(bf16[96,128,256]{2,1,0:T(8,128)(2,1)} %param.15, s32[1024]{0:T(1024)S(1)} %get-tuple-element.42), kind=kCustom, calls=%fused_computation.3 | custom fusion | bytes 3145824 | tf_op jit(solution)/shard_map/gather | solution.py:46
  111.8 4.7 %gather_fusion.2 = bf16[24,128,256]{2,1,0:T(8,128)(2,1)} fusion(bf16[96,128,256]{2,1,0:T(8,128)(2,1)} %param.15, s32[1024]{0:T(1024)S(1)} %get-tuple-element.43), kind=kCustom, calls=%fused_computation.2 | custom fusion | bytes 3145824 | tf_op jit(solution)/shard_map/gather | solution.py:46
  116.5 0.6 gather_fusion.1
  117.2 0.7 fusion.132
  117.8 0.6 iota_compare_fusion.1
  118.4 0.7 iota_compare_fusion.2
  119.1 0.7 iota_compare_fusion.3
  119.8 0.7 iota_compare_fusion.4
  120.6 6.9 %fusion.35 = bf16[512,768]{1,0:T(8,128)(2,1)S(1)} fusion(bf16[4096,768]{1,0:T(8,128)(2,1)} %all-gather.3.cloned.1.call-done, bf16[128,4096]{1,0:T(8,128)(2,1)S(1)} %collective-permute-done.2, bf16[128,4096]{1,0:T(8,128)(2,1)} %collective-permute-done.1, bf16[128,4096]{1,0:T(8,128)(2,1)} %collective-permute-done, bf16[128,4096]{1,0:T(8,128)(2,1)S(1)} %fusion.34), kind=kOutput, calls=%fused_computation.56 | convolution fusion | flops 3238395904 | bytes 11272192 | tf_op jit(solution)/shard_map/dot_general | solution.py:89
  127.8 0.7 fusion.131
  129.0 1.4 subtract_convert_fusion.1
  131.2 3.0 %bitcast_reduce_fusion = (f32[4,128]{1,0:T(4,128)S(1)}, f32[3072,128,4]{1,0,2:T(8,128)S(1)}) fusion(pred[3072]{0:T(1024)(128)(4,1)S(1)} %iota_compare_fusion.1, bf16[128,4,128]{2,0,1:T(8,128)(2,1)S(1)} %pad_maximum_fusion.1, bf16[3072,256]{1,0:T(8,128)(2,1)} %bitcast.238), kind=kOutput, calls=%fused_computation.8 | convolution fusion | flops 407371264 | bytes 7214080 | tf_op jit(solution)/shard_map/ngd,kd->gnk/dot_general | solution.py:49
  134.5 1.1 bitcast_reduce_fusion.1
  135.9 1.1 bitcast_reduce_fusion.2
  137.1 2.0 fusion.10
  139.1 2.0 fusion.8
  141.4 1.7 fusion.20
  143.4 1.7 fusion.22
  145.3 2.2 %fusion.6 = f32[4,128]{1,0:T(4,128)S(1)} fusion(f32[3072,128,4]{1,0,2:T(8,128)S(1)} %get-tuple-element.31, f32[4,128]{1,0:T(4,128)S(1)} %max.29, pred[3072]{0:T(1024)(128)(4,1)S(1)} %iota_compare_fusion.3), kind=kLoop, calls=%fused_computation.27 | loop fusion | flops 6290944 | bytes 6298624 | tf_op jit(solution)/shard_map/reduce_sum | solution.py:57
  147.5 1.7 fusion.24
  149.3 12.7 %all-gather.5.cloned.1.call-done = bf16[512,4096]{0,1:T(8,128)(2,1)} async-done(((bf16[512,512]{0,1:T(8,128)(2,1)}), bf16[512,4096]{0,1:T(8,128)(2,1)}) %all-gather.5.cloned.1.call-update) | async-done | bytes 4194320 | tf_op jit(solution)/shard_map/all_gather | solution.py:71
  162.0 3.7 %convolution_convert_fusion = bf16[256,4096]{1,0:T(8,128)(2,1)S(1)} fusion(bf16[512,4096]{0,1:T(8,128)(2,1)} %all-gather.5.cloned.1.call-done, bf16[128,512]{0,1:T(8,128)(2,1)S(1)} %bitcast.247, bf16[128,512]{0,1:T(8,128)(2,1)S(1)} %bitcast.249), kind=kOutput, calls=%fused_computation.23 | convolution fusion | flops 1075314688 | bytes 6553600 | tf_op jit(solution)/shard_map/dot_general | solution.py:126
  165.8 0.9 collective-permute-start.4
  166.8 1.1 bitcast_reduce_fusion.3
  167.9 2.0 fusion.4
  170.2 1.7 fusion.26
  172.1 1.3 convolution_convert_fusion.1
  173.5 1.0 slice.211
  174.8 2.8 %collective-permute-start.5 = (bf16[128,4096]{1,0:T(8,128)(2,1)S(1)}, bf16[128,4096]{1,0:T(8,128)(2,1)}, u32[]{:S(2)}, u32[]{:S(2)}) collective-permute-start(bf16[128,4096]{1,0:T(8,128)(2,1)S(1)} %add_convert_fusion.1), channel_id=1, source_target_pairs={{0,2},{2,0},{1,3},{3,1},{4,6},{6,4},{5,7},{7,5},{8,10},{10,8},{9,1... | collective-permute-start | bytes 3145736 | tf_op jit(solution)/shard_map/ppermute | solution.py:131
  177.7 1.0 copy.43
  178.8 0.9 pad_maximum_fusion
  179.6 1.5 gather_fusion.6
  181.1 0.8 bitcast_select_fusion
  182.0 18.7 %collective-permute-done.5 = bf16[128,4096]{1,0:T(8,128)(2,1)} collective-permute-done((bf16[128,4096]{1,0:T(8,128)(2,1)S(1)}, bf16[128,4096]{1,0:T(8,128)(2,1)}, u32[]{:S(2)}, u32[]{:S(2)}) %collective-permute-start.5) | collective-permute-done | bytes 1048608 | tf_op jit(solution)/shard_map/ppermute | solution.py:131
  200.7 3.0 %add_convert_fusion = bf16[128,4096]{1,0:T(8,128)(2,1)} fusion(bf16[128,4096]{1,0:T(8,128)(2,1)} %collective-permute-done.5, bf16[128,4096]{1,0:T(8,128)(2,1)} %collective-permute-done.3, bf16[256,4096]{1,0:T(8,128)(2,1)S(1)} %convolution_convert_fusion.1), kind=kLoop, calls=%fused_computation.54 | loop fusion | flops 3145728 | bytes 4194304 | tf_op jit(solution)/shard_map/convert_element_type | solution.py:133
  (75 shorter events, 4.4 us)
Async XLA Ops:
  7.2 87.4 %copy-start = (s32[256]{0:T(256)S(1)}, s32[256]{0:T(256)}, u32[]{:S(2)}) copy-start(s32[256]{0:T(256)} %param.13) | copy-start | bytes 3076
  7.2 90.5 %copy-start.8 = (s32[4,24]{1,0:T(4,128)S(1)}, s32[4,24]{1,0:T(4,128)}, u32[]{:S(2)}) copy-start(s32[4,24]{1,0:T(4,128)} %param.14) | copy-start | bytes 1156
  7.2 113.4 %all-gather.3.cloned.1.call-start = ((), (), s32[]{:S(2)}) async-start(), calls=%async_computation | async-start | bytes 7077888 | tf_op jit(solution)/shard_map/all_gather | solution.py:71
  26.8 135.2 %all-gather.5.cloned.1.call-start = ((), (), s32[]{:S(2)}) async-start(), calls=%async_computation.1 | async-start | bytes 4718592 | tf_op jit(solution)/shard_map/all_gather | solution.py:71
  30.6 89.9 %collective-permute-start.2 = (bf16[128,4096]{1,0:T(8,128)(2,1)S(1)}, bf16[128,4096]{1,0:T(8,128)(2,1)S(1)}, u32[]{:S(2)}, u32[]{:S(2)}) collective-permute-start(bf16[128,4096]{1,0:T(8,128)(2,1)S(1)} %fusion.34), channel_id=1, source_target_pairs={{0,3},{1,2},{2,1},{3,0},{4,7},{5,6},{6,5},{7,4},{8,11},{9,10},{10,... | collective-permute-start | bytes 3145736 | tf_op jit(solution)/shard_map/ppermute | solution.py:84
  38.2 82.3 %collective-permute-start.1 = (bf16[128,4096]{1,0:T(8,128)(2,1)S(1)}, bf16[128,4096]{1,0:T(8,128)(2,1)}, u32[]{:S(2)}, u32[]{:S(2)}) collective-permute-start(bf16[128,4096]{1,0:T(8,128)(2,1)S(1)} %fusion.34), channel_id=1, source_target_pairs={{0,2},{1,3},{2,0},{3,1},{4,6},{5,7},{6,4},{7,5},{8,10},{9,11},{10,... | collective-permute-start | bytes 3145736 | tf_op jit(solution)/shard_map/ppermute | solution.py:84
  38.9 81.6 %collective-permute-start = (bf16[128,4096]{1,0:T(8,128)(2,1)S(1)}, bf16[128,4096]{1,0:T(8,128)(2,1)}, u32[]{:S(2)}, u32[]{:S(2)}) collective-permute-start(bf16[128,4096]{1,0:T(8,128)(2,1)S(1)} %fusion.34), channel_id=1, source_target_pairs={{0,1},{1,0},{2,3},{3,2},{4,5},{5,4},{6,7},{7,6},{8,9},{9,8},{10,11... | collective-permute-start | bytes 3145736 | tf_op jit(solution)/shard_map/ppermute | solution.py:84
  97.8 18.7 %copy-start.2 = (s32[256]{0:T(256)S(1)}, s32[256]{0:T(256)}, u32[]{:S(2)}) copy-start(s32[256]{0:T(256)} %param.12) | copy-start | bytes 3076
  130.9 3.6 %copy-start.6 = (bf16[24,128,256]{2,1,0:T(8,128)(2,1)S(1)}, bf16[24,128,256]{2,1,0:T(8,128)(2,1)}, u32[]{:S(2)}) copy-start(bf16[24,128,256]{2,1,0:T(8,128)(2,1)} %gather_fusion.4) | copy-start | bytes 4718596
  134.5 1.4 copy-start.5
  137.1 4.3 %copy-start.7 = (bf16[24,128,256]{2,1,0:T(8,128)(2,1)S(1)}, bf16[24,128,256]{2,1,0:T(8,128)(2,1)}, u32[]{:S(2)}) copy-start(bf16[24,128,256]{2,1,0:T(8,128)(2,1)} %gather_fusion.5) | copy-start | bytes 4718596
  162.0 4.8 %copy-start.4 = (bf16[24,128,256]{2,1,0:T(8,128)(2,1)S(1)}, bf16[24,128,256]{2,1,0:T(8,128)(2,1)}, u32[]{:S(2)}) copy-start(bf16[24,128,256]{2,1,0:T(8,128)(2,1)} %gather_fusion.2) | copy-start | bytes 4718596
  165.8 8.7 %collective-permute-start.4 = (bf16[128,4096]{1,0:T(8,128)(2,1)S(1)}, bf16[128,4096]{1,0:T(8,128)(2,1)S(1)}, u32[]{:S(2)}, u32[]{:S(2)}) collective-permute-start(bf16[128,4096]{1,0:T(8,128)(2,1)S(1)} %slice.223), channel_id=1, source_target_pairs={{0,1},{1,0},{2,3},{3,2},{4,5},{5,4},{6,7},{7,6},{8,9},{9,8},{10,11... | collective-permute-start | bytes 3145736 | tf_op jit(solution)/shard_map/ppermute | solution.py:127
  169.9 2.2 %copy-start.3 = (bf16[512,4096]{0,1:T(8,128)(2,1)S(1)}, bf16[512,4096]{0,1:T(8,128)(2,1)}, u32[]{:S(2)}) copy-start(bf16[512,4096]{0,1:T(8,128)(2,1)} %all-gather.5.cloned.1.call-done) | copy-start | bytes 12582916
  172.1 31.6 %copy-start.1 = (s32[256]{0:T(256)S(1)}, s32[256]{0:T(256)}, u32[]{:S(2)}) copy-start(s32[256]{0:T(256)} %param.13) | copy-start | bytes 3076
  174.5 7.5 %collective-permute-start.3 = (bf16[128,4096]{1,0:T(8,128)(2,1)}, bf16[128,4096]{1,0:T(8,128)(2,1)}, u32[]{:S(2)}, u32[]{:S(2)}) collective-permute-start(bf16[128,4096]{1,0:T(8,128)(2,1)} %slice.211), channel_id=1, source_target_pairs={{0,1},{1,0},{2,3},{3,2},{4,5},{5,4},{6,7},{7,6},{8,9},{9,8},{10,11... | collective-permute-start | bytes 3145736 | tf_op jit(solution)/shard_map/ppermute | solution.py:127
  174.8 25.9 %collective-permute-start.5 = (bf16[128,4096]{1,0:T(8,128)(2,1)S(1)}, bf16[128,4096]{1,0:T(8,128)(2,1)}, u32[]{:S(2)}, u32[]{:S(2)}) collective-permute-start(bf16[128,4096]{1,0:T(8,128)(2,1)S(1)} %add_convert_fusion.1), channel_id=1, source_target_pairs={{0,2},{2,0},{1,3},{3,1},{4,6},{6,4},{5,7},{7,5},{8,10},{10,8},{9,1... | collective-permute-start | bytes 3145736 | tf_op jit(solution)/shard_map/ppermute | solution.py:131
Sparse Core Ops, SparseCore 0:
  26.9 79.8 all-gather.2
  108.6 53.3 all-gather.4

commit v11 on v10

--- a/solution.py
+++ b/solution.py
@@ -91,7 +91,8 @@
         staged_gather(w_qkv, REQ_AXES, 0),
         preferred_element_type=jnp.float32,
     ).astype(jnp.bfloat16)
-    full_out = staged_gather(w_out, REQ_AXES, 1)
+    half = w_out.shape[1] // 2
+    out_halves = [staged_gather(w_out[:, h * half:(h + 1) * half], REQ_AXES, 1) for h in range(2)]
     group = QH // KVH
     heads_here = w_qkv.shape[1] // ((group + 2) * HEAD)
     assert heads_here == 1 and pool.shape[2] == 2 * HEAD
@@ -121,15 +122,21 @@
         )
         return result.astype(jnp.bfloat16).transpose(1, 0, 2).reshape(NEW, group * HEAD)
 
-    def pair_sum_of(first, second):
-        both = jnp.concatenate([context_of(first), context_of(second)], 0)
-        shares = jnp.dot(both, full_out, preferred_element_type=jnp.float32).astype(jnp.bfloat16)
+    def pair_sum_of(both, weights):
+        shares = jnp.dot(both, weights, preferred_element_type=jnp.float32).astype(jnp.bfloat16)
         taken = lax.ppermute(shares[NEW:], "core", perm=[(0, 1), (1, 0)])
         return shares[:NEW].astype(jnp.float32) + taken.astype(jnp.float32)
 
-    theirs = pair_sum_of(2, 3).astype(jnp.bfloat16)
-    crossed = lax.ppermute(theirs, "yhi", perm=[(0, 1), (1, 0)])
-    total = pair_sum_of(0, 1) + crossed.astype(jnp.float32)
+    other_pair = jnp.concatenate([context_of(2), context_of(3)], 0)
+    own_pair = jnp.concatenate([context_of(0), context_of(1)], 0)
+    totals = []
+    for weights in out_halves:
+        theirs = pair_sum_of(other_pair, weights).astype(jnp.bfloat16)
+        crossed = lax.ppermute(theirs, "yhi", perm=[(0, 1), (1, 0)])
+        totals.append((pair_sum_of(own_pair, weights), crossed))
+    total = jnp.stack([mine + crossed.astype(jnp.float32) for mine, crossed in totals], 2)
+    n_req = out_halves[0].shape[1] // half
+    total = total.reshape(NEW, n_req, half, 2).transpose(0, 1, 3, 2).reshape(NEW, -1)
     return (total.astype(jnp.bfloat16), new_kv)
 
 

time: 211 us -> 239 us (1.13)
  blocking collectives: 69.4 us -> 81.1 us
  starting transfers between devices: 12.1 us -> 20.2 us
  local copies, waits for them, and re-layouts: 26.5 us -> 33 us
  waiting for transfers between devices: 31.5 us -> 25.1 us
  matrix products: 26.9 us -> 32.5 us
  other arithmetic: 22 us -> 24.5 us
    all_gather x4 -> x6, blocking collectives: 69.4 us -> 81.1 us  [staged_gather(): values = lax.all_gather(values, name, axis=axis, tiled=True)]
    all_gather x2 -> x3, waiting for transfers between devices: 12.8 us -> 6.74 us  [staged_gather(): values = lax.all_gather(values, name, axis=axis, tiled=True)]
    ppermute x2 -> x4, starting transfers between devices: 0.93 us -> 5.48 us  [pair_sum_of(): taken = lax.ppermute(shares[NEW:], 'core', perm=[(0, 1), (1, 0)])]
    ppermute x3, starting transfers between devices: 8.26 us -> 11.5 us  [per_device(): lax.ppermute(normed, TP_AXES, perm=[(s, s ^ k) for s in range(n_tp)])]
    dot_general x2 -> x4, matrix products: 4.98 us -> 8.15 us  [pair_sum_of(): jnp.dot(both, weights, preferred_element_type=jnp.float32)]
    convert_element_type x1, other arithmetic: 3.03 us -> 0.1 us  [per_device(): return (total.astype(jnp.bfloat16), new_kv)]
    convert_element_type x1 -> x2, other arithmetic: 0.31 us -> 3.23 us  [per_device(): theirs = pair_sum_of(other_pair, weights).astype(jnp.bfloat16)]
    another operation x2 -> x4, other arithmetic: 1.85 us -> 4.61 us
  transfers between devices with their start and end apart: 8 -> 12, of which waited for: 2 -> 3; matrix products, arithmetic and copies ran while one was open for 33% -> 36% of each run, Pallas kernels for 0% -> 0%
where the time goes in v11:
time: 239 us; the launch traced here: 238 us
  blocking collectives  81.1 us (34%)
  local copies, waits for them, and re-layouts  33 us (14%)
  matrix products  32.5 us (14%)
  waiting for transfers between devices  25.1 us (11%)
  other arithmetic  24.5 us (10%)
  between operations  21.8 us (9%)
  starting transfers between devices  20.2 us (8%)
    all_gather x6, blocking collectives, staged_gather(): values = lax.all_gather(values, name, axis=axis, tiled=True)  81.1 us
    gather x4, local copies, waits for them, and re-layouts, padded_attention(): cache = pool[page_row].reshape(-1, 2 * HEAD)  18.8 us
    ppermute x2, waiting for transfers between devices, per_device(): crossed = lax.ppermute(theirs, 'yhi', perm=[(0, 1), (1, 0)])  18.3 us
    ppermute x3, starting transfers between devices, per_device(): lax.ppermute(normed, TP_AXES, perm=[(s, s ^ k) for s in range(n_tp)])  11.5 us
    dot_general x8, matrix products, value_weighted_rows(): jnp.einsum(form, weights.astype(jnp.bfloat16), values, preferred_element_...  8.37 us
    reduce_sum x8, other arithmetic, padded_attention(): total = cached_exp.sum(-1) + recent_exponent.sum(-1)  8.19 us
    dot_general x4, matrix products, pair_sum_of(): jnp.dot(both, weights, preferred_element_type=jnp.float32)  8.15 us
    dot_general x4, matrix products, padded_attention(): jnp.einsum('ngd,kd->gnk', query_matrix, cache[:, :HEAD], preferred_elemen...  7.96 us
  transfers between devices with their start and end apart: 12, of which 3 were waited for; matrix products, arithmetic and copies ran while one was open for 36% of the time, Pallas kernels for 0%

profile of v11, /device:TPU:1, one launch (start us, length us, event | category | flops | bytes accessed | tf_op | source)
XLA Modules:
  0.0 238.2 jit_solution(11395198978799780050)
XLA Ops:
  7.2 11.9 %all_gather.27 = bf16[256,768]{1,0:T(8,128)(2,1)S(1)} all-gather(bf16[64,768]{1,0:T(8,128)(2,1)} %param.10), channel_id=1, replica_groups=mesh['z'=8,'ylo'=2,'x'=4,'yhi'=2,'core'=2] {'x'}, dimensions={0}, use_global_device_ids=true | all-gather | bytes 491520 | tf_op jit(solution)/shard_map/all_gather | solution.py:71
  19.2 7.6 %all_gather.28 = bf16[512,768]{1,0:T(8,128)(2,1)} all-gather(bf16[256,768]{1,0:T(8,128)(2,1)S(1)} %all_gather.27), channel_id=1, replica_groups=mesh['z'=8,'ylo'=2,'x'=4,'yhi'=2,'core'=2] {'ylo'}, dimensions={0}, use_global_device_ids=true | all-gather | bytes 1179648 | tf_op jit(solution)/shard_map/all_gather | solution.py:71
  27.6 9.1 %all_gather.33 = bf16[512,128]{0,1:T(8,128)(2,1)S(1)} all-gather(bf16[512,32]{0,1:T(8,128)(2,1)S(1)} %get-tuple-element.11), channel_id=1, replica_groups=mesh['z'=8,'ylo'=2,'x'=4,'yhi'=2,'core'=2] {'x'}, dimensions={1}, use_global_device_ids=true | all-gather | bytes 163840 | tf_op jit(solution)/shard_map/all_gather | solution.py:71
  36.7 5.4 %all_gather.34 = bf16[512,256]{0,1:T(8,128)(2,1)} all-gather(bf16[512,128]{0,1:T(8,128)(2,1)S(1)} %all_gather.33), channel_id=1, replica_groups=mesh['z'=8,'ylo'=2,'x'=4,'yhi'=2,'core'=2] {'ylo'}, dimensions={1}, use_global_device_ids=true | all-gather | bytes 393216 | tf_op jit(solution)/shard_map/all_gather | solution.py:71
  42.9 1.5 fusion.32
  44.4 1.6 fusion.34
  46.0 10.8 %collective-permute-start.2 = (bf16[128,4096]{1,0:T(8,128)(2,1)S(1)}, bf16[128,4096]{1,0:T(8,128)(2,1)S(1)}, u32[]{:S(2)}, u32[]{:S(2)}) collective-permute-start(bf16[128,4096]{1,0:T(8,128)(2,1)S(1)} %fusion.34), channel_id=1, source_target_pairs={{0,3},{1,2},{2,1},{3,0},{4,7},{5,6},{6,5},{7,4},{8,11},{9,10},{10,... | collective-permute-start | bytes 3145736 | tf_op jit(solution)/shard_map/ppermute | solution.py:84
  57.5 10.3 %all_gather.30 = bf16[512,128]{0,1:T(8,128)(2,1)S(1)} all-gather(bf16[512,32]{0,1:T(8,128)(2,1)S(1)} %get-tuple-element.10), channel_id=1, replica_groups=mesh['z'=8,'ylo'=2,'x'=4,'yhi'=2,'core'=2] {'x'}, dimensions={1}, use_global_device_ids=true | all-gather | bytes 163840 | tf_op jit(solution)/shard_map/all_gather | solution.py:71
  67.8 36.8 %all_gather.31 = bf16[512,256]{0,1:T(8,128)(2,1)} all-gather(bf16[512,128]{0,1:T(8,128)(2,1)S(1)} %all_gather.30), channel_id=1, replica_groups=mesh['z'=8,'ylo'=2,'x'=4,'yhi'=2,'core'=2] {'ylo'}, dimensions={1}, use_global_device_ids=true | all-gather | bytes 393216 | tf_op jit(solution)/shard_map/all_gather | solution.py:71
  115.3 4.6 %gather_fusion.5 = bf16[24,128,256]{2,1,0:T(8,128)(2,1)} fusion(bf16[96,128,256]{2,1,0:T(8,128)(2,1)} %param.15, s32[1024]{0:T(1024)S(1)} %get-tuple-element.44), kind=kCustom, calls=%fused_computation.5 | custom fusion | bytes 3145824 | tf_op jit(solution)/shard_map/gather | solution.py:46
  119.9 4.7 %gather_fusion.4 = bf16[24,128,256]{2,1,0:T(8,128)(2,1)} fusion(bf16[96,128,256]{2,1,0:T(8,128)(2,1)} %param.15, s32[1024]{0:T(1024)S(1)} %get-tuple-element.45), kind=kCustom, calls=%fused_computation.4 | custom fusion | bytes 3145824 | tf_op jit(solution)/shard_map/gather | solution.py:46
  124.5 4.7 %gather_fusion.3 = bf16[24,128,256]{2,1,0:T(8,128)(2,1)} fusion(bf16[96,128,256]{2,1,0:T(8,128)(2,1)} %param.15, s32[1024]{0:T(1024)S(1)} %get-tuple-element.46), kind=kCustom, calls=%fused_computation.3 | custom fusion | bytes 3145824 | tf_op jit(solution)/shard_map/gather | solution.py:46
  129.3 4.8 %gather_fusion.2 = bf16[24,128,256]{2,1,0:T(8,128)(2,1)} fusion(bf16[96,128,256]{2,1,0:T(8,128)(2,1)} %param.15, s32[1024]{0:T(1024)S(1)} %get-tuple-element.47), kind=kCustom, calls=%fused_computation.2 | custom fusion | bytes 3145824 | tf_op jit(solution)/shard_map/gather | solution.py:46
  136.7 7.0 %fusion.35 = bf16[512,768]{1,0:T(8,128)(2,1)S(1)} fusion(bf16[4096,768]{1,0:T(8,128)(2,1)} %all-gather.4.cloned.1.call-done, bf16[128,4096]{1,0:T(8,128)(2,1)S(1)} %collective-permute-done.2, bf16[128,4096]{1,0:T(8,128)(2,1)} %collective-permute-done.1, bf16[128,4096]{1,0:T(8,128)(2,1)} %collective-permute-done, bf16[128,4096]{1,0:T(8,128)(2,1)S(1)} %fusion.34), kind=kOutput, calls=%fused_computation.56 | convolution fusion | flops 3238395904 | bytes 11272192 | tf_op jit(solution)/shard_map/dot_general | solution.py:89
  145.2 1.4 subtract_convert_fusion.1
  147.2 2.9 %bitcast_reduce_fusion = (f32[4,128]{1,0:T(4,128)S(1)}, f32[3072,128,4]{1,0,2:T(8,128)S(1)}) fusion(pred[3072]{0:T(1024)(128)(4,1)S(1)} %iota_compare_fusion.1, bf16[128,4,128]{2,0,1:T(8,128)(2,1)S(1)} %pad_maximum_fusion.7, bf16[3072,256]{1,0:T(8,128)(2,1)} %bitcast.246), kind=kOutput, calls=%fused_computation.8 | convolution fusion | flops 407371264 | bytes 7214080 | tf_op jit(solution)/shard_map/ngd,kd->gnk/dot_general | solution.py:49
  150.4 1.7 fusion.20
  152.1 2.0 fusion.10
  154.4 1.1 bitcast_reduce_fusion.1
  155.5 1.7 fusion.22
  157.2 2.0 fusion.8
  159.9 0.9 fusion.56
  160.8 2.4 %convolution_convert_fusion = bf16[256,2048]{1,0:T(8,128)(2,1)S(1)} fusion(bf16[512,2048]{0,1:T(8,128)(2,1)} %all-gather.8.cloned.1.call-done, bf16[128,512]{0,1:T(8,128)(2,1)S(1)} %bitcast.257, bf16[128,512]{0,1:T(8,128)(2,1)} %bitcast.259), kind=kOutput, calls=%fused_computation.49 | convolution fusion | flops 537919488 | bytes 3407872 | tf_op jit(solution)/shard_map/dot_general | solution.py:126
  164.0 2.9 %bitcast_reduce_fusion.2 = (f32[4,128]{1,0:T(4,128)S(1)}, f32[3072,128,4]{1,0,2:T(8,128)S(1)}) fusion(pred[3072]{0:T(1024)(128)(4,1)S(1)} %iota_compare_fusion.3, bf16[512,4,64]{2,0,1:T(8,128)(2,1)S(1)} %get-tuple-element.4, bf16[512,4,64]{2,0,1:T(8,128)(2,1)S(1)} %get-tuple-element.5, bf16[3072,256]{1,0:T(8,128)(2,1)} %bitcast.242), kind=kOutput, calls=%fused_computation.14 | convolution fusion | flops 407633408 | bytes 7607296 | tf_op jit(solution)/shard_map/ngd,kd->gnk/dot_general | solution.py:49
  167.0 1.1 bitcast_reduce_fusion.3
  168.5 2.0 fusion.6
  170.5 2.0 fusion.4
  172.5 1.7 fusion.24
  174.5 1.7 fusion.26
  177.2 0.9 slice.249
  178.6 6.7 %all-gather.6.cloned.1.call-done = bf16[512,2048]{0,1:T(8,128)(2,1)} async-done(((bf16[512,256]{0,1:T(8,128)(2,1)}), bf16[512,2048]{0,1:T(8,128)(2,1)}) %all-gather.6.cloned.1.call-update) | async-done | bytes 2097168 | tf_op jit(solution)/shard_map/all_gather | solution.py:71
  185.3 2.4 %convolution_convert_fusion.2 = bf16[256,2048]{1,0:T(8,128)(2,1)S(1)} fusion(bf16[512,2048]{0,1:T(8,128)(2,1)} %all-gather.6.cloned.1.call-done, bf16[128,512]{0,1:T(8,128)(2,1)S(1)} %bitcast.258, bf16[128,512]{0,1:T(8,128)(2,1)} %bitcast.260), kind=kOutput, calls=%fused_computation.51 | convolution fusion | flops 537919488 | bytes 3407872 | tf_op jit(solution)/shard_map/dot_general | solution.py:126
  187.7 0.8 slice.247
  188.6 5.0 %collective-permute-start.4 = (bf16[128,2048]{1,0:T(8,128)(2,1)}, bf16[128,2048]{1,0:T(8,128)(2,1)}, u32[]{:S(2)}, u32[]{:S(2)}) collective-permute-start(bf16[128,2048]{1,0:T(8,128)(2,1)} %slice.247), channel_id=1, source_target_pairs={{0,1},{1,0},{2,3},{3,2},{4,5},{5,4},{6,7},{7,6},{8,9},{9,8},{10,11... | collective-permute-start | bytes 1572872 | tf_op jit(solution)/shard_map/ppermute | solution.py:127
  193.6 2.5 %convolution_convert_fusion.3 = bf16[256,2048]{1,0:T(8,128)(2,1)S(1)} fusion(bf16[512,2048]{0,1:T(8,128)(2,1)} %all-gather.6.cloned.1.call-done, bf16[128,512]{0,1:T(8,128)(2,1)} %bitcast.262, bf16[128,512]{0,1:T(8,128)(2,1)} %bitcast.264), kind=kOutput, calls=%fused_computation.52 | convolution fusion | flops 537919488 | bytes 3407872 | tf_op jit(solution)/shard_map/dot_general | solution.py:126
  196.1 1.0 copy-done.4
  197.9 1.0 copy.47
  198.9 0.9 pad_maximum_fusion.2
  199.8 1.5 gather_fusion.6
  201.3 1.2 add_convert_fusion.1
  202.5 2.8 %collective-permute-start.8 = (bf16[128,2048]{1,0:T(8,128)(2,1)S(1)}, bf16[128,2048]{1,0:T(8,128)(2,1)S(1)}, u32[]{:S(2)}, u32[]{:S(2)}) collective-permute-start(bf16[128,2048]{1,0:T(8,128)(2,1)S(1)} %add_convert_fusion.1), channel_id=1, source_target_pairs={{0,2},{2,0},{1,3},{3,1},{4,6},{6,4},{5,7},{7,5},{8,10},{10,8},{9,1... | collective-permute-start | bytes 1572872 | tf_op jit(solution)/shard_map/ppermute | solution.py:135
  205.3 2.0 add_convert_fusion.3
  207.6 0.8 bitcast_select_fusion
  208.4 8.7 %collective-permute-done.8 = bf16[128,2048]{1,0:T(8,128)(2,1)S(1)} collective-permute-done((bf16[128,2048]{1,0:T(8,128)(2,1)S(1)}, bf16[128,2048]{1,0:T(8,128)(2,1)S(1)}, u32[]{:S(2)}, u32[]{:S(2)}) %collective-permute-start.8) | collective-permute-done | bytes 524320 | tf_op jit(solution)/shard_map/ppermute | solution.py:135
  217.1 1.3 add_convert_fusion
  218.7 9.6 %collective-permute-done.5 = bf16[128,2048]{1,0:T(8,128)(2,1)S(1)} collective-permute-done((bf16[128,2048]{1,0:T(8,128)(2,1)}, bf16[128,2048]{1,0:T(8,128)(2,1)S(1)}, u32[]{:S(2)}, u32[]{:S(2)}) %collective-permute-start.5) | collective-permute-done | bytes 524320 | tf_op jit(solution)/shard_map/ppermute | solution.py:135
  228.3 1.5 add_convert_fusion.2
  230.3 1.3 copy.48
  (110 shorter events, 16.3 us)
Async XLA Ops:
  7.2 103.1 %copy-start = (s32[256]{0:T(256)S(1)}, s32[256]{0:T(256)}, u32[]{:S(2)}) copy-start(s32[256]{0:T(256)} %param.13) | copy-start | bytes 3076
  7.2 103.7 %copy-start.2 = (s32[256]{0:T(256)S(1)}, s32[256]{0:T(256)}, u32[]{:S(2)}) copy-start(s32[256]{0:T(256)} %param.12) | copy-start | bytes 3076
  7.2 108.0 %copy-start.13 = (s32[4,24]{1,0:T(4,128)S(1)}, s32[4,24]{1,0:T(4,128)}, u32[]{:S(2)}) copy-start(s32[4,24]{1,0:T(4,128)} %param.14) | copy-start | bytes 1156
  7.2 129.5 %all-gather.4.cloned.1.call-start = ((), (), s32[]{:S(2)}) async-start(), calls=%async_computation | async-start | bytes 7077888 | tf_op jit(solution)/shard_map/all_gather | solution.py:71
  26.8 133.9 %all-gather.8.cloned.1.call-start = ((), (), s32[]{:S(2)}) async-start(), calls=%async_computation.2 | async-start | bytes 2359296 | tf_op jit(solution)/shard_map/all_gather | solution.py:71
  42.2 143.1 %all-gather.6.cloned.1.call-start = ((), (), s32[]{:S(2)}) async-start(), calls=%async_computation.1 | async-start | bytes 2359296 | tf_op jit(solution)/shard_map/all_gather | solution.py:71
  46.0 90.7 %collective-permute-start.2 = (bf16[128,4096]{1,0:T(8,128)(2,1)S(1)}, bf16[128,4096]{1,0:T(8,128)(2,1)S(1)}, u32[]{:S(2)}, u32[]{:S(2)}) collective-permute-start(bf16[128,4096]{1,0:T(8,128)(2,1)S(1)} %fusion.34), channel_id=1, source_target_pairs={{0,3},{1,2},{2,1},{3,0},{4,7},{5,6},{6,5},{7,4},{8,11},{9,10},{10,... | collective-permute-start | bytes 3145736 | tf_op jit(solution)/shard_map/ppermute | solution.py:84
  56.8 79.9 %collective-permute-start.1 = (bf16[128,4096]{1,0:T(8,128)(2,1)S(1)}, bf16[128,4096]{1,0:T(8,128)(2,1)}, u32[]{:S(2)}, u32[]{:S(2)}) collective-permute-start(bf16[128,4096]{1,0:T(8,128)(2,1)S(1)} %fusion.34), channel_id=1, source_target_pairs={{0,2},{1,3},{2,0},{3,1},{4,6},{5,7},{6,4},{7,5},{8,10},{9,11},{10,... | collective-permute-start | bytes 3145736 | tf_op jit(solution)/shard_map/ppermute | solution.py:84
  57.5 79.2 %collective-permute-start = (bf16[128,4096]{1,0:T(8,128)(2,1)S(1)}, bf16[128,4096]{1,0:T(8,128)(2,1)}, u32[]{:S(2)}, u32[]{:S(2)}) collective-permute-start(bf16[128,4096]{1,0:T(8,128)(2,1)S(1)} %fusion.34), channel_id=1, source_target_pairs={{0,1},{1,0},{2,3},{3,2},{4,5},{5,4},{6,7},{7,6},{8,9},{9,8},{10,11... | collective-permute-start | bytes 3145736 | tf_op jit(solution)/shard_map/ppermute | solution.py:84
  135.9 23.3 %copy-start.11 = (pred[128,128]{0,1:T(8,128)(4,1)}, pred[128,128]{0,1:T(8,128)(4,1)S(1)}, u32[]{:S(2)}) copy-start(pred[128,128]{0,1:T(8,128)(4,1)S(1)} %iota_compare_fusion) | copy-start | bytes 49156
  147.1 3.3 %copy-start.8 = (bf16[24,128,256]{2,1,0:T(8,128)(2,1)S(1)}, bf16[24,128,256]{2,1,0:T(8,128)(2,1)}, u32[]{:S(2)}) copy-start(bf16[24,128,256]{2,1,0:T(8,128)(2,1)} %gather_fusion.5) | copy-start | bytes 4718596
  152.1 2.3 copy-start.7
  163.2 3.7 %copy-start.5 = (bf16[24,128,256]{2,1,0:T(8,128)(2,1)S(1)}, bf16[24,128,256]{2,1,0:T(8,128)(2,1)}, u32[]{:S(2)}) copy-start(bf16[24,128,256]{2,1,0:T(8,128)(2,1)} %gather_fusion.2) | copy-start | bytes 4718596
  164.0 37.2 %collective-permute-start.7 = (bf16[128,2048]{1,0:T(8,128)(2,1)}, bf16[128,2048]{1,0:T(8,128)(2,1)}, u32[]{:S(2)}, u32[]{:S(2)}) collective-permute-start(bf16[128,2048]{1,0:T(8,128)(2,1)} %slice.251), channel_id=1, source_target_pairs={{0,1},{1,0},{2,3},{3,2},{4,5},{5,4},{6,7},{7,6},{8,9},{9,8},{10,11... | collective-permute-start | bytes 1572872 | tf_op jit(solution)/shard_map/ppermute | solution.py:127
  166.9 1.1 copy-start.12
  168.5 4.0 %copy-start.6 = (bf16[24,128,256]{2,1,0:T(8,128)(2,1)S(1)}, bf16[24,128,256]{2,1,0:T(8,128)(2,1)}, u32[]{:S(2)}) copy-start(bf16[24,128,256]{2,1,0:T(8,128)(2,1)} %gather_fusion.3) | copy-start | bytes 4718596
  174.2 2.2 copy-start.3
  174.5 2.7 %copy-start.9 = (bf16[128,4,128]{0,2,1:T(8,128)(2,1)}, bf16[128,4,128]{0,2,1:T(8,128)(2,1)S(1)}, u32[]{:S(2)}) copy-start(bf16[128,4,128]{0,2,1:T(8,128)(2,1)S(1)} %fusion.55) | copy-start | bytes 393220
  176.4 2.2 copy-start.10
  178.1 29.5 %copy-start.14 = (pred[512]{0:T(512)(128)(4,1)S(1)}, pred[512]{0:T(512)(128)(4,1)}, u32[]{:S(2)}) copy-start(pred[512]{0:T(512)(128)(4,1)} %broadcast_bitcast_fusion) | copy-start | bytes 1540
  178.1 30.4 %collective-permute-start.6 = (bf16[128,2048]{1,0:T(8,128)(2,1)}, bf16[128,2048]{1,0:T(8,128)(2,1)}, u32[]{:S(2)}, u32[]{:S(2)}) collective-permute-start(bf16[128,2048]{1,0:T(8,128)(2,1)} %slice.249), channel_id=1, source_target_pairs={{0,1},{1,0},{2,3},{3,2},{4,5},{5,4},{6,7},{7,6},{8,9},{9,8},{10,11... | collective-permute-start | bytes 1572872 | tf_op jit(solution)/shard_map/ppermute | solution.py:127
  188.6 16.7 %collective-permute-start.4 = (bf16[128,2048]{1,0:T(8,128)(2,1)}, bf16[128,2048]{1,0:T(8,128)(2,1)}, u32[]{:S(2)}, u32[]{:S(2)}) collective-permute-start(bf16[128,2048]{1,0:T(8,128)(2,1)} %slice.247), channel_id=1, source_target_pairs={{0,1},{1,0},{2,3},{3,2},{4,5},{5,4},{6,7},{7,6},{8,9},{9,8},{10,11... | collective-permute-start | bytes 1572872 | tf_op jit(solution)/shard_map/ppermute | solution.py:127
  196.1 1.0 copy-start.4
  197.9 20.8 %collective-permute-start.3 = (bf16[128,2048]{1,0:T(8,128)(2,1)}, bf16[128,2048]{1,0:T(8,128)(2,1)}, u32[]{:S(2)}, u32[]{:S(2)}) collective-permute-start(bf16[128,2048]{1,0:T(8,128)(2,1)} %slice.235), channel_id=1, source_target_pairs={{0,1},{1,0},{2,3},{3,2},{4,5},{5,4},{6,7},{7,6},{8,9},{9,8},{10,11... | collective-permute-start | bytes 1572872 | tf_op jit(solution)/shard_map/ppermute | solution.py:127
  202.5 14.6 %collective-permute-start.8 = (bf16[128,2048]{1,0:T(8,128)(2,1)S(1)}, bf16[128,2048]{1,0:T(8,128)(2,1)S(1)}, u32[]{:S(2)}, u32[]{:S(2)}) collective-permute-start(bf16[128,2048]{1,0:T(8,128)(2,1)S(1)} %add_convert_fusion.1), channel_id=1, source_target_pairs={{0,2},{2,0},{1,3},{3,1},{4,6},{6,4},{5,7},{7,5},{8,10},{10,8},{9,1... | collective-permute-start | bytes 1572872 | tf_op jit(solution)/shard_map/ppermute | solution.py:135
  207.3 21.0 %collective-permute-start.5 = (bf16[128,2048]{1,0:T(8,128)(2,1)}, bf16[128,2048]{1,0:T(8,128)(2,1)S(1)}, u32[]{:S(2)}, u32[]{:S(2)}) collective-permute-start(bf16[128,2048]{1,0:T(8,128)(2,1)} %add_convert_fusion.3), channel_id=1, source_target_pairs={{0,2},{2,0},{1,3},{3,1},{4,6},{6,4},{5,7},{7,5},{8,10},{10,8},{9,1... | collective-permute-start | bytes 1572872 | tf_op jit(solution)/shard_map/ppermute | solution.py:135
  207.6 24.0 %copy-start.1 = (s32[256]{0:T(256)S(1)}, s32[256]{0:T(256)}, u32[]{:S(2)}) copy-start(s32[256]{0:T(256)} %param.13) | copy-start | bytes 3076
Sparse Core Ops, SparseCore 0:
  26.9 79.8 all-gather.3
  108.7 35.4 all-gather.7
  145.9 39.3 all-gather.5
